TPU v7x, 128 devices: a whole 4x4x4 slice. The times are simulated.
128 devices in a mesh: mode: 8 (over x, core), member: 16 (over z, y).
Axes of the slice: x: 4, y: 4, z: 4, core: 2. Of those that a mesh axis runs over, the one named last changes fastest.
Arguments:
- ground_accel: bfloat16 [4, 639], replicated, may hold values from -6 to 6
- modal_kernel: bfloat16 [4096, 512], P(('mode', 'member')), may hold values from -0.25 to 0.25
- mode_shapes: bfloat16 [98304, 4096], P('member', 'mode'), may hold values from -0.09375 to 0.09375
- member_owner: int32 [16384, 1], P('member'), may hold values from 0 to 127; in each aligned block of 128 rows (0 to 127, 128 to 255, ...) at most 2 rows name the same one
- member_group: int32 [16384, 1], P('member'), may hold values from 0 to 3
- record_table: int32 [512, 8], P(('mode', 'member')), may hold values from 0 to 3
- case_coef: float32 [8, 6], replicated, may hold values from -1.5 to 1.5
- gravity: float32 [512, 8], P(('mode', 'member')), may hold values from -10 to 10
Outputs:
- demand: float32 [512, 8], P(('mode', 'member'))
Inputs may be any that keep to these rules, and one draw needn't show every extreme that they name: `member_owner`: in each aligned block of 1024 / 8 members no owner is named more than 2 times, a bound that some block reaches.
All inputs are finite; a program needn't handle non-finite values.
Results may differ from a plain program's by a relative error of at most 0.0065.
Values may be sent and summed in bfloat16 or wider, within the bound.
No kernel may reach another device: no remote copies, remote signals or barrier semaphores. Data moves between devices by JAX's collectives and lax.ppermute only.
A program may use at most 64 MiB of HBM per device.

v0:
```python
import jax
import jax.numpy as jnp
from jax import lax
from jax.sharding import PartitionSpec as P


def lagged_table(ground_accel, tap_count):
    record_count, span_len = ground_accel.shape
    step_count = span_len - tap_count + 1
    offsets = tap_count - 1 + jnp.arange(step_count)[None, :] - jnp.arange(tap_count)[:, None]
    lag_table = ground_accel[:, offsets]
    return jnp.transpose(lag_table, (1, 0, 2)).reshape(tap_count, record_count * step_count)


def local(
    ground_accel,
    modal_kernel,
    mode_shapes,
    member_owner,
    member_group,
    record_table,
    case_coef,
    gravity,
):
    tap_count = modal_kernel.shape[1]
    record_count = ground_accel.shape[0]
    comp_count = case_coef.shape[1]
    group_count = gravity.shape[0]
    n_mode = lax.axis_size("mode")
    n_member = lax.axis_size("member")
    lagged = lagged_table(ground_accel, tap_count)
    local_resp = jnp.dot(modal_kernel, lagged, preferred_element_type=jnp.float32).astype(
        jnp.bfloat16
    )
    modal_resp = lax.all_gather(local_resp, "member", axis=0, tiled=True)
    own_rows = mode_shapes.shape[0] // n_mode
    forces = lax.psum_scatter(
        jnp.dot(mode_shapes, modal_resp, preferred_element_type=jnp.float32).astype(jnp.bfloat16),
        "mode",
        scatter_dimension=0,
        tiled=True,
    ).astype(jnp.float32)
    members_here = own_rows // comp_count
    owner_total = n_mode * n_member
    slot_depth = max(2, 2 * members_here // owner_total)
    packed = forces.reshape(members_here, comp_count * forces.shape[1])
    first_row = lax.axis_index("mode") * members_here
    owner_ids = lax.dynamic_slice_in_dim(member_owner[:, 0], first_row, members_here)
    group_ids = lax.dynamic_slice_in_dim(member_group[:, 0], first_row, members_here)
    position = jnp.arange(members_here)
    earlier = (owner_ids[:, None] == owner_ids[None, :]) & (position[None, :] < position[:, None])
    member_rank = jnp.sum(earlier.astype(jnp.int32), axis=1)
    slot_index = owner_ids * slot_depth + member_rank
    slot_total = owner_total * slot_depth
    placement = jnp.arange(slot_total)[:, None] == slot_index[None, :]
    outgoing = jnp.dot(placement.astype(jnp.float32), packed, precision=lax.Precision.HIGHEST)
    slot_labels = jnp.max(jnp.where(placement, group_ids[None, :], -1), axis=1)
    incoming, slot_tags = (
        lax.all_to_all(
            outgoing.reshape(owner_total, slot_depth, -1).astype(jnp.bfloat16),
            ("mode", "member"),
            split_axis=0,
            concat_axis=0,
            tiled=True,
        ).astype(jnp.float32),
        lax.all_to_all(
            slot_labels.reshape(owner_total, slot_depth),
            ("mode", "member"),
            split_axis=0,
            concat_axis=0,
            tiled=True,
        ),
    )
    selector = (jnp.arange(group_count)[:, None] == slot_tags.reshape(-1)[None, :]).astype(
        jnp.float32
    )
    group_sums = jnp.dot(
        selector, incoming.reshape(selector.shape[1], -1), precision=lax.Precision.HIGHEST
    )
    group_sums = group_sums.reshape(group_count, comp_count, record_count, -1)
    case_mix = jnp.einsum("sc,gcrt->gsrt", case_coef, group_sums, precision=lax.Precision.HIGHEST)
    record_pick = (record_table[:, :, None] == jnp.arange(record_count)[None, None, :]).astype(
        jnp.float32
    )
    selected = jnp.sum(record_pick[:, :, :, None] * case_mix, axis=2)
    combined = gravity[:, :, None] + selected
    return jnp.max(jnp.abs(combined), axis=2)


def solution(mesh):
    placed = (
        P(),
        P(("mode", "member"), None),
        P("member", "mode"),
        P("member", None),
        P("member", None),
        P(("mode", "member"), None),
        P(),
        P(("mode", "member"), None),
    )
    return jax.shard_map(
        local, mesh=mesh, in_specs=placed, out_specs=P(("mode", "member"), None), check_vma=False
    )
```

profile of v0, /device:TPU:0, one launch (start us, length us, event | category | flops | bytes accessed | tf_op | source)
XLA Modules:
  0.0 376.7 jit_solution(7160551659993161368)
XLA Ops:
  6.5 0.0 copy-start
  6.5 0.0 reduce-scatter.2.cloned.1.call-start
  6.5 0.9 copy.22
  7.4 0.1 fusion.5
  7.5 227.3 %gather_fusion = bf16[65536,4]{1,0:T(8,128)(2,1)} fusion(bf16[4,639]{0,1:T(8,128)(2,1)S(1)} %copy.22, s32[65536]{0:T(1024)S(1)} %fusion.5), kind=kCustom, calls=%fused_computation | custom fusion | bytes 1310720 | tf_op jit(solution)/shard_map/gather | solution.py:11
  234.8 17.2 %copy.23 = bf16[512,128,4]{0,1,2:T(8,128)(2,1)S(1)} copy(bf16[512,128,4]{2,1,0:T(8,128)(2,1)} %bitcast.43) | data formatting | bytes 1048576 | tf_op jit(solution)/shard_map/gather | solution.py:11
  252.1 0.0 copy-done
  252.1 0.2 fusion.3
  252.3 25.6 %all_gather.3 = bf16[512,512]{1,0:T(8,128)(2,1)S(1)} all-gather(bf16[32,512]{1,0:T(8,128)(2,1)S(1)} %fusion.3), channel_id=1, replica_groups=mesh['mode'=8,'member'=16] {'member'}, dimensions={0}, use_global_device_ids=true | all-gather | bytes 557056 | tf_op jit(solution)/shard_map/all_gather | solution.py:35
  278.0 8.3 %fusion = bf16[6144,512]{0,1:T(8,128)(2,1)} fusion(bf16[512,512]{1,0:T(8,128)(2,1)S(1)} %all_gather.3, bf16[6144,512]{1,0:T(8,128)(2,1)} %param.10), kind=kOutput, calls=%fused_computation.2 | convolution fusion | flops 3224371200 | bytes 13107200 | tf_op jit(solution)/shard_map/dot_general | solution.py:38
  286.2 0.0 reduce-scatter.2.cloned.1.call-update
  286.2 0.0 copy-start.1
  286.3 0.7 dynamic-slice_bitcast_fusion.1
  286.9 0.7 dynamic-slice_bitcast_fusion
  287.6 0.2 convert_reduce_fusion
  287.7 0.7 multiply_add_fusion.1
  288.4 0.1 select_reduce_fusion
  288.5 0.8 all_to_all.9
  289.3 7.9 %all-to-all-start = ((s32[128,1,2]{2,1,0:T(1,128)}), s32[128,1,2]{2,1,0:T(1,128)S(1)}, u32[]{:S(2)}, u32[]{:S(2)}) async-start(s32[128,1,2]{2,1,0:T(1,128)} %bitcast.2), calls=%async_computation | async-start | bytes 131072 | tf_op jit(solution)/shard_map/all_to_all | solution.py:66
  297.3 31.5 %reduce-scatter.2.cloned.1.call-done = bf16[768,512]{0,1:T(8,128)(2,1)} async-done(((bf16[6144,512]{0,1:T(8,128)(2,1)}), bf16[768,512]{0,1:T(8,128)(2,1)}) %reduce-scatter.2.cloned.1.call-update) | async-done | bytes 786448 | tf_op jit(solution)/shard_map/reduce_scatter | solution.py:37
  328.8 1.4 copy.24
  330.2 0.7 reshape.112
  330.9 0.6 convolution_convert_fusion.1
  331.5 2.8 copy.25
  334.3 0.0 copy-start.3
  334.3 0.0 copy-start.2
  334.3 0.0 all-to-all-done
  334.3 8.4 %all-to-all-start.1 = ((bf16[128,2,3072]{2,1,0:T(2,128)(2,1)}), bf16[128,2,3072]{2,1,0:T(2,128)(2,1)S(1)}, u32[]{:S(2)}, u32[]{:S(2)}) async-start(bf16[128,2,3072]{2,1,0:T(2,128)(2,1)} %copy.25), calls=%async_computation.2 | async-start | bytes 3145728 | tf_op jit(solution)/shard_map/all_to_all | solution.py:59
  342.7 0.0 copy-done.1
  342.7 0.5 broadcast.73
  343.2 0.8 reduce.3
  344.0 0.1 eq.85
  344.1 22.9 %all-to-all-done.1 = bf16[128,2,3072]{2,1,0:T(2,128)(2,1)S(1)} async-done(((bf16[128,2,3072]{2,1,0:T(2,128)(2,1)}), bf16[128,2,3072]{2,1,0:T(2,128)(2,1)S(1)}, u32[]{:S(2)}, u32[]{:S(2)}) %all-to-all-start.1) | async-done | bytes 1572896 | tf_op jit(solution)/shard_map/all_to_all | solution.py:59
  367.1 0.6 reshape.102
  367.7 0.7 copy.26
  368.4 0.5 fusion.14
  368.9 0.0 copy-done.3
  368.9 0.2 fusion.2
  369.1 0.0 copy-done.2
  369.2 0.7 abs_reduce_fusion
  (3 shorter events, 0.0 us)
Async XLA Ops:
  6.5 245.6 %copy-start = (bf16[32,512]{1,0:T(8,128)(2,1)S(1)}, bf16[32,512]{1,0:T(8,128)(2,1)}, u32[]{:S(2)}) copy-start(bf16[32,512]{1,0:T(8,128)(2,1)} %param.9) | copy-start | bytes 98308
  6.5 322.2 %reduce-scatter.2.cloned.1.call-start = ((), (), s32[]{:S(2)}) async-start(), calls=%async_computation.3 | async-start | bytes 7077888 | tf_op jit(solution)/shard_map/reduce_scatter | solution.py:37
  286.2 56.4 %copy-start.1 = (s32[4,8]{1,0:T(4,128)S(1)}, s32[4,8]{1,0:T(4,128)}, u32[]{:S(2)}) copy-start(s32[4,8]{1,0:T(4,128)} %param.13) | copy-start | bytes 388
  289.3 45.0 %all-to-all-start = ((s32[128,1,2]{2,1,0:T(1,128)}), s32[128,1,2]{2,1,0:T(1,128)S(1)}, u32[]{:S(2)}, u32[]{:S(2)}) async-start(s32[128,1,2]{2,1,0:T(1,128)} %bitcast.2), calls=%async_computation | async-start | bytes 131072 | tf_op jit(solution)/shard_map/all_to_all | solution.py:66
  334.3 34.7 %copy-start.3 = (f32[8,6]{1,0:T(8,128)S(1)}, f32[8,6]{1,0:T(8,128)}, u32[]{:S(2)}) copy-start(f32[8,6]{1,0:T(8,128)} %param.14) | copy-start | bytes 580
  334.3 34.9 %copy-start.2 = (f32[4,8]{1,0:T(4,128)S(1)}, f32[4,8]{1,0:T(4,128)}, u32[]{:S(2)}) copy-start(f32[4,8]{1,0:T(4,128)} %param.15) | copy-start | bytes 388
  334.3 32.8 %all-to-all-start.1 = ((bf16[128,2,3072]{2,1,0:T(2,128)(2,1)}), bf16[128,2,3072]{2,1,0:T(2,128)(2,1)S(1)}, u32[]{:S(2)}, u32[]{:S(2)}) async-start(bf16[128,2,3072]{2,1,0:T(2,128)(2,1)} %copy.25), calls=%async_computation.2 | async-start | bytes 3145728 | tf_op jit(solution)/shard_map/all_to_all | solution.py:59
Sparse Core Ops, SparseCore 0:
  286.4 42.3 reduce-scatter.1
where the time goes:
time: 377 us
  local copies, waits for them, and re-layouts  254 us (67%)
  waiting for transfers between devices  54.5 us (14%)
  blocking collectives  25.6 us (7%)
  starting transfers between devices  16.3 us (4%)
  between operations  13.5 us (4%)
  matrix products  9.82 us (3%)
    gather x2, local copies, waits for them, and re-layouts, lagged_table(): lag_table = ground_accel[:, offsets]  245 us
    reduce_scatter x1, waiting for transfers between devices, local(): lax.psum_scatter(jnp.dot(mode_shapes, modal_resp, preferred_element_type=...  31.5 us
    all_gather x1, blocking collectives, local(): modal_resp = lax.all_gather(local_resp, 'member', axis=0, tiled=True)  25.6 us
    all_to_all x1, waiting for transfers between devices, local(): lax.all_to_all(outgoing.reshape(owner_total, slot_depth, -1).astype(jnp.b...  22.9 us
    all_to_all x1, starting transfers between devices, local(): lax.all_to_all(outgoing.reshape(owner_total, slot_depth, -1).astype(jnp.b...  8.39 us
    dot_general x1, matrix products, local(): jnp.dot(mode_shapes, modal_resp, preferred_element_type=jnp.float32)  8.25 us
    all_to_all x1, starting transfers between devices, local(): lax.all_to_all(slot_labels.reshape(owner_total, slot_depth), ('mode', 'me...  7.94 us
  transfers between devices with their start and end apart: 3, of which 2 were waited for; matrix products, arithmetic and copies ran while one was open for 2% of the time, Pallas kernels for 0%

commit v1 on v0

--- a/solution.py
+++ b/solution.py
@@ -7,9 +7,9 @@
 def lagged_table(ground_accel, tap_count):
     record_count, span_len = ground_accel.shape
     step_count = span_len - tap_count + 1
-    offsets = tap_count - 1 + jnp.arange(step_count)[None, :] - jnp.arange(tap_count)[:, None]
-    lag_table = ground_accel[:, offsets]
-    return jnp.transpose(lag_table, (1, 0, 2)).reshape(tap_count, record_count * step_count)
+    tiled = jnp.tile(ground_accel, (1, step_count + 1))[:, : step_count * (span_len + 1)]
+    windows = tiled.reshape(record_count, step_count, span_len + 1)[:, :, :tap_count]
+    return windows.reshape(record_count * step_count, tap_count)
 
 
 def local(
@@ -29,9 +29,9 @@
     n_mode = lax.axis_size("mode")
     n_member = lax.axis_size("member")
     lagged = lagged_table(ground_accel, tap_count)
-    local_resp = jnp.dot(modal_kernel, lagged, preferred_element_type=jnp.float32).astype(
-        jnp.bfloat16
-    )
+    local_resp = lax.dot_general(
+        modal_kernel[:, ::-1], lagged, (((1,), (1,)), ((), ())), preferred_element_type=jnp.float32
+    ).astype(jnp.bfloat16)
     modal_resp = lax.all_gather(local_resp, "member", axis=0, tiled=True)
     own_rows = mode_shapes.shape[0] // n_mode
     forces = lax.psum_scatter(

time: 377 us -> 135 us (0.36)
  local copies, waits for them, and re-layouts: 254 us -> 12.3 us
    gather x2 -> x0, local copies, waits for them, and re-layouts: 245 us -> none  [lagged_table(): lag_table = ground_accel[:, offsets]]
  transfers between devices with their start and end apart: 3 -> 3, of which waited for: 2 -> 2; matrix products, arithmetic and copies ran while one was open for 2% -> 7% of each run, Pallas kernels for 0% -> 0%
where the time goes in v1:
time: 135 us
  waiting for transfers between devices  54.5 us (40%)
  blocking collectives  25.6 us (19%)
  starting transfers between devices  16.3 us (12%)
  between operations  13.5 us (10%)
  local copies, waits for them, and re-layouts  12.3 us (9%)
  matrix products  9.84 us (7%)
  other arithmetic  2.5 us (2%)
    reduce_scatter x1, waiting for transfers between devices, local(): lax.psum_scatter(jnp.dot(mode_shapes, modal_resp, preferred_element_type=...  31.5 us
    all_gather x1, blocking collectives, local(): modal_resp = lax.all_gather(local_resp, 'member', axis=0, tiled=True)  25.6 us
    all_to_all x1, waiting for transfers between devices, local(): lax.all_to_all(outgoing.reshape(owner_total, slot_depth, -1).astype(jnp.b...  22.9 us
    all_to_all x1, starting transfers between devices, local(): lax.all_to_all(outgoing.reshape(owner_total, slot_depth, -1).astype(jnp.b...  8.39 us
    dot_general x1, matrix products, local(): jnp.dot(mode_shapes, modal_resp, preferred_element_type=jnp.float32)  8.28 us
    all_to_all x1, starting transfers between devices, local(): lax.all_to_all(slot_labels.reshape(owner_total, slot_depth), ('mode', 'me...  7.94 us
    convert_element_type x1, local copies, waits for them, and re-layouts, local(): outgoing.reshape(owner_total, slot_depth, -1).astype(jnp.bfloat16)  2.77 us
  transfers between devices with their start and end apart: 3, of which 2 were waited for; matrix products, arithmetic and copies ran while one was open for 7% of the time, Pallas kernels for 0%

profile of v1, /device:TPU:0, one launch (start us, length us, event | category | flops | bytes accessed | tf_op | source)
XLA Modules:
  0.0 134.6 jit_solution(4952856009396040289)
XLA Ops:
  6.5 0.0 copy-start
  6.5 0.0 reduce-scatter.2.cloned.1.call-start
  6.5 1.6 %rev.3 = bf16[32,512]{1,0:T(8,128)(2,1)S(1)} reverse(bf16[32,512]{1,0:T(8,128)(2,1)} %param.9), dimensions={1} | reverse | bytes 65536 | tf_op jit(solution)/shard_map/rev | solution.py:33
  8.2 0.7 tile.4
  8.9 0.6 tile.10
  9.6 0.2 slice.8
  9.8 0.1 copy.27
  9.9 0.2 convolution_convert_fusion.2
  10.2 25.6 %all_gather.3 = bf16[512,512]{1,0:T(8,128)(2,1)S(1)} all-gather(bf16[32,512]{1,0:T(8,128)(2,1)S(1)} %convolution_convert_fusion.2), channel_id=1, replica_groups=mesh['mode'=8,'member'=16] {'member'}, dimensions={0}, use_global_device_ids=true | all-gather | bytes 557056 | tf_op jit(solution)/shard_map/all_gather | solution.py:35
  35.8 8.3 %fusion = bf16[6144,512]{0,1:T(8,128)(2,1)} fusion(bf16[512,512]{1,0:T(8,128)(2,1)S(1)} %all_gather.3, bf16[6144,512]{1,0:T(8,128)(2,1)} %param.10), kind=kOutput, calls=%fused_computation.1 | convolution fusion | flops 3224371200 | bytes 13107200 | tf_op jit(solution)/shard_map/dot_general | solution.py:38
  44.1 0.0 reduce-scatter.2.cloned.1.call-update
  44.1 0.7 dynamic-slice_bitcast_fusion.1
  44.8 0.7 dynamic-slice_bitcast_fusion
  45.4 0.2 convert_reduce_fusion
  45.6 0.7 multiply_add_fusion.1
  46.3 0.1 select_reduce_fusion
  46.4 0.8 all_to_all.9
  47.2 7.9 %all-to-all-start = ((s32[128,1,2]{2,1,0:T(1,128)}), s32[128,1,2]{2,1,0:T(1,128)S(1)}, u32[]{:S(2)}, u32[]{:S(2)}) async-start(s32[128,1,2]{2,1,0:T(1,128)} %bitcast.2), calls=%async_computation | async-start | bytes 131072 | tf_op jit(solution)/shard_map/all_to_all | solution.py:66
  55.1 31.5 %reduce-scatter.2.cloned.1.call-done = bf16[768,512]{0,1:T(8,128)(2,1)} async-done(((bf16[6144,512]{0,1:T(8,128)(2,1)}), bf16[768,512]{0,1:T(8,128)(2,1)}) %reduce-scatter.2.cloned.1.call-update) | async-done | bytes 786448 | tf_op jit(solution)/shard_map/reduce_scatter | solution.py:37
  86.7 1.4 %copy.17 = bf16[768,512]{1,0:T(8,128)(2,1)S(1)} copy(bf16[768,512]{0,1:T(8,128)(2,1)} %reduce-scatter.2.cloned.1.call-done) | data formatting | bytes 1572864 | tf_op jit(solution)/shard_map/reduce_scatter | solution.py:37
  88.1 0.7 reshape.68
  88.7 0.6 convolution_convert_fusion.1
  89.4 2.8 %copy.18 = bf16[128,2,3072]{2,1,0:T(2,128)(2,1)} copy(bf16[128,2,3072]{2,0,1:T(8,128)(2,1)S(1)} %convolution_convert_fusion.1) | data formatting | bytes 3145728 | tf_op jit(solution)/shard_map/convert_element_type | solution.py:60
  92.1 0.0 copy-start.1
  92.1 0.0 all-to-all-done
  92.1 8.4 %all-to-all-start.1 = ((bf16[128,2,3072]{2,1,0:T(2,128)(2,1)}), bf16[128,2,3072]{2,1,0:T(2,128)(2,1)S(1)}, u32[]{:S(2)}, u32[]{:S(2)}) async-start(bf16[128,2,3072]{2,1,0:T(2,128)(2,1)} %copy.18), calls=%async_computation.2 | async-start | bytes 3145728 | tf_op jit(solution)/shard_map/all_to_all | solution.py:59
  100.5 0.0 copy-done.1
  100.6 0.5 broadcast.35
  101.1 0.8 reduce.3
  101.9 0.1 eq.85
  102.0 22.9 %all-to-all-done.1 = bf16[128,2,3072]{2,1,0:T(2,128)(2,1)S(1)} async-done(((bf16[128,2,3072]{2,1,0:T(2,128)(2,1)}), bf16[128,2,3072]{2,1,0:T(2,128)(2,1)S(1)}, u32[]{:S(2)}, u32[]{:S(2)}) %all-to-all-start.1) | async-done | bytes 1572896 | tf_op jit(solution)/shard_map/all_to_all | solution.py:59
  125.0 0.6 reshape.67
  125.6 0.7 copy.19
  126.3 0.0 copy-start.2
  126.3 0.5 fusion.11
  126.8 0.0 copy-done
  126.8 0.2 fusion.2
  127.0 0.0 copy-done.2
  127.0 0.7 abs_reduce_fusion
  (3 shorter events, 0.0 us)
Async XLA Ops:
  6.5 120.3 %copy-start = (f32[8,6]{1,0:T(8,128)S(1)}, f32[8,6]{1,0:T(8,128)}, u32[]{:S(2)}) copy-start(f32[8,6]{1,0:T(8,128)} %param.14) | copy-start | bytes 580
  6.5 80.1 %reduce-scatter.2.cloned.1.call-start = ((), (), s32[]{:S(2)}) async-start(), calls=%async_computation.3 | async-start | bytes 7077888 | tf_op jit(solution)/shard_map/reduce_scatter | solution.py:37
  47.2 45.0 %all-to-all-start = ((s32[128,1,2]{2,1,0:T(1,128)}), s32[128,1,2]{2,1,0:T(1,128)S(1)}, u32[]{:S(2)}, u32[]{:S(2)}) async-start(s32[128,1,2]{2,1,0:T(1,128)} %bitcast.2), calls=%async_computation | async-start | bytes 131072 | tf_op jit(solution)/shard_map/all_to_all | solution.py:66
  92.1 8.4 %copy-start.1 = (s32[4,8]{1,0:T(4,128)S(1)}, s32[4,8]{1,0:T(4,128)}, u32[]{:S(2)}) copy-start(s32[4,8]{1,0:T(4,128)} %param.13) | copy-start | bytes 388
  92.1 32.8 %all-to-all-start.1 = ((bf16[128,2,3072]{2,1,0:T(2,128)(2,1)}), bf16[128,2,3072]{2,1,0:T(2,128)(2,1)S(1)}, u32[]{:S(2)}, u32[]{:S(2)}) async-start(bf16[128,2,3072]{2,1,0:T(2,128)(2,1)} %copy.18), calls=%async_computation.2 | async-start | bytes 3145728 | tf_op jit(solution)/shard_map/all_to_all | solution.py:59
  126.3 0.7 copy-start.2
Sparse Core Ops, SparseCore 0:
  44.2 42.3 reduce-scatter.1

commit v2 on v1

v2 whole, which is shorter than its diff:
```python
import jax
import jax.numpy as jnp
from jax import lax
from jax.sharding import PartitionSpec as P


def lagged_table(ground_accel, tap_count):
    record_count, span_len = ground_accel.shape
    step_count = span_len - tap_count + 1
    tiled = jnp.tile(ground_accel, (1, step_count + 1))[:, : step_count * (span_len + 1)]
    windows = tiled.reshape(record_count, step_count, span_len + 1)[:, :, :tap_count]
    return windows.reshape(record_count * step_count, tap_count)


def local(
    ground_accel,
    modal_kernel,
    mode_shapes,
    member_owner,
    member_group,
    record_table,
    case_coef,
    gravity,
):
    tap_count = modal_kernel.shape[1]
    record_count = ground_accel.shape[0]
    comp_count = case_coef.shape[1]
    n_mode = lax.axis_size("mode")
    n_member = lax.axis_size("member")
    groups_here = gravity.shape[0]
    group_total = groups_here * n_mode * n_member
    lagged = lagged_table(ground_accel, tap_count)
    local_resp = lax.dot_general(
        modal_kernel[:, ::-1], lagged, (((1,), (1,)), ((), ())), preferred_element_type=jnp.float32
    ).astype(jnp.bfloat16)
    modal_resp = lax.all_gather(local_resp, "member", axis=0, tiled=True)
    partial = jnp.dot(mode_shapes, modal_resp, preferred_element_type=jnp.float32).astype(
        jnp.bfloat16
    )
    members_here = member_owner.shape[0]
    packed = partial.reshape(members_here, comp_count * partial.shape[1])
    group_index = member_owner[:, 0] * groups_here + member_group[:, 0]
    selector = (jnp.arange(group_total)[:, None] == group_index[None, :]).astype(jnp.bfloat16)
    group_part = jnp.dot(selector, packed, preferred_element_type=jnp.float32)
    by_mode = lax.psum_scatter(
        group_part.astype(jnp.bfloat16), "mode", scatter_dimension=0, tiled=True
    )
    group_sums = lax.psum_scatter(
        by_mode.astype(jnp.float32), "member", scatter_dimension=0, tiled=True
    )
    group_sums = group_sums.reshape(groups_here, comp_count, record_count, -1)
    case_mix = jnp.einsum("sc,gcrt->gsrt", case_coef, group_sums, precision=lax.Precision.HIGHEST)
    record_pick = (record_table[:, :, None] == jnp.arange(record_count)[None, None, :]).astype(
        jnp.float32
    )
    selected = jnp.sum(record_pick[:, :, :, None] * case_mix, axis=2)
    combined = gravity[:, :, None] + selected
    return jnp.max(jnp.abs(combined), axis=2)


def solution(mesh):
    placed = (
        P(),
        P(("mode", "member"), None),
        P("member", "mode"),
        P("member", None),
        P("member", None),
        P(("mode", "member"), None),
        P(),
        P(("mode", "member"), None),
    )
    return jax.shard_map(
        local, mesh=mesh, in_specs=placed, out_specs=P(("mode", "member"), None), check_vma=False
    )
```

time: 135 us -> 199 us (1.47)
  blocking collectives: 25.6 us -> 109 us
  waiting for transfers between devices: 54.5 us -> 33.9 us
  starting transfers between devices: 16.3 us -> 0.01 us
  local copies, waits for them, and re-layouts: 12.3 us -> 24.2 us
  matrix products: 9.84 us -> 16.2 us
    unnamed x0 -> x1, blocking collectives: none -> 83.7 us
    all_to_all x2 -> x0, waiting for transfers between devices: 22.9 us -> none  [the longest x1 22.9 us: local(): lax.all_to_all(outgoing.reshape(owner_total, slot_depth, -1).astype(jnp.b...]
    all_to_all x2 -> x0, starting transfers between devices: 16.3 us -> none  [the longest x1 8.39 us: local(): lax.all_to_all(outgoing.reshape(owner_total, slot_depth, -1).astype(jnp.b...]
    reshape x2, local copies, waits for them, and re-layouts: 1.28 us -> 11.5 us  [the longest x1 11.5 us: local(): packed = partial.reshape(members_here, comp_count * partial.shape[1])]
    dot_general x2 -> x1, matrix products: 1.11 us -> 7.56 us  [local(): group_part = jnp.dot(selector, packed, preferred_element_type=jnp.float32)]
    convert_element_type x1, local copies, waits for them, and re-layouts: 2.77 us -> 8.68 us  [local(): jnp.dot(mode_shapes, modal_resp, preferred_element_type=jnp.float32)]
    reduce_scatter x1, waiting for transfers between devices: 31.5 us -> 33.8 us  [local(): lax.psum_scatter(group_part.astype(jnp.bfloat16), 'mode', scatter_dimensi...]
  transfers between devices with their start and end apart: 3 -> 1, of which waited for: 2 -> 1; matrix products, arithmetic and copies ran while one was open for 7% -> 0% of each run, Pallas kernels for 0% -> 0%
where the time goes in v2:
time: 199 us
  blocking collectives  109 us (55%)
  waiting for transfers between devices  33.9 us (17%)
  local copies, waits for them, and re-layouts  24.2 us (12%)
  matrix products  16.2 us (8%)
  between operations  14.2 us (7%)
    unnamed x1, blocking collectives  83.7 us
    reduce_scatter x1, waiting for transfers between devices, local(): lax.psum_scatter(group_part.astype(jnp.bfloat16), 'mode', scatter_dimensi...  33.8 us
    all_gather x1, blocking collectives, local(): modal_resp = lax.all_gather(local_resp, 'member', axis=0, tiled=True)  25.6 us
    reshape x1, local copies, waits for them, and re-layouts, local(): packed = partial.reshape(members_here, comp_count * partial.shape[1])  11.5 us
    convert_element_type x1, local copies, waits for them, and re-layouts, local(): jnp.dot(mode_shapes, modal_resp, preferred_element_type=jnp.float32)  8.68 us
    dot_general x1, matrix products, local(): jnp.dot(mode_shapes, modal_resp, preferred_element_type=jnp.float32)  8.21 us
    dot_general x1, matrix products, local(): group_part = jnp.dot(selector, packed, preferred_element_type=jnp.float32)  7.56 us
  transfers between devices with their start and end apart: 1, of which 1 were waited for; matrix products, arithmetic and copies ran while one was open for 0% of the time, Pallas kernels for 0%

profile of v2, /device:TPU:0, one launch (start us, length us, event | category | flops | bytes accessed | tf_op | source)
XLA Modules:
  0.0 198.6 jit_solution(844657869856164750)
XLA Ops:
  6.5 0.0 copy-start
  6.5 0.0 reduce-scatter.2.cloned.1.call-start
  6.5 0.8 tile.4
  7.3 0.6 tile.10
  7.9 0.2 slice.8
  8.2 0.1 copy.21
  8.3 1.6 rev.3
  9.9 0.2 convolution_convert_fusion.2
  10.2 25.6 %all_gather.3 = bf16[512,512]{1,0:T(8,128)(2,1)S(1)} all-gather(bf16[32,512]{1,0:T(8,128)(2,1)S(1)} %convolution_convert_fusion.2), channel_id=1, replica_groups=mesh['mode'=8,'member'=16] {'member'}, dimensions={0}, use_global_device_ids=true | all-gather | bytes 557056 | tf_op jit(solution)/shard_map/all_gather | solution.py:36
  35.8 8.2 %fusion = bf16[6144,512]{0,1:T(8,128)(2,1)} fusion(bf16[512,512]{1,0:T(8,128)(2,1)S(1)} %all_gather.3, bf16[6144,512]{1,0:T(8,128)(2,1)} %param.10), kind=kOutput, calls=%fused_computation.1 | convolution fusion | flops 3224371200 | bytes 13107200 | tf_op jit(solution)/shard_map/dot_general | solution.py:37
  44.0 8.7 %copy.14 = bf16[6144,512]{1,0:T(8,128)(2,1)} copy(bf16[6144,512]{0,1:T(8,128)(2,1)} %fusion) | data formatting | bytes 12582912 | tf_op jit(solution)/shard_map/convert_element_type | solution.py:37
  52.7 0.0 copy-start.1
  52.7 0.0 copy-start.2
  52.7 11.5 %reshape.37 = bf16[1024,3072]{1,0:T(8,128)(2,1)} reshape(bf16[6144,512]{1,0:T(8,128)(2,1)} %copy.14) | data formatting | bytes 12582912 | tf_op jit(solution)/shard_map/reshape | solution.py:41
  64.2 0.0 copy-done.1
  64.2 0.0 copy-done.2
  64.2 0.0 copy-start.5
  64.2 0.0 copy-start.3
  64.2 0.0 copy-start.4
  64.3 7.6 %convolution_convert_fusion.1 = bf16[512,3072]{1,0:T(8,128)(2,1)} fusion(bf16[1024,3072]{1,0:T(8,128)(2,1)} %reshape.37, s32[1024]{0:T(1024)S(1)} %bitcast.28), kind=kOutput, calls=%fused_computation.2 | convolution fusion | flops 3223322624 | bytes 9441280 | tf_op jit(solution)/shard_map/dot_general | solution.py:44
  71.8 0.0 reduce-scatter.2.cloned.1.call-update
  71.8 0.0 copy-done.5
  71.9 0.6 dynamic-slice
  73.1 0.0 copy-done.3
  73.1 33.8 %reduce-scatter.2.cloned.1.call-done = bf16[64,3072]{1,0:T(8,128)(2,1)} async-done(((bf16[512,3072]{1,0:T(8,128)(2,1)}), bf16[64,3072]{1,0:T(8,128)(2,1)}) %reduce-scatter.2.cloned.1.call-update) | async-done | bytes 393232 | tf_op jit(solution)/shard_map/reduce_scatter | solution.py:45
  107.0 83.7 %all-reduce.2 = f32[64,3072]{1,0:T(8,128)S(1)} all-reduce(bf16[64,3072]{1,0:T(8,128)(2,1)} %reduce-scatter.2.cloned.1.call-done), channel_id=3, replica_groups=mesh['mode'=8,'member'=16] {'member'}, use_global_device_ids=true, to_apply=%region_1.0.clone | all-reduce | flops 196608 | bytes 1179648
  190.8 0.0 copy-done
  190.8 0.2 fusion.2
  191.0 0.0 copy-done.4
  191.0 0.7 abs_reduce_fusion
  (5 shorter events, 0.1 us)
Async XLA Ops:
  6.5 184.2 %copy-start = (f32[8,6]{1,0:T(8,128)S(1)}, f32[8,6]{1,0:T(8,128)}, u32[]{:S(2)}) copy-start(f32[8,6]{1,0:T(8,128)} %param.14) | copy-start | bytes 580
  6.5 100.4 %reduce-scatter.2.cloned.1.call-start = ((), (), s32[]{:S(2)}) async-start(), calls=%async_computation.1 | async-start | bytes 3538944 | tf_op jit(solution)/shard_map/reduce_scatter | solution.py:45
  52.7 11.5 %copy-start.1 = (s32[1024,1]{0,1:T(1,128)S(1)}, s32[1024,1]{0,1:T(1,128)}, u32[]{:S(2)}) copy-start(s32[1024,1]{0,1:T(1,128)} %param.12) | copy-start | bytes 12292
  52.7 11.5 %copy-start.2 = (s32[1024,1]{0,1:T(1,128)S(1)}, s32[1024,1]{0,1:T(1,128)}, u32[]{:S(2)}) copy-start(s32[1024,1]{0,1:T(1,128)} %param.11) | copy-start | bytes 12292
  64.2 7.6 %copy-start.5 = (u32[128]{0:T(128)S(1)}, u32[128]{0:T(128)}, u32[]{:S(2)}) copy-start(u32[128]{0:T(128)} %constant.11) | copy-start | bytes 1540
  64.2 8.9 %copy-start.3 = (s32[4,8]{1,0:T(4,128)S(1)}, s32[4,8]{1,0:T(4,128)}, u32[]{:S(2)}) copy-start(s32[4,8]{1,0:T(4,128)} %param.13) | copy-start | bytes 388
  64.2 126.7 %copy-start.4 = (f32[4,8]{1,0:T(4,128)S(1)}, f32[4,8]{1,0:T(4,128)}, u32[]{:S(2)}) copy-start(f32[4,8]{1,0:T(4,128)} %param.15) | copy-start | bytes 388
Sparse Core Ops, SparseCore 0:
  72.0 34.9 reduce-scatter.1

commit v3 on v2

--- a/solution.py
+++ b/solution.py
@@ -42,18 +42,19 @@
     group_index = member_owner[:, 0] * groups_here + member_group[:, 0]
     selector = (jnp.arange(group_total)[:, None] == group_index[None, :]).astype(jnp.bfloat16)
     group_part = jnp.dot(selector, packed, preferred_element_type=jnp.float32)
-    by_mode = lax.psum_scatter(
-        group_part.astype(jnp.bfloat16), "mode", scatter_dimension=0, tiled=True
-    )
-    group_sums = lax.psum_scatter(
-        by_mode.astype(jnp.float32), "member", scatter_dimension=0, tiled=True
-    )
-    group_sums = group_sums.reshape(groups_here, comp_count, record_count, -1)
-    case_mix = jnp.einsum("sc,gcrt->gsrt", case_coef, group_sums, precision=lax.Precision.HIGHEST)
-    record_pick = (record_table[:, :, None] == jnp.arange(record_count)[None, None, :]).astype(
+    group_part = group_part.reshape(group_total, comp_count, record_count, -1)
+    all_records = lax.all_gather(record_table, ("mode", "member"), axis=0, tiled=True)
+    record_pick = (all_records[:, :, None] == jnp.arange(record_count)[None, None, :]).astype(
         jnp.float32
     )
-    selected = jnp.sum(record_pick[:, :, :, None] * case_mix, axis=2)
+    case_mix = jnp.einsum("sc,gcrt->gsrt", case_coef, group_part, precision=lax.Precision.HIGHEST)
+    share = jnp.sum(record_pick[:, :, :, None] * case_mix, axis=2)
+    owner_total = n_mode * n_member
+    share = share.reshape(owner_total, groups_here, share.shape[1], share.shape[2])
+    received = lax.all_to_all(
+        share.astype(jnp.bfloat16), ("mode", "member"), split_axis=0, concat_axis=0, tiled=True
+    )
+    selected = jnp.sum(received.astype(jnp.float32), axis=0)
     combined = gravity[:, :, None] + selected
     return jnp.max(jnp.abs(combined), axis=2)
 

time: 199 us -> 171 us (0.86)
  waiting for transfers between devices: 33.9 us -> 0 us
  between operations: 14.2 us -> 0.11 us
  matrix products: 16.2 us -> 30.1 us
  local copies, waits for them, and re-layouts: 24.2 us -> 32.3 us
  blocking collectives: 109 us -> 107 us
    unnamed x1 -> x0, blocking collectives: 83.7 us -> none
    all_gather x0 -> x1, blocking collectives: none -> 55.2 us  [local(): lax.all_gather(record_table, ('mode', 'member'), axis=0, tiled=True)]
    reduce_scatter x1 -> x0, waiting for transfers between devices: 33.8 us -> none  [local(): lax.psum_scatter(group_part.astype(jnp.bfloat16), 'mode', scatter_dimensi...]
    all_to_all x0 -> x1, blocking collectives: none -> 25.9 us  [local(): lax.all_to_all(share.astype(jnp.bfloat16), ('mode', 'member'), split_axis...]
    dot_general x1, matrix products: 0.19 us -> 16.1 us  [local(): jnp.einsum('sc,gcrt->gsrt', case_coef, group_part, precision=lax.Precisio...]
    dot_general x0 -> x1, local copies, waits for them, and re-layouts: none -> 8.71 us  [local(): group_part = jnp.dot(selector, packed, preferred_element_type=jnp.float32)]
  transfers between devices with their start and end apart: 1 -> 0, of which waited for: 1 -> 0; matrix products, arithmetic and copies ran while one was open for 0% -> 0% of each run, Pallas kernels for 0% -> 0%
where the time goes in v3:
time: 171 us; the launch traced here: 170 us
  blocking collectives  107 us (63%)
  local copies, waits for them, and re-layouts  32.3 us (19%)
  matrix products  30.1 us (18%)
    all_gather x1, blocking collectives, local(): lax.all_gather(record_table, ('mode', 'member'), axis=0, tiled=True)  55.2 us
    all_to_all x1, blocking collectives, local(): lax.all_to_all(share.astype(jnp.bfloat16), ('mode', 'member'), split_axis...  25.9 us
    all_gather x1, blocking collectives, local(): modal_resp = lax.all_gather(local_resp, 'member', axis=0, tiled=True)  25.6 us
    dot_general x1, matrix products, local(): jnp.einsum('sc,gcrt->gsrt', case_coef, group_part, precision=lax.Precisio...  16.1 us
    reshape x1, local copies, waits for them, and re-layouts, local(): packed = partial.reshape(members_here, comp_count * partial.shape[1])  11.5 us
    dot_general x1, local copies, waits for them, and re-layouts, local(): group_part = jnp.dot(selector, packed, preferred_element_type=jnp.float32)  8.71 us
    convert_element_type x1, local copies, waits for them, and re-layouts, local(): jnp.dot(mode_shapes, modal_resp, preferred_element_type=jnp.float32)  8.68 us
    dot_general x1, matrix products, local(): jnp.dot(mode_shapes, modal_resp, preferred_element_type=jnp.float32)  8.21 us

profile of v3, /device:TPU:0, one launch (start us, length us, event | category | flops | bytes accessed | tf_op | source)
XLA Modules:
  0.0 170.4 jit_solution(5427172519029143191)
XLA Ops:
  0.0 0.0 copy-start
  0.0 0.8 tile.4
  0.8 0.6 tile.10
  1.4 0.2 slice.8
  1.6 0.1 copy.25
  1.8 1.6 rev.3
  3.4 0.2 convolution_convert_fusion.1
  3.7 25.6 %all_gather.7 = bf16[512,512]{1,0:T(8,128)(2,1)S(1)} all-gather(bf16[32,512]{1,0:T(8,128)(2,1)S(1)} %convolution_convert_fusion.1), channel_id=1, replica_groups=mesh['mode'=8,'member'=16] {'member'}, dimensions={0}, use_global_device_ids=true | all-gather | bytes 557056 | tf_op jit(solution)/shard_map/all_gather | solution.py:36
  29.3 8.2 %fusion.3 = bf16[6144,512]{0,1:T(8,128)(2,1)} fusion(bf16[512,512]{1,0:T(8,128)(2,1)S(1)} %all_gather.7, bf16[6144,512]{1,0:T(8,128)(2,1)} %param.10), kind=kOutput, calls=%fused_computation.5 | convolution fusion | flops 3224371200 | bytes 13107200 | tf_op jit(solution)/shard_map/dot_general | solution.py:37
  37.5 8.7 %copy.13 = bf16[6144,512]{1,0:T(8,128)(2,1)} copy(bf16[6144,512]{0,1:T(8,128)(2,1)} %fusion.3) | data formatting | bytes 12582912 | tf_op jit(solution)/shard_map/convert_element_type | solution.py:37
  46.2 11.5 %reshape.38 = bf16[1024,3072]{1,0:T(8,128)(2,1)} reshape(bf16[6144,512]{1,0:T(8,128)(2,1)} %copy.13) | data formatting | bytes 12582912 | tf_op jit(solution)/shard_map/reshape | solution.py:41
  57.6 0.0 copy-start.3
  57.6 0.0 copy-start.1
  57.6 0.0 copy-start.2
  57.6 8.7 %copy.18 = bf16[3072,1024]{1,0:T(8,128)(2,1)} copy(bf16[3072,1024]{0,1:T(8,128)(2,1)} %bitcast.32) | data formatting | bytes 12582912 | tf_op jit(solution)/shard_map/dot_general | solution.py:44
  66.4 0.0 copy-done.3
  66.4 55.2 %all-gather = s32[128,4,8]{2,1,0:T(4,128)S(1)} all-gather(s32[1,4,8]{2,1,0:T(4,128)S(1)} %bitcast.40), channel_id=1, replica_groups=mesh['mode'=8,'member'=16] {'mode','member'}, dimensions={0}, use_global_device_ids=true | all-gather | bytes 16512 | tf_op jit(solution)/shard_map/all_gather | solution.py:46
  121.6 0.2 fusion.10
  121.8 0.0 copy-done.1
  121.8 0.0 copy-done.2
  121.8 5.6 %fusion.7 = f32[512,6,4,128]{3,0,2,1:T(8,128)S(1)} fusion(bf16[6,4,128,1024]{3,2,1,0:T(8,128)(2,1)} %bitcast.33, s32[1024]{0:T(1024)S(1)} %bitcast.39), kind=kOutput, calls=%fused_computation.9 | convolution fusion | flops 3221749760 | bytes 12587008 | tf_op jit(solution)/shard_map/dot_general | solution.py:44
  127.4 0.0 copy-done
  127.4 0.0 copy-start.4
  127.4 16.1 %fusion = bf16[512,8,128]{2,1,0:T(8,128)(2,1)S(1)} fusion(f32[512,8,4]{1,2,0:T(4,128)S(1)} %fusion.10, f32[512,6,4,128]{3,0,2,1:T(8,128)S(1)} %fusion.7, f32[8,6]{1,0:T(8,128)S(1)} %copy-done), kind=kOutput, calls=%fused_computation.2 | convolution fusion | flops 154664960 | bytes 7405760 | tf_op jit(solution)/shard_map/sc,gcrt->gsrt/dot_general | solution.py:50
  143.5 25.9 %all_to_all.5 = bf16[128,4,8,128]{3,2,1,0:T(8,128)(2,1)S(1)} all-to-all(bf16[128,4,8,128]{3,2,1,0:T(8,128)(2,1)S(1)} %bitcast.38), channel_id=1, replica_groups=mesh['mode'=8,'member'=16] {'mode','member'}, dimensions={0} | all-to-all | bytes 2097152 | tf_op jit(solution)/shard_map/all_to_all | solution.py:54
  169.4 0.2 convert_reduce_fusion
  169.6 0.0 copy-done.4
  169.6 0.7 abs_reduce_fusion
  (2 shorter events, 0.0 us)
Async XLA Ops:
  0.0 127.4 %copy-start = (f32[8,6]{1,0:T(8,128)S(1)}, f32[8,6]{1,0:T(8,128)}, u32[]{:S(2)}) copy-start(f32[8,6]{1,0:T(8,128)} %param.14) | copy-start | bytes 580
  57.6 8.7 %copy-start.3 = (s32[4,8]{1,0:T(4,128)S(1)}, s32[4,8]{1,0:T(4,128)}, u32[]{:S(2)}) copy-start(s32[4,8]{1,0:T(4,128)} %param.13) | copy-start | bytes 388
  57.6 64.1 %copy-start.1 = (s32[1024,1]{0,1:T(1,128)S(1)}, s32[1024,1]{0,1:T(1,128)}, u32[]{:S(2)}) copy-start(s32[1024,1]{0,1:T(1,128)} %param.12) | copy-start | bytes 12292
  57.6 64.2 %copy-start.2 = (s32[1024,1]{0,1:T(1,128)S(1)}, s32[1024,1]{0,1:T(1,128)}, u32[]{:S(2)}) copy-start(s32[1024,1]{0,1:T(1,128)} %param.11) | copy-start | bytes 12292
  127.4 42.2 %copy-start.4 = (f32[4,8]{1,0:T(4,128)S(1)}, f32[4,8]{1,0:T(4,128)}, u32[]{:S(2)}) copy-start(f32[4,8]{1,0:T(4,128)} %param.15) | copy-start | bytes 388

commit v4 on v3

v4 whole, which is shorter than its diff:
```python
import functools

import jax
import jax.numpy as jnp
from jax import lax
from jax.experimental import pallas as pl
from jax.experimental.pallas import tpu as pltpu
from jax.sharding import PartitionSpec as P


def lagged_table(ground_accel, tap_count):
    record_count, span_len = ground_accel.shape
    step_count = span_len - tap_count + 1
    tiled = jnp.tile(ground_accel, (1, step_count + 1))[:, : step_count * (span_len + 1)]
    windows = tiled.reshape(record_count, step_count, span_len + 1)[:, :, :tap_count]
    return windows.reshape(record_count * step_count, tap_count)


def group_kernel(ms_ref, resp_ref, sel_ref, q_ref, p_scr, *, comps, tile):
    @pl.when(pl.program_id(0) == 0)
    def _():
        q_ref[...] = jnp.zeros_like(q_ref)

    part = jnp.dot(ms_ref[...], resp_ref[...], preferred_element_type=jnp.float32)
    part = part.astype(jnp.bfloat16).astype(jnp.float32)
    slabs = p_scr.shape[0]
    for k in range(slabs):
        p_scr[k] = part[:, k * 128 : (k + 1) * 128]
    sel = sel_ref[...]
    for c in range(comps):
        comp_rows = jnp.concatenate(
            [p_scr[k, pl.ds(c, tile, stride=comps), :] for k in range(slabs)], axis=1
        ).astype(jnp.bfloat16)
        q_ref[c] += jnp.dot(sel, comp_rows, preferred_element_type=jnp.float32)


def group_parts(mode_shapes, modal_resp, selector, comps, tile=128):
    modes = mode_shapes.shape[1]
    groups, members = selector.shape
    width = modal_resp.shape[1]
    return pl.pallas_call(
        functools.partial(group_kernel, comps=comps, tile=tile),
        grid=(members // tile,),
        in_specs=[
            pl.BlockSpec((tile * comps, modes), lambda k: (k, 0)),
            pl.BlockSpec((modes, width), lambda k: (0, 0)),
            pl.BlockSpec((groups, tile), lambda k: (0, k)),
        ],
        out_specs=pl.BlockSpec((comps, groups, width), lambda k: (0, 0, 0)),
        out_shape=jax.ShapeDtypeStruct((comps, groups, width), jnp.float32),
        scratch_shapes=[pltpu.VMEM((width // 128, tile * comps, 128), jnp.float32)],
        compiler_params=pltpu.CompilerParams(vmem_limit_bytes=48 * 1024 * 1024),
    )(mode_shapes, modal_resp, selector)


def local(
    ground_accel,
    modal_kernel,
    mode_shapes,
    member_owner,
    member_group,
    record_table,
    case_coef,
    gravity,
):
    tap_count = modal_kernel.shape[1]
    record_count = ground_accel.shape[0]
    comp_count = case_coef.shape[1]
    n_mode = lax.axis_size("mode")
    n_member = lax.axis_size("member")
    groups_here, case_count = gravity.shape
    owner_total = n_mode * n_member
    group_total = groups_here * owner_total
    lagged = lagged_table(ground_accel, tap_count)
    local_resp = lax.dot_general(
        modal_kernel[:, ::-1], lagged, (((1,), (1,)), ((), ())), preferred_element_type=jnp.float32
    ).astype(jnp.bfloat16)
    resp_rows, width = local_resp.shape
    rec_col = lax.all_gather(record_table, "mode", axis=0, tiled=True).reshape(-1)
    rec_rows = -(-rec_col.shape[0] // width)
    rec_rows = -(-rec_rows // 8) * 8
    rec_block = jnp.zeros((rec_rows * width,), jnp.bfloat16).at[: rec_col.shape[0]].set(
        rec_col.astype(jnp.bfloat16)
    )
    payload = jnp.concatenate([local_resp, rec_block.reshape(rec_rows, width)], axis=0)
    gathered = lax.all_gather(payload, "member", axis=0)
    modal_resp = gathered[:, :resp_rows].reshape(n_member * resp_rows, width)
    rec_all = gathered[:, resp_rows:].reshape(n_member, -1)[:, : rec_col.shape[0]]
    rec_all = rec_all.astype(jnp.int32).reshape(n_member, n_mode, groups_here, case_count)
    rec_all = jnp.transpose(rec_all, (1, 0, 2, 3)).reshape(group_total, case_count)

    group_index = member_owner[:, 0] * groups_here + member_group[:, 0]
    selector = (jnp.arange(group_total)[:, None] == group_index[None, :]).astype(jnp.bfloat16)
    group_part = group_parts(mode_shapes, modal_resp, selector, comp_count)
    group_part = group_part.reshape(comp_count, group_total, record_count, -1)
    record_pick = (rec_all[:, :, None] == jnp.arange(record_count)[None, None, :]).astype(
        jnp.float32
    )
    picked = jnp.sum(record_pick[None, :, :, :, None] * group_part[:, :, None, :, :], axis=3)
    share = jnp.sum(case_coef.T[:, None, :, None] * picked, axis=0)
    share = share.reshape(owner_total, groups_here, case_count, share.shape[-1])
    received = lax.all_to_all(
        share.astype(jnp.bfloat16), ("mode", "member"), split_axis=0, concat_axis=0, tiled=True
    )
    selected = jnp.sum(received.astype(jnp.float32), axis=0)
    combined = gravity[:, :, None] + selected
    return jnp.max(jnp.abs(combined), axis=2)


def solution(mesh):
    placed = (
        P(),
        P(("mode", "member"), None),
        P("member", "mode"),
        P("member", None),
        P("member", None),
        P(("mode", "member"), None),
        P(),
        P(("mode", "member"), None),
    )
    return jax.shard_map(
        local, mesh=mesh, in_specs=placed, out_specs=P(("mode", "member"), None), check_vma=False
    )
```

time: 171 us -> 118 us (0.69)
  blocking collectives: 107 us -> 63.7 us
  matrix products: 30.1 us -> 0.24 us
  other arithmetic: 1.16 us -> 24 us
  local copies, waits for them, and re-layouts: 32.3 us -> 12.4 us
  Pallas kernels: 0 us -> 17.1 us
    all_gather x2, blocking collectives: 80.8 us -> 38.2 us  [the longest x1 26.1 us: local(): gathered = lax.all_gather(payload, 'member', axis=0)]
    dot_general x3 -> x0, matrix products: 29.9 us -> none  [the longest x1 16.1 us: local(): jnp.einsum('sc,gcrt->gsrt', case_coef, group_part, precision=lax.Precisio...]
    reduce_sum x0 -> x2, other arithmetic: none -> 22 us  [the longest x1 16.5 us: local(): jnp.sum(record_pick[None, :, :, :, None] * group_part[:, :, None, :, :],...]
    pallas_call x0 -> x1, Pallas kernels: none -> 17.1 us  [group_parts(): pl.pallas_call(functools.partial(group_kernel, comps=comps, tile=tile), g...]
    reshape x1, local copies, waits for them, and re-layouts: 11.5 us -> 0.02 us  [local(): rec_block.reshape(rec_rows, width)]
    dot_general x1 -> x0, local copies, waits for them, and re-layouts: 8.71 us -> none  [local(): group_part = jnp.dot(selector, packed, preferred_element_type=jnp.float32)]
    convert_element_type x1 -> x2, local copies, waits for them, and re-layouts: 8.68 us -> 0.5 us  [the longest x1 0.4 us: local(): (rec_all[:, :, None] == jnp.arange(record_count)[None, None, :]).astype(j...]
    mul x0 -> x1, local copies, waits for them, and re-layouts: none -> 7.61 us  [local(): record_pick[None, :, :, :, None] * group_part[:, :, None, :, :]]
where the time goes in v4:
time: 118 us
  blocking collectives  63.7 us (54%)
  other arithmetic  24 us (20%)
  Pallas kernels  17.1 us (14%)
  local copies, waits for them, and re-layouts  12.4 us (11%)
    all_gather x1, blocking collectives, local(): gathered = lax.all_gather(payload, 'member', axis=0)  26.1 us
    all_to_all x1, blocking collectives, local(): lax.all_to_all(share.astype(jnp.bfloat16), ('mode', 'member'), split_axis...  25.5 us
    pallas_call x1, Pallas kernels, group_parts(): pl.pallas_call(functools.partial(group_kernel, comps=comps, tile=tile), g...  17.1 us
    reduce_sum x1, other arithmetic, local(): jnp.sum(record_pick[None, :, :, :, None] * group_part[:, :, None, :, :],...  16.5 us
    all_gather x1, blocking collectives, local(): lax.all_gather(record_table, 'mode', axis=0, tiled=True).reshape(-1)  12.1 us
    mul x1, local copies, waits for them, and re-layouts, local(): record_pick[None, :, :, :, None] * group_part[:, :, None, :, :]  7.61 us
    reduce_sum x1, other arithmetic, local(): share = jnp.sum(case_coef.T[:, None, :, None] * picked, axis=0)  5.5 us

profile of v4, /device:TPU:0, one launch (start us, length us, event | category | flops | bytes accessed | tf_op | source)
XLA Modules:
  0.0 117.5 jit_solution(4502734526874912787)
XLA Ops:
  0.0 0.7 tile.4
  0.7 0.6 tile.10
  1.4 0.2 slice.31
  1.6 0.1 copy.23
  1.7 1.6 %rev.3 = bf16[32,512]{1,0:T(8,128)(2,1)S(1)} reverse(bf16[32,512]{1,0:T(8,128)(2,1)} %param.11), dimensions={1} | reverse | bytes 65536 | tf_op jit(solution)/shard_map/rev | solution.py:76
  3.4 12.1 %all-gather.1 = s32[8,4,8]{2,1,0:T(4,128)S(1)} all-gather(s32[1,4,8]{2,1,0:T(4,128)} %bitcast.31), channel_id=1, replica_groups=mesh['mode'=8,'member'=16] {'mode'}, dimensions={0}, use_global_device_ids=true | all-gather | bytes 1152 | tf_op jit(solution)/shard_map/all_gather | solution.py:79
  15.5 0.1 convert_element_type.31
  15.7 0.2 convolution_convert_fusion
  15.9 26.1 %all-gather = bf16[640,512]{1,0:T(8,128)(2,1)S(1)} all-gather(bf16[40,512]{1,0:T(8,128)(2,1)S(1)} %pad_maximum_fusion), channel_id=2, replica_groups=mesh['mode'=8,'member'=16] {'member'}, dimensions={0}, use_global_device_ids=true | all-gather | bytes 696320 | tf_op jit(solution)/shard_map/all_gather | solution.py:86
  42.1 0.7 multiply_add_fusion
  42.8 0.3 fusion.sel_ref
  43.1 0.0 copy-start
  43.1 17.1 %shard_map.82 = f32[6,512,512]{2,1,0:T(8,128)} custom-call(bf16[6144,512]{1,0:T(8,128)(2,1)} %ms_ref.1, bf16[512,512]{1,0:T(8,128)(2,1)S(1)} %bitcast.19, bf16[512,1024]{1,0:T(8,128)(2,1)S(1)} %fusion.sel_ref), custom_call_target="tpu_custom_call" | custom-call | tf_op jit(solution)/shard_map/pallas_call | solution.py:41
  60.2 7.6 %mul.38 = f32[6,512,4,128]{3,2,1,0:T(4,128)} reshape(f32[6,512,512]{2,1,0:T(8,128)} %shard_map.82) | data formatting | bytes 12582912 | tf_op jit(solution)/shard_map/mul | solution.py:99
  67.8 0.5 copy.17
  68.3 0.1 copy.18
  68.4 0.1 copy.19
  68.5 0.4 copy.20
  69.0 0.0 copy-done
  69.0 0.1 copy.16
  69.0 16.5 %multiply_reduce_fusion = f32[6,512,8,128]{3,2,1,0:T(8,128)} fusion(f32[6,512,4,128]{3,2,1,0:T(4,128)} %mul.38, f32[512,8,4]{1,2,0:T(4,128)S(1)} %copy.20), kind=kLoop, calls=%fused_computation | loop fusion | flops 22020096 | bytes 18939904 | tf_op jit(solution)/shard_map/reduce_sum | solution.py:99
  85.6 0.0 copy-start.1
  85.6 5.5 %multiply_reduce_fusion.1 = bf16[512,8,128]{2,1,0:T(8,128)(2,1)S(1)} fusion(f32[6,512,8,128]{3,2,1,0:T(8,128)} %multiply_reduce_fusion, f32[6,8]{1,0:T(8,128)S(1)} %copy.16), kind=kLoop, calls=%fused_computation.1 | loop fusion | flops 5767168 | bytes 13631680 | tf_op jit(solution)/shard_map/reduce_sum | solution.py:100
  91.1 25.5 %all_to_all.5 = bf16[128,4,8,128]{3,2,1,0:T(8,128)(2,1)S(1)} all-to-all(bf16[128,4,8,128]{3,2,1,0:T(8,128)(2,1)S(1)} %bitcast.20), channel_id=1, replica_groups=mesh['mode'=8,'member'=16] {'mode','member'}, dimensions={0} | all-to-all | bytes 2097152 | tf_op jit(solution)/shard_map/all_to_all | solution.py:102
  116.6 0.2 convert_reduce_fusion
  116.8 0.0 copy-done.1
  116.8 0.7 abs_reduce_fusion
  (10 shorter events, 0.2 us)
Async XLA Ops:
  43.1 25.9 %copy-start = (f32[8,6]{1,0:T(8,128)S(1)}, f32[8,6]{1,0:T(8,128)}, u32[]{:S(2)}) copy-start(f32[8,6]{1,0:T(8,128)} %param.16) | copy-start | bytes 580
  85.6 31.2 %copy-start.1 = (f32[4,8]{1,0:T(4,128)S(1)}, f32[4,8]{1,0:T(4,128)}, u32[]{:S(2)}) copy-start(f32[4,8]{1,0:T(4,128)} %param.17) | copy-start | bytes 388

commit v5 on v4

--- a/solution.py
+++ b/solution.py
@@ -16,41 +16,73 @@
     return windows.reshape(record_count * step_count, tap_count)
 
 
-def group_kernel(ms_ref, resp_ref, sel_ref, q_ref, p_scr, *, comps, tile):
-    @pl.when(pl.program_id(0) == 0)
-    def _():
-        q_ref[...] = jnp.zeros_like(q_ref)
-
+def group_kernel(
+    coef_ref, ms_ref, resp_ref, sel_ref, pick_ref, out_ref, p_scr, q_scr, *, comps, tile, records
+):
+    k = pl.program_id(0)
+    rows = tile * comps
+    slabs, _, lanes = p_scr.shape
     part = jnp.dot(ms_ref[...], resp_ref[...], preferred_element_type=jnp.float32)
     part = part.astype(jnp.bfloat16).astype(jnp.float32)
-    slabs = p_scr.shape[0]
-    for k in range(slabs):
-        p_scr[k] = part[:, k * 128 : (k + 1) * 128]
-    sel = sel_ref[...]
-    for c in range(comps):
-        comp_rows = jnp.concatenate(
-            [p_scr[k, pl.ds(c, tile, stride=comps), :] for k in range(slabs)], axis=1
-        ).astype(jnp.bfloat16)
-        q_ref[c] += jnp.dot(sel, comp_rows, preferred_element_type=jnp.float32)
+    for l in range(slabs):
+        p_scr[l, pl.ds(pl.multiple_of(k * rows, 8), rows), :] = part[:, l * lanes : (l + 1) * lanes]
+
+    @pl.when(k == pl.num_programs(0) - 1)
+    def _():
+        sel = sel_ref[...]
+        groups, members = sel.shape
+        for c in range(comps):
+            comp_rows = jnp.concatenate(
+                [p_scr[l, pl.ds(c, members, stride=comps), :] for l in range(slabs)], axis=1
+            ).astype(jnp.bfloat16)
+            q_scr[c] = jnp.dot(sel, comp_rows, preferred_element_type=jnp.float32)
+        cases = coef_ref.shape[0]
+        steps = q_scr.shape[2] // records
+        chunk = 64
+
+        def mix(i, carry):
+            g0 = pl.multiple_of(i * chunk, chunk)
+            for s in range(cases):
+                acc = jnp.zeros((chunk, steps), jnp.float32)
+                for r in range(records):
+                    mixed = coef_ref[s, 0] * q_scr[0, pl.ds(g0, chunk), pl.ds(r * steps, steps)]
+                    for c in range(1, comps):
+                        mixed = mixed + coef_ref[s, c] * q_scr[
+                            c, pl.ds(g0, chunk), pl.ds(r * steps, steps)
+                        ]
+                    pick = pick_ref[pl.ds(g0, chunk), pl.ds(s * records + r, 1)]
+                    acc = acc + pick * mixed
+                out_ref[pl.ds(g0 * cases + s, chunk, stride=cases), :] = acc
+            return carry
+
+        lax.fori_loop(0, groups // chunk, mix, 0)
 
 
-def group_parts(mode_shapes, modal_resp, selector, comps, tile=128):
-    modes = mode_shapes.shape[1]
+def group_shares(case_coef, mode_shapes, modal_resp, selector, record_pick, comps, tile=128):
+    rows, modes = mode_shapes.shape
     groups, members = selector.shape
     width = modal_resp.shape[1]
+    cases = case_coef.shape[0]
+    records = record_pick.shape[1] // cases
+    steps = width // records
     return pl.pallas_call(
-        functools.partial(group_kernel, comps=comps, tile=tile),
+        functools.partial(group_kernel, comps=comps, tile=tile, records=records),
         grid=(members // tile,),
         in_specs=[
+            pl.BlockSpec(memory_space=pltpu.SMEM),
             pl.BlockSpec((tile * comps, modes), lambda k: (k, 0)),
             pl.BlockSpec((modes, width), lambda k: (0, 0)),
-            pl.BlockSpec((groups, tile), lambda k: (0, k)),
+            pl.BlockSpec((groups, members), lambda k: (0, 0)),
+            pl.BlockSpec((groups, cases * records), lambda k: (0, 0)),
         ],
-        out_specs=pl.BlockSpec((comps, groups, width), lambda k: (0, 0, 0)),
-        out_shape=jax.ShapeDtypeStruct((comps, groups, width), jnp.float32),
-        scratch_shapes=[pltpu.VMEM((width // 128, tile * comps, 128), jnp.float32)],
-        compiler_params=pltpu.CompilerParams(vmem_limit_bytes=48 * 1024 * 1024),
-    )(mode_shapes, modal_resp, selector)
+        out_specs=pl.BlockSpec((groups * cases, steps), lambda k: (0, 0)),
+        out_shape=jax.ShapeDtypeStruct((groups * cases, steps), jnp.float32),
+        scratch_shapes=[
+            pltpu.VMEM((width // 128, rows, 128), jnp.float32),
+            pltpu.VMEM((comps, groups, width), jnp.float32),
+        ],
+        compiler_params=pltpu.CompilerParams(vmem_limit_bytes=56 * 1024 * 1024),
+    )(case_coef, mode_shapes, modal_resp, selector, record_pick)
 
 
 def local(
@@ -91,13 +123,12 @@
 
     group_index = member_owner[:, 0] * groups_here + member_group[:, 0]
     selector = (jnp.arange(group_total)[:, None] == group_index[None, :]).astype(jnp.bfloat16)
-    group_part = group_parts(mode_shapes, modal_resp, selector, comp_count)
-    group_part = group_part.reshape(comp_count, group_total, record_count, -1)
     record_pick = (rec_all[:, :, None] == jnp.arange(record_count)[None, None, :]).astype(
         jnp.float32
     )
-    picked = jnp.sum(record_pick[None, :, :, :, None] * group_part[:, :, None, :, :], axis=3)
-    share = jnp.sum(case_coef.T[:, None, :, None] * picked, axis=0)
+    share = group_shares(
+        case_coef, mode_shapes, modal_resp, selector, record_pick.reshape(group_total, -1), comp_count
+    )
     share = share.reshape(owner_total, groups_here, case_count, share.shape[-1])
     received = lax.all_to_all(
         share.astype(jnp.bfloat16), ("mode", "member"), split_axis=0, concat_axis=0, tiled=True

time: 118 us -> 91.6 us (0.78)
  other arithmetic: 24 us -> 4.67 us
  local copies, waits for them, and re-layouts: 12.4 us -> 5.32 us
    reduce_sum x2 -> x0, other arithmetic: 22 us -> none  [the longest x1 16.5 us: local(): jnp.sum(record_pick[None, :, :, :, None] * group_part[:, :, None, :, :],...]
    mul x1 -> x0, local copies, waits for them, and re-layouts: 7.61 us -> none  [local(): record_pick[None, :, :, :, None] * group_part[:, :, None, :, :]]
    convert_element_type x0 -> x1, other arithmetic: none -> 1.69 us  [local(): share.astype(jnp.bfloat16)]
where the time goes in v5:
time: 91.6 us; the launch traced here: 91 us
  blocking collectives  63.7 us (70%)
  Pallas kernels  16.9 us (18%)
  local copies, waits for them, and re-layouts  5.32 us (6%)
  other arithmetic  4.67 us (5%)
    all_gather x1, blocking collectives, local(): gathered = lax.all_gather(payload, 'member', axis=0)  26.1 us
    all_to_all x1, blocking collectives, local(): lax.all_to_all(share.astype(jnp.bfloat16), ('mode', 'member'), split_axis...  25.5 us
    pallas_call x1, Pallas kernels, group_shares(): pl.pallas_call(functools.partial(group_kernel, comps=comps, tile=tile, re...  16.9 us
    all_gather x1, blocking collectives, local(): lax.all_gather(record_table, 'mode', axis=0, tiled=True).reshape(-1)  12.1 us

profile of v5, /device:TPU:0, one launch (start us, length us, event | category | flops | bytes accessed | tf_op | source)
XLA Modules:
  0.0 91.0 jit_solution(15742468072334031219)
XLA Ops:
  0.0 12.1 %all-gather.1 = s32[8,4,8]{2,1,0:T(4,128)S(1)} all-gather(s32[1,4,8]{2,1,0:T(4,128)} %bitcast.31), channel_id=1, replica_groups=mesh['mode'=8,'member'=16] {'mode'}, dimensions={0}, use_global_device_ids=true | all-gather | bytes 1152 | tf_op jit(solution)/shard_map/all_gather | solution.py:111
  12.1 0.1 convert_element_type.28
  12.3 1.6 %rev.3 = bf16[32,512]{1,0:T(8,128)(2,1)S(1)} reverse(bf16[32,512]{1,0:T(8,128)(2,1)} %param.11), dimensions={1} | reverse | bytes 65536 | tf_op jit(solution)/shard_map/rev | solution.py:108
  13.9 0.7 tile.4
  14.7 0.6 tile.10
  15.3 0.2 slice.31
  15.5 0.1 copy.31
  15.7 0.2 convolution_convert_fusion
  15.9 26.1 %all-gather = bf16[640,512]{1,0:T(8,128)(2,1)S(1)} all-gather(bf16[40,512]{1,0:T(8,128)(2,1)S(1)} %pad_maximum_fusion), channel_id=2, replica_groups=mesh['mode'=8,'member'=16] {'member'}, dimensions={0}, use_global_device_ids=true | all-gather | bytes 696320 | tf_op jit(solution)/shard_map/all_gather | solution.py:118
  42.0 0.0 copy-start
  42.0 0.0 copy-start.1
  42.0 0.8 slice.33
  42.9 0.1 eq.46
  43.0 0.5 copy.24
  43.5 0.1 copy.25
  43.6 0.1 copy.26
  43.8 0.1 copy.27
  43.9 0.0 copy-done
  43.9 0.0 copy-done.1
  44.0 1.3 %fusion.sel_ref = bf16[512,1024]{1,0:T(8,128)(2,1)} fusion(s32[1024]{0:T(1024)S(1)} %bitcast.30), kind=kLoop, calls=%fused_computation.2 | loop fusion | flops 1048576 | bytes 1052672 | tf_op jit(solution)/shard_map/convert_element_type | solution.py:125
  45.2 0.7 compare_convert_fusion.pick_ref
  46.0 16.9 %shard_map.82 = f32[4096,128]{1,0:T(8,128)} custom-call(f32[8,6]{1,0:T(8,128)} %coef_ref.1, bf16[6144,512]{1,0:T(8,128)(2,1)} %ms_ref.1, bf16[512,512]{1,0:T(8,128)(2,1)} %bitcast.25, bf16[512,1024]{1,0:T(8,128)(2,1)} %fusion.sel_ref, f32[512,32]{1,0:T(8,128)} %compare_convert_fusion.pick_ref), custom_call_target="tpu_custom_call" | custom-call | tf_op jit(solution)/shard_map/pallas_call | solution.py:68
  62.9 1.7 %convert_element_type.31 = bf16[4096,128]{1,0:T(8,128)(2,1)S(1)} convert(f32[4096,128]{1,0:T(8,128)} %shard_map.82) | non-fusion elementwise | flops 524288 | bytes 3145728 | tf_op jit(solution)/shard_map/convert_element_type | solution.py:134
  64.6 0.0 copy-start.2
  64.6 25.5 %all_to_all.5 = bf16[128,4,8,128]{3,2,1,0:T(8,128)(2,1)S(1)} all-to-all(bf16[128,4,8,128]{3,2,1,0:T(8,128)(2,1)S(1)} %bitcast.20), channel_id=1, replica_groups=mesh['mode'=8,'member'=16] {'mode','member'}, dimensions={0} | all-to-all | bytes 2097152 | tf_op jit(solution)/shard_map/all_to_all | solution.py:133
  90.1 0.2 convert_reduce_fusion
  90.3 0.0 copy-done.2
  90.3 0.7 abs_reduce_fusion
  (12 shorter events, 0.2 us)
Async XLA Ops:
  42.0 1.9 %copy-start = (s32[1024,1]{0,1:T(1,128)S(1)}, s32[1024,1]{0,1:T(1,128)}, u32[]{:S(2)}) copy-start(s32[1024,1]{0,1:T(1,128)} %param.14) | copy-start | bytes 12292
  42.0 1.9 %copy-start.1 = (s32[1024,1]{0,1:T(1,128)S(1)}, s32[1024,1]{0,1:T(1,128)}, u32[]{:S(2)}) copy-start(s32[1024,1]{0,1:T(1,128)} %param.13) | copy-start | bytes 12292
  64.6 25.7 %copy-start.2 = (f32[4,8]{1,0:T(4,128)S(1)}, f32[4,8]{1,0:T(4,128)}, u32[]{:S(2)}) copy-start(f32[4,8]{1,0:T(4,128)} %param.17) | copy-start | bytes 388

commit v6 on v5

--- a/solution.py
+++ b/solution.py
@@ -108,14 +108,18 @@
         modal_kernel[:, ::-1], lagged, (((1,), (1,)), ((), ())), preferred_element_type=jnp.float32
     ).astype(jnp.bfloat16)
     resp_rows, width = local_resp.shape
-    rec_col = lax.all_gather(record_table, "mode", axis=0, tiled=True).reshape(-1)
+    rec_col = lax.all_to_all(
+        jnp.broadcast_to(record_table[None], (n_mode,) + record_table.shape), "mode", 0, 0
+    ).reshape(-1)
     rec_rows = -(-rec_col.shape[0] // width)
     rec_rows = -(-rec_rows // 8) * 8
     rec_block = jnp.zeros((rec_rows * width,), jnp.bfloat16).at[: rec_col.shape[0]].set(
         rec_col.astype(jnp.bfloat16)
     )
     payload = jnp.concatenate([local_resp, rec_block.reshape(rec_rows, width)], axis=0)
-    gathered = lax.all_gather(payload, "member", axis=0)
+    gathered = lax.all_to_all(
+        jnp.broadcast_to(payload[None], (n_member,) + payload.shape), "member", 0, 0
+    )
     modal_resp = gathered[:, :resp_rows].reshape(n_member * resp_rows, width)
     rec_all = gathered[:, resp_rows:].reshape(n_member, -1)[:, : rec_col.shape[0]]
     rec_all = rec_all.astype(jnp.int32).reshape(n_member, n_mode, groups_here, case_count)

time: 91.6 us -> 79.9 us (0.87)
  blocking collectives: 63.7 us -> 24 us
  waiting for transfers between devices: 0 us -> 13.2 us
  starting transfers between devices: 0 us -> 12.4 us
  local copies, waits for them, and re-layouts: 5.32 us -> 7.48 us
    all_gather x2 -> x0, blocking collectives: 38.2 us -> none  [the longest x1 26.1 us: local(): gathered = lax.all_gather(payload, 'member', axis=0)]
    all_to_all x0 -> x2, waiting for transfers between devices: none -> 13.2 us  [the longest x1 11.5 us: local(): lax.all_to_all(jnp.broadcast_to(payload[None], (n_member,) + payload.shap...]
    all_to_all x0 -> x2, starting transfers between devices: none -> 12.4 us  [the longest x1 8.05 us: local(): lax.all_to_all(jnp.broadcast_to(payload[None], (n_member,) + payload.shap...]
    broadcast_in_dim x0 -> x2, local copies, waits for them, and re-layouts: none -> 2.17 us  [the longest x1 1.28 us: local(): jnp.broadcast_to(record_table[None], (n_mode,) + record_table.shape)]
    all_to_all x1, blocking collectives: 25.5 us -> 24 us  [local(): lax.all_to_all(share.astype(jnp.bfloat16), ('mode', 'member'), split_axis...]
  transfers between devices with their start and end apart: 0 -> 2, of which waited for: 0 -> 2; matrix products, arithmetic and copies ran while one was open for 0% -> 6% of each run, Pallas kernels for 0% -> 0%
where the time goes in v6:
time: 79.9 us; the launch traced here: 79.2 us
  blocking collectives  24 us (30%)
  Pallas kernels  16.9 us (21%)
  waiting for transfers between devices  13.2 us (17%)
  starting transfers between devices  12.4 us (16%)
  local copies, waits for them, and re-layouts  7.48 us (9%)
  other arithmetic  4.65 us (6%)
    all_to_all x1, blocking collectives, local(): lax.all_to_all(share.astype(jnp.bfloat16), ('mode', 'member'), split_axis...  24 us
    pallas_call x1, Pallas kernels, group_shares(): pl.pallas_call(functools.partial(group_kernel, comps=comps, tile=tile, re...  16.9 us
    all_to_all x1, waiting for transfers between devices, local(): lax.all_to_all(jnp.broadcast_to(payload[None], (n_member,) + payload.shap...  11.5 us
    all_to_all x1, starting transfers between devices, local(): lax.all_to_all(jnp.broadcast_to(payload[None], (n_member,) + payload.shap...  8.05 us
    all_to_all x1, starting transfers between devices, local(): lax.all_to_all(jnp.broadcast_to(record_table[None], (n_mode,) + record_ta...  4.38 us
    all_to_all x1, waiting for transfers between devices, local(): lax.all_to_all(jnp.broadcast_to(record_table[None], (n_mode,) + record_ta...  1.71 us
    convert_element_type x1, other arithmetic, local(): share.astype(jnp.bfloat16)  1.69 us
    rev x1, local copies, waits for them, and re-layouts, local(): modal_kernel[:, ::-1]  1.64 us
  transfers between devices with their start and end apart: 2, of which 2 were waited for; matrix products, arithmetic and copies ran while one was open for 6% of the time, Pallas kernels for 0%

profile of v6, /device:TPU:0, one launch (start us, length us, event | category | flops | bytes accessed | tf_op | source)
XLA Modules:
  0.0 79.2 jit_solution(166192405285823724)
XLA Ops:
  0.0 1.3 %broadcast_in_dim.4 = s32[8,4,8]{2,1,0:T(4,128)} broadcast(s32[4,8]{1,0:T(4,128)} %param.15), dimensions={1,2} | broadcast | bytes 1152 | tf_op jit(solution)/shard_map/broadcast_in_dim | solution.py:112
  1.3 4.4 %all-to-all-start = ((s32[8,4,8]{2,1,0:T(4,128)}), s32[8,4,8]{2,1,0:T(4,128)S(1)}, u32[]{:S(2)}, u32[]{:S(2)}) async-start(s32[8,4,8]{2,1,0:T(4,128)} %broadcast_in_dim.4), calls=%async_computation | async-start | bytes 32768 | tf_op jit(solution)/shard_map/all_to_all | solution.py:111
  5.7 1.6 %rev.3 = bf16[32,512]{1,0:T(8,128)(2,1)S(1)} reverse(bf16[32,512]{1,0:T(8,128)(2,1)} %param.11), dimensions={1} | reverse | bytes 65536 | tf_op jit(solution)/shard_map/rev | solution.py:108
  7.3 0.7 tile.4
  8.1 0.6 tile.10
  8.7 0.2 slice.31
  8.9 0.1 copy.27
  9.0 0.0 copy-start
  9.0 0.0 copy-start.1
  9.1 0.2 convolution_convert_fusion
  9.3 1.7 %all-to-all-done = s32[8,4,8]{2,1,0:T(4,128)S(1)} async-done(((s32[8,4,8]{2,1,0:T(4,128)}), s32[8,4,8]{2,1,0:T(4,128)S(1)}, u32[]{:S(2)}, u32[]{:S(2)}) %all-to-all-start) | async-done | bytes 1056 | tf_op jit(solution)/shard_map/all_to_all | solution.py:111
  11.0 0.1 convert_element_type.28
  11.2 0.9 %broadcast_in_dim.5 = bf16[16,40,512]{2,1,0:T(8,128)(2,1)} broadcast(bf16[40,512]{1,0:T(8,128)(2,1)S(1)} %pad_maximum_fusion), dimensions={1,2} | broadcast | bytes 696320 | tf_op jit(solution)/shard_map/broadcast_in_dim | solution.py:121
  12.1 8.0 %all-to-all-start.1 = ((bf16[16,40,512]{2,1,0:T(8,128)(2,1)}), bf16[16,40,512]{2,1,0:T(8,128)(2,1)S(1)}, u32[]{:S(2)}, u32[]{:S(2)}) async-start(bf16[16,40,512]{2,1,0:T(8,128)(2,1)} %broadcast_in_dim.5), calls=%async_computation.1 | async-start | bytes 1310720 | tf_op jit(solution)/shard_map/all_to_all | solution.py:120
  20.1 0.1 eq.46
  20.2 0.0 copy-done
  20.2 0.0 copy-done.1
  20.2 1.3 %fusion.sel_ref = bf16[512,1024]{1,0:T(8,128)(2,1)} fusion(s32[1024]{0:T(1024)S(1)} %bitcast.26), kind=kLoop, calls=%fused_computation.2 | loop fusion | flops 1048576 | bytes 1052672 | tf_op jit(solution)/shard_map/convert_element_type | solution.py:129
  21.5 11.5 %all-to-all-done.1 = bf16[16,40,512]{2,1,0:T(8,128)(2,1)S(1)} async-done(((bf16[16,40,512]{2,1,0:T(8,128)(2,1)}), bf16[16,40,512]{2,1,0:T(8,128)(2,1)S(1)}, u32[]{:S(2)}, u32[]{:S(2)}) %all-to-all-start.1) | async-done | bytes 655392 | tf_op jit(solution)/shard_map/all_to_all | solution.py:120
  33.0 0.5 copy.20
  33.6 0.1 copy.21
  33.7 0.1 copy.22
  33.9 0.1 copy.23
  34.0 0.7 compare_convert_fusion.pick_ref
  34.7 0.8 %slice.33 = bf16[16,32,512]{2,1,0:T(8,128)(2,1)} slice(bf16[16,40,512]{2,1,0:T(8,128)(2,1)S(1)} %all-to-all-done.1), slice={[0:16], [0:32], [0:512]} | slice | bytes 1048576 | tf_op jit(solution)/shard_map/slice | solution.py:123
  35.6 16.9 %shard_map.82 = f32[4096,128]{1,0:T(8,128)} custom-call(f32[8,6]{1,0:T(8,128)} %coef_ref.1, bf16[6144,512]{1,0:T(8,128)(2,1)} %ms_ref.1, bf16[512,512]{1,0:T(8,128)(2,1)} %bitcast.21, bf16[512,1024]{1,0:T(8,128)(2,1)} %fusion.sel_ref, f32[512,32]{1,0:T(8,128)} %compare_convert_fusion.pick_ref), custom_call_target="tpu_custom_call" | custom-call | tf_op jit(solution)/shard_map/pallas_call | solution.py:68
  52.5 1.7 %convert_element_type.31 = bf16[4096,128]{1,0:T(8,128)(2,1)S(1)} convert(f32[4096,128]{1,0:T(8,128)} %shard_map.82) | non-fusion elementwise | flops 524288 | bytes 3145728 | tf_op jit(solution)/shard_map/convert_element_type | solution.py:138
  54.2 0.0 copy-start.2
  54.2 24.0 %all_to_all.15 = bf16[128,4,8,128]{3,2,1,0:T(8,128)(2,1)S(1)} all-to-all(bf16[128,4,8,128]{3,2,1,0:T(8,128)(2,1)S(1)} %bitcast.18), channel_id=1, replica_groups=mesh['mode'=8,'member'=16] {'mode','member'}, dimensions={0} | all-to-all | bytes 2097152 | tf_op jit(solution)/shard_map/all_to_all | solution.py:137
  78.2 0.2 convert_reduce_fusion
  78.4 0.0 copy-done.2
  78.4 0.7 abs_reduce_fusion
  (12 shorter events, 0.2 us)
Async XLA Ops:
  1.3 9.7 %all-to-all-start = ((s32[8,4,8]{2,1,0:T(4,128)}), s32[8,4,8]{2,1,0:T(4,128)S(1)}, u32[]{:S(2)}, u32[]{:S(2)}) async-start(s32[8,4,8]{2,1,0:T(4,128)} %broadcast_in_dim.4), calls=%async_computation | async-start | bytes 32768 | tf_op jit(solution)/shard_map/all_to_all | solution.py:111
  9.0 11.2 %copy-start = (s32[1024,1]{0,1:T(1,128)S(1)}, s32[1024,1]{0,1:T(1,128)}, u32[]{:S(2)}) copy-start(s32[1024,1]{0,1:T(1,128)} %param.14) | copy-start | bytes 12292
  9.0 11.2 %copy-start.1 = (s32[1024,1]{0,1:T(1,128)S(1)}, s32[1024,1]{0,1:T(1,128)}, u32[]{:S(2)}) copy-start(s32[1024,1]{0,1:T(1,128)} %param.13) | copy-start | bytes 12292
  12.1 21.0 %all-to-all-start.1 = ((bf16[16,40,512]{2,1,0:T(8,128)(2,1)}), bf16[16,40,512]{2,1,0:T(8,128)(2,1)S(1)}, u32[]{:S(2)}, u32[]{:S(2)}) async-start(bf16[16,40,512]{2,1,0:T(8,128)(2,1)} %broadcast_in_dim.5), calls=%async_computation.1 | async-start | bytes 1310720 | tf_op jit(solution)/shard_map/all_to_all | solution.py:120
  54.2 24.2 %copy-start.2 = (f32[4,8]{1,0:T(4,128)S(1)}, f32[4,8]{1,0:T(4,128)}, u32[]{:S(2)}) copy-start(f32[4,8]{1,0:T(4,128)} %param.17) | copy-start | bytes 388

commit v7 on v6

--- a/solution.py
+++ b/solution.py
@@ -38,21 +38,33 @@
             q_scr[c] = jnp.dot(sel, comp_rows, preferred_element_type=jnp.float32)
         cases = coef_ref.shape[0]
         steps = q_scr.shape[2] // records
+        per = lanes // steps
         chunk = 64
+        lane = lax.broadcasted_iota(jnp.int32, (chunk, lanes), 1)
 
         def mix(i, carry):
             g0 = pl.multiple_of(i * chunk, chunk)
-            for s in range(cases):
-                acc = jnp.zeros((chunk, steps), jnp.float32)
-                for r in range(records):
-                    mixed = coef_ref[s, 0] * q_scr[0, pl.ds(g0, chunk), pl.ds(r * steps, steps)]
-                    for c in range(1, comps):
-                        mixed = mixed + coef_ref[s, c] * q_scr[
-                            c, pl.ds(g0, chunk), pl.ds(r * steps, steps)
-                        ]
-                    pick = pick_ref[pl.ds(g0, chunk), pl.ds(s * records + r, 1)]
-                    acc = acc + pick * mixed
-                out_ref[pl.ds(g0 * cases + s, chunk, stride=cases), :] = acc
+            for u in range(cases // per):
+                packed = None
+                for e in range(per):
+                    s = u * per + e
+                    acc = jnp.zeros((chunk, lanes), jnp.float32)
+                    for l in range(slabs):
+                        cols = pl.ds(l * lanes, lanes)
+                        mixed = coef_ref[s, 0] * q_scr[0, pl.ds(g0, chunk), cols]
+                        for c in range(1, comps):
+                            mixed = mixed + coef_ref[s, c] * q_scr[c, pl.ds(g0, chunk), cols]
+                        weight = pick_ref[pl.ds(g0, chunk), pl.ds(s * records + l * per, 1)]
+                        weight = jnp.broadcast_to(weight, (chunk, lanes))
+                        for j in range(1, per):
+                            other = pick_ref[pl.ds(g0, chunk), pl.ds(s * records + l * per + j, 1)]
+                            weight = jnp.where(lane >= j * steps, other, weight)
+                        acc = acc + weight * mixed
+                    total = acc
+                    for j in range(1, per):
+                        total = total + pltpu.roll(acc, j * steps, 1)
+                    packed = total if packed is None else jnp.where(lane >= e * steps, total, packed)
+                out_ref[pl.ds(g0 * (cases // per) + u, chunk, stride=cases // per), :] = packed
             return carry
 
         lax.fori_loop(0, groups // chunk, mix, 0)
@@ -65,6 +77,7 @@
     cases = case_coef.shape[0]
     records = record_pick.shape[1] // cases
     steps = width // records
+    per = 128 // steps
     return pl.pallas_call(
         functools.partial(group_kernel, comps=comps, tile=tile, records=records),
         grid=(members // tile,),
@@ -75,8 +88,8 @@
             pl.BlockSpec((groups, members), lambda k: (0, 0)),
             pl.BlockSpec((groups, cases * records), lambda k: (0, 0)),
         ],
-        out_specs=pl.BlockSpec((groups * cases, steps), lambda k: (0, 0)),
-        out_shape=jax.ShapeDtypeStruct((groups * cases, steps), jnp.float32),
+        out_specs=pl.BlockSpec((groups * cases // per, 128), lambda k: (0, 0)),
+        out_shape=jax.ShapeDtypeStruct((groups * cases // per, 128), jnp.float32),
         scratch_shapes=[
             pltpu.VMEM((width // 128, rows, 128), jnp.float32),
             pltpu.VMEM((comps, groups, width), jnp.float32),
@@ -103,11 +116,15 @@
     groups_here, case_count = gravity.shape
     owner_total = n_mode * n_member
     group_total = groups_here * owner_total
+    halves = 2
     lagged = lagged_table(ground_accel, tap_count)
+    lagged = lagged.reshape(record_count, halves, -1, tap_count)
+    lagged = jnp.transpose(lagged, (1, 0, 2, 3)).reshape(-1, tap_count)
     local_resp = lax.dot_general(
         modal_kernel[:, ::-1], lagged, (((1,), (1,)), ((), ())), preferred_element_type=jnp.float32
     ).astype(jnp.bfloat16)
-    resp_rows, width = local_resp.shape
+    resp_rows, resp_cols = local_resp.shape
+    width = resp_cols // halves
     rec_col = lax.all_to_all(
         jnp.broadcast_to(record_table[None], (n_mode,) + record_table.shape), "mode", 0, 0
     ).reshape(-1)
@@ -116,30 +133,36 @@
     rec_block = jnp.zeros((rec_rows * width,), jnp.bfloat16).at[: rec_col.shape[0]].set(
         rec_col.astype(jnp.bfloat16)
     )
-    payload = jnp.concatenate([local_resp, rec_block.reshape(rec_rows, width)], axis=0)
-    gathered = lax.all_to_all(
-        jnp.broadcast_to(payload[None], (n_member,) + payload.shape), "member", 0, 0
-    )
-    modal_resp = gathered[:, :resp_rows].reshape(n_member * resp_rows, width)
-    rec_all = gathered[:, resp_rows:].reshape(n_member, -1)[:, : rec_col.shape[0]]
-    rec_all = rec_all.astype(jnp.int32).reshape(n_member, n_mode, groups_here, case_count)
-    rec_all = jnp.transpose(rec_all, (1, 0, 2, 3)).reshape(group_total, case_count)
-
     group_index = member_owner[:, 0] * groups_here + member_group[:, 0]
     selector = (jnp.arange(group_total)[:, None] == group_index[None, :]).astype(jnp.bfloat16)
-    record_pick = (rec_all[:, :, None] == jnp.arange(record_count)[None, None, :]).astype(
-        jnp.float32
-    )
-    share = group_shares(
-        case_coef, mode_shapes, modal_resp, selector, record_pick.reshape(group_total, -1), comp_count
-    )
-    share = share.reshape(owner_total, groups_here, case_count, share.shape[-1])
-    received = lax.all_to_all(
-        share.astype(jnp.bfloat16), ("mode", "member"), split_axis=0, concat_axis=0, tiled=True
-    )
-    selected = jnp.sum(received.astype(jnp.float32), axis=0)
-    combined = gravity[:, :, None] + selected
-    return jnp.max(jnp.abs(combined), axis=2)
+    demand = None
+    record_pick = None
+    for h in range(halves):
+        payload = local_resp[:, h * width : (h + 1) * width]
+        if h == 0:
+            payload = jnp.concatenate([payload, rec_block.reshape(rec_rows, width)], axis=0)
+        gathered = lax.all_to_all(
+            jnp.broadcast_to(payload[None], (n_member,) + payload.shape), "member", 0, 0
+        )
+        modal_resp = gathered[:, :resp_rows].reshape(n_member * resp_rows, width)
+        if h == 0:
+            rec_all = gathered[:, resp_rows:].reshape(n_member, -1)[:, : rec_col.shape[0]]
+            rec_all = rec_all.astype(jnp.int32).reshape(n_member, n_mode, groups_here, case_count)
+            rec_all = jnp.transpose(rec_all, (1, 0, 2, 3)).reshape(group_total, case_count)
+            record_pick = (rec_all[:, :, None] == jnp.arange(record_count)[None, None, :]).astype(
+                jnp.float32
+            )
+            record_pick = record_pick.reshape(group_total, -1)
+        share = group_shares(case_coef, mode_shapes, modal_resp, selector, record_pick, comp_count)
+        share = share.reshape(owner_total, groups_here, -1, share.shape[-1])
+        received = lax.all_to_all(
+            share.astype(jnp.bfloat16), ("mode", "member"), split_axis=0, concat_axis=0, tiled=True
+        )
+        selected = jnp.sum(received.astype(jnp.float32), axis=0)
+        selected = selected.reshape(groups_here, case_count, -1)
+        peak = jnp.max(jnp.abs(gravity[:, :, None] + selected), axis=2)
+        demand = peak if demand is None else jnp.maximum(demand, peak)
+    return demand
 
 
 def solution(mesh):

time: 79.9 us -> 109 us (1.36)
  blocking collectives: 24 us -> 0 us
  starting transfers between devices: 12.4 us -> 34.1 us
  Pallas kernels: 16.9 us -> 34.4 us
  waiting for transfers between devices: 13.2 us -> 23.8 us
  other arithmetic: 4.65 us -> 7.46 us
    all_to_all x1 -> x0, blocking collectives: 24 us -> none  [local(): lax.all_to_all(share.astype(jnp.bfloat16), ('mode', 'member'), split_axis...]
    all_to_all x0 -> x2, starting transfers between devices: none -> 18.2 us  [local(): lax.all_to_all(share.astype(jnp.bfloat16), ('mode', 'member'), split_axis...]
    pallas_call x1 -> x2, Pallas kernels: 16.9 us -> 34.4 us  [group_shares(): pl.pallas_call(functools.partial(group_kernel, comps=comps, tile=tile, re...]
    all_to_all x0 -> x2, waiting for transfers between devices: none -> 13.3 us  [local(): lax.all_to_all(share.astype(jnp.bfloat16), ('mode', 'member'), split_axis...]
    all_to_all x1 -> x2, waiting for transfers between devices: 11.5 us -> 7.96 us  [local(): lax.all_to_all(jnp.broadcast_to(payload[None], (n_member,) + payload.shap...]
    all_to_all x1 -> x2, starting transfers between devices: 8.05 us -> 11.6 us  [local(): lax.all_to_all(jnp.broadcast_to(payload[None], (n_member,) + payload.shap...]
    convert_element_type x1 -> x2, other arithmetic: 1.69 us -> 4.14 us  [local(): share.astype(jnp.bfloat16)]
    rev x1, local copies, waits for them, and re-layouts: 1.64 us -> 0.33 us  [local(): modal_kernel[:, ::-1]]
  transfers between devices with their start and end apart: 2 -> 5, of which waited for: 2 -> 3; matrix products, arithmetic and copies ran while one was open for 6% -> 10% of each run, Pallas kernels for 0% -> 32%
where the time goes in v7:
time: 109 us; the launch traced here: 107 us
  Pallas kernels  34.4 us (32%)
  starting transfers between devices  34.1 us (31%)
  waiting for transfers between devices  23.8 us (22%)
  other arithmetic  7.46 us (7%)
  local copies, waits for them, and re-layouts  6.99 us (6%)
    pallas_call x2, Pallas kernels, group_shares(): pl.pallas_call(functools.partial(group_kernel, comps=comps, tile=tile, re...  34.4 us
    all_to_all x2, starting transfers between devices, local(): lax.all_to_all(share.astype(jnp.bfloat16), ('mode', 'member'), split_axis...  18.2 us
    all_to_all x2, waiting for transfers between devices, local(): lax.all_to_all(share.astype(jnp.bfloat16), ('mode', 'member'), split_axis...  13.3 us
    all_to_all x2, starting transfers between devices, local(): lax.all_to_all(jnp.broadcast_to(payload[None], (n_member,) + payload.shap...  11.6 us
    all_to_all x2, waiting for transfers between devices, local(): lax.all_to_all(jnp.broadcast_to(payload[None], (n_member,) + payload.shap...  7.96 us
    all_to_all x1, starting transfers between devices, local(): lax.all_to_all(jnp.broadcast_to(record_table[None], (n_mode,) + record_ta...  4.38 us
    convert_element_type x2, other arithmetic, local(): share.astype(jnp.bfloat16)  4.14 us
    all_to_all x1, waiting for transfers between devices, local(): lax.all_to_all(jnp.broadcast_to(record_table[None], (n_mode,) + record_ta...  2.61 us
  transfers between devices with their start and end apart: 5, of which 3 were waited for; matrix products, arithmetic and copies ran while one was open for 10% of the time, Pallas kernels for 32%

profile of v7, /device:TPU:0, one launch (start us, length us, event | category | flops | bytes accessed | tf_op | source)
XLA Modules:
  0.0 107.3 jit_solution(1330055304491774952)
XLA Ops:
  0.0 1.3 %broadcast_in_dim.6 = s32[8,4,8]{2,1,0:T(4,128)} broadcast(s32[4,8]{1,0:T(4,128)} %param.15), dimensions={1,2} | broadcast | bytes 1152 | tf_op jit(solution)/shard_map/broadcast_in_dim | solution.py:129
  1.3 4.4 %all-to-all-start = ((s32[8,4,8]{2,1,0:T(4,128)}), s32[8,4,8]{2,1,0:T(4,128)S(1)}, u32[]{:S(2)}, u32[]{:S(2)}) async-start(s32[8,4,8]{2,1,0:T(4,128)} %broadcast_in_dim.6), calls=%async_computation | async-start | bytes 32768 | tf_op jit(solution)/shard_map/all_to_all | solution.py:128
  5.7 0.7 tile.4
  6.4 0.6 tile.10
  7.0 0.0 copy-start.1
  7.1 0.2 slice.39
  7.3 0.1 copy.30
  7.4 0.0 copy-start.2
  7.4 0.0 copy-start.3
  7.5 0.3 copy-done.1
  7.8 0.3 rev.3
  8.1 0.2 convolution_convert_fusion
  8.4 2.6 %all-to-all-done = s32[8,4,8]{2,1,0:T(4,128)S(1)} async-done(((s32[8,4,8]{2,1,0:T(4,128)}), s32[8,4,8]{2,1,0:T(4,128)S(1)}, u32[]{:S(2)}, u32[]{:S(2)}) %all-to-all-start) | async-done | bytes 1056 | tf_op jit(solution)/shard_map/all_to_all | solution.py:128
  11.0 0.1 convert_element_type.37
  11.2 0.8 broadcast_in_dim.7
  11.9 8.0 %all-to-all-start.1 = ((bf16[16,40,256]{2,1,0:T(8,128)(2,1)}), bf16[16,40,256]{2,1,0:T(8,128)(2,1)S(1)}, u32[]{:S(2)}, u32[]{:S(2)}) async-start(bf16[16,40,256]{2,1,0:T(8,128)(2,1)} %broadcast_in_dim.7), calls=%async_computation.1 | async-start | bytes 655360 | tf_op jit(solution)/shard_map/all_to_all | solution.py:144
  20.0 0.0 copy-done.2
  20.0 0.0 copy-done.3
  20.0 0.1 eq.46
  20.1 1.3 %fusion.sel_ref = bf16[512,1024]{1,0:T(8,128)(2,1)} fusion(s32[1024]{0:T(1024)S(1)} %bitcast.32), kind=kLoop, calls=%fused_computation.1 | loop fusion | flops 1048576 | bytes 1052672 | tf_op jit(solution)/shard_map/convert_element_type | solution.py:137
  21.4 8.0 %all-to-all-done.1 = bf16[16,40,256]{2,1,0:T(8,128)(2,1)S(1)} async-done(((bf16[16,40,256]{2,1,0:T(8,128)(2,1)}), bf16[16,40,256]{2,1,0:T(8,128)(2,1)S(1)}, u32[]{:S(2)}, u32[]{:S(2)}) %all-to-all-start.1) | async-done | bytes 327712 | tf_op jit(solution)/shard_map/all_to_all | solution.py:144
  29.3 0.7 broadcast_in_dim.8
  30.1 3.5 %all-to-all-start.3 = ((bf16[16,32,256]{2,1,0:T(8,128)(2,1)}), bf16[16,32,256]{2,1,0:T(8,128)(2,1)S(1)}, u32[]{:S(2)}, u32[]{:S(2)}) async-start(bf16[16,32,256]{2,1,0:T(8,128)(2,1)} %broadcast_in_dim.8), calls=%async_computation.3 | async-start | bytes 524288 | tf_op jit(solution)/shard_map/all_to_all | solution.py:144
  33.6 0.3 copy.23
  33.9 0.1 copy.24
  34.1 0.1 copy.25
  34.2 0.1 copy.26
  34.4 0.7 slice.42
  35.1 0.7 compare_convert_fusion.pick_ref
  35.8 17.2 %shard_map.82 = f32[2048,128]{1,0:T(8,128)} custom-call(f32[8,6]{1,0:T(8,128)} %coef_ref.3, bf16[6144,512]{1,0:T(8,128)(2,1)} %ms_ref.3, bf16[512,256]{1,0:T(8,128)(2,1)} %bitcast.28, bf16[512,1024]{1,0:T(8,128)(2,1)} %fusion.sel_ref, f32[512,32]{1,0:T(8,128)} %compare_convert_fusion.pick_ref), custom_call_target="tpu_custom_call" | custom-call | tf_op jit(solution)/shard_map/pallas_call | solution.py:81
  53.0 2.1 %convert_element_type.40 = bf16[2048,128]{1,0:T(8,128)(2,1)} convert(f32[2048,128]{1,0:T(8,128)} %shard_map.82) | non-fusion elementwise | flops 262144 | bytes 1572864 | tf_op jit(solution)/shard_map/convert_element_type | solution.py:159
  55.1 0.0 all-to-all-done.3
  55.1 0.0 copy-start
  55.1 8.4 %all-to-all-start.2 = ((bf16[128,4,4,128]{3,2,1,0:T(4,128)(2,1)}), bf16[128,4,4,128]{3,2,1,0:T(4,128)(2,1)S(1)}, u32[]{:S(2)}, u32[]{:S(2)}) async-start(bf16[128,4,4,128]{3,2,1,0:T(4,128)(2,1)} %bitcast.9), calls=%async_computation.2 | async-start | bytes 1048576 | tf_op jit(solution)/shard_map/all_to_all | solution.py:158
  63.5 0.0 copy-done
  63.6 17.2 %shard_map.83 = f32[2048,128]{1,0:T(8,128)} custom-call(f32[8,6]{1,0:T(8,128)} %coef_ref.3, bf16[6144,512]{1,0:T(8,128)(2,1)} %ms_ref.3, bf16[512,256]{1,0:T(8,128)(2,1)} %bitcast.27, bf16[512,1024]{1,0:T(8,128)(2,1)} %fusion.sel_ref, f32[512,32]{1,0:T(8,128)} %compare_convert_fusion.pick_ref), custom_call_target="tpu_custom_call" | custom-call | tf_op jit(solution)/shard_map/pallas_call | solution.py:81
  80.8 0.0 copy-start.4
  80.8 2.1 %convert_element_type.43 = bf16[2048,128]{1,0:T(8,128)(2,1)} convert(f32[2048,128]{1,0:T(8,128)} %shard_map.83) | non-fusion elementwise | flops 262144 | bytes 1572864 | tf_op jit(solution)/shard_map/convert_element_type | solution.py:159
  82.9 0.0 all-to-all-done.2
  82.9 9.8 %all-to-all-start.4 = ((bf16[128,4,4,128]{3,2,1,0:T(4,128)(2,1)}), bf16[128,4,4,128]{3,2,1,0:T(4,128)(2,1)S(1)}, u32[]{:S(2)}, u32[]{:S(2)}) async-start(bf16[128,4,4,128]{3,2,1,0:T(4,128)(2,1)} %bitcast.11), calls=%async_computation.4 | async-start | bytes 1048576 | tf_op jit(solution)/shard_map/all_to_all | solution.py:158
  92.6 0.3 convert_reduce_fusion.1
  92.9 0.1 reshape.87
  93.0 13.2 %all-to-all-done.4 = bf16[128,4,4,128]{3,2,1,0:T(4,128)(2,1)S(1)} async-done(((bf16[128,4,4,128]{3,2,1,0:T(4,128)(2,1)}), bf16[128,4,4,128]{3,2,1,0:T(4,128)(2,1)S(1)}, u32[]{:S(2)}, u32[]{:S(2)}) %all-to-all-start.4) | async-done | bytes 524320 | tf_op jit(solution)/shard_map/all_to_all | solution.py:158
  106.2 0.3 convert_reduce_fusion
  106.5 0.1 reshape.89
  106.6 0.0 copy-done.4
  106.6 0.2 abs_reduce_fusion
  106.8 0.6 max.3
  (14 shorter events, 0.2 us)
Async XLA Ops:
  1.3 9.7 %all-to-all-start = ((s32[8,4,8]{2,1,0:T(4,128)}), s32[8,4,8]{2,1,0:T(4,128)S(1)}, u32[]{:S(2)}, u32[]{:S(2)}) async-start(s32[8,4,8]{2,1,0:T(4,128)} %broadcast_in_dim.6), calls=%async_computation | async-start | bytes 32768 | tf_op jit(solution)/shard_map/all_to_all | solution.py:128
  7.0 0.8 copy-start.1
  7.4 12.6 %copy-start.2 = (s32[1024,1]{0,1:T(1,128)S(1)}, s32[1024,1]{0,1:T(1,128)}, u32[]{:S(2)}) copy-start(s32[1024,1]{0,1:T(1,128)} %param.14) | copy-start | bytes 12292
  7.4 12.6 %copy-start.3 = (s32[1024,1]{0,1:T(1,128)S(1)}, s32[1024,1]{0,1:T(1,128)}, u32[]{:S(2)}) copy-start(s32[1024,1]{0,1:T(1,128)} %param.13) | copy-start | bytes 12292
  11.9 17.4 %all-to-all-start.1 = ((bf16[16,40,256]{2,1,0:T(8,128)(2,1)}), bf16[16,40,256]{2,1,0:T(8,128)(2,1)S(1)}, u32[]{:S(2)}, u32[]{:S(2)}) async-start(bf16[16,40,256]{2,1,0:T(8,128)(2,1)} %broadcast_in_dim.7), calls=%async_computation.1 | async-start | bytes 655360 | tf_op jit(solution)/shard_map/all_to_all | solution.py:144
  30.1 25.1 %all-to-all-start.3 = ((bf16[16,32,256]{2,1,0:T(8,128)(2,1)}), bf16[16,32,256]{2,1,0:T(8,128)(2,1)S(1)}, u32[]{:S(2)}, u32[]{:S(2)}) async-start(bf16[16,32,256]{2,1,0:T(8,128)(2,1)} %broadcast_in_dim.8), calls=%async_computation.3 | async-start | bytes 524288 | tf_op jit(solution)/shard_map/all_to_all | solution.py:144
  55.1 8.4 %copy-start = (bf16[16,32,256]{2,1,0:T(8,128)(2,1)}, bf16[16,32,256]{2,1,0:T(8,128)(2,1)S(1)}, u32[]{:S(2)}) copy-start(bf16[16,32,256]{2,1,0:T(8,128)(2,1)S(1)} %all-to-all-done.3) | copy-start | bytes 786436
  55.1 27.7 %all-to-all-start.2 = ((bf16[128,4,4,128]{3,2,1,0:T(4,128)(2,1)}), bf16[128,4,4,128]{3,2,1,0:T(4,128)(2,1)S(1)}, u32[]{:S(2)}, u32[]{:S(2)}) async-start(bf16[128,4,4,128]{3,2,1,0:T(4,128)(2,1)} %bitcast.9), calls=%async_computation.2 | async-start | bytes 1048576 | tf_op jit(solution)/shard_map/all_to_all | solution.py:158
  80.8 25.8 %copy-start.4 = (f32[4,8]{1,0:T(4,128)S(1)}, f32[4,8]{1,0:T(4,128)}, u32[]{:S(2)}) copy-start(f32[4,8]{1,0:T(4,128)} %param.17) | copy-start | bytes 388
  82.9 23.4 %all-to-all-start.4 = ((bf16[128,4,4,128]{3,2,1,0:T(4,128)(2,1)}), bf16[128,4,4,128]{3,2,1,0:T(4,128)(2,1)S(1)}, u32[]{:S(2)}, u32[]{:S(2)}) async-start(bf16[128,4,4,128]{3,2,1,0:T(4,128)(2,1)} %bitcast.11), calls=%async_computation.4 | async-start | bytes 1048576 | tf_op jit(solution)/shard_map/all_to_all | solution.py:158

commit v8 on v6

v8 whole, which is shorter than its diff:
```python
import functools

import jax
import jax.numpy as jnp
from jax import lax
from jax.experimental import pallas as pl
from jax.experimental.pallas import tpu as pltpu
from jax.sharding import PartitionSpec as P


def lagged_table(ground_accel, tap_count):
    record_count, span_len = ground_accel.shape
    step_count = span_len - tap_count + 1
    tiled = jnp.tile(ground_accel, (1, step_count + 1))[:, : step_count * (span_len + 1)]
    windows = tiled.reshape(record_count, step_count, span_len + 1)[:, :, :tap_count]
    return windows.reshape(record_count * step_count, tap_count)


def shape_sum_kernel(ms_ref, gi_ref, gs_ref, m_scr, *, comps, tile):
    k = pl.program_id(0)
    rows = tile * comps
    slabs, _, lanes = m_scr.shape
    block = ms_ref[...].astype(jnp.float32)
    for l in range(slabs):
        m_scr[l, pl.ds(pl.multiple_of(k * rows, 8), rows), :] = block[:, l * lanes : (l + 1) * lanes]

    @pl.when(k == pl.num_programs(0) - 1)
    def _():
        groups = gs_ref.shape[1]
        members = gi_ref.shape[1]
        sel = (lax.broadcasted_iota(jnp.int32, (groups, members), 0) == gi_ref[...]).astype(
            jnp.bfloat16
        )
        for c in range(comps):
            comp_rows = jnp.concatenate(
                [m_scr[l, pl.ds(c, members, stride=comps), :] for l in range(slabs)], axis=1
            ).astype(jnp.bfloat16)
            gs_ref[c] = jnp.dot(sel, comp_rows, preferred_element_type=jnp.float32).astype(
                jnp.bfloat16
            )


def shape_sums(mode_shapes, group_index, groups, comps, tile=128):
    rows, modes = mode_shapes.shape
    members = group_index.shape[1]
    return pl.pallas_call(
        functools.partial(shape_sum_kernel, comps=comps, tile=tile),
        grid=(members // tile,),
        in_specs=[
            pl.BlockSpec((tile * comps, modes), lambda k: (k, 0)),
            pl.BlockSpec((1, members), lambda k: (0, 0)),
        ],
        out_specs=pl.BlockSpec((comps, groups, modes), lambda k: (0, 0, 0)),
        out_shape=jax.ShapeDtypeStruct((comps, groups, modes), jnp.bfloat16),
        scratch_shapes=[pltpu.VMEM((modes // 128, rows, 128), jnp.float32)],
        compiler_params=pltpu.CompilerParams(vmem_limit_bytes=48 * 1024 * 1024),
    )(mode_shapes, group_index)


def mix_kernel(coef_ref, gs_ref, resp_ref, pick_ref, out_ref, q_scr, *, records):
    c = pl.program_id(0)
    comps = pl.num_programs(0)
    q_scr[c] = jnp.dot(gs_ref[0], resp_ref[...], preferred_element_type=jnp.float32)

    @pl.when(c == comps - 1)
    def _():
        groups = q_scr.shape[1]
        cases = coef_ref.shape[0]
        steps = q_scr.shape[2] // records
        chunk = 64

        def mix(i, carry):
            g0 = pl.multiple_of(i * chunk, chunk)
            for s in range(cases):
                acc = jnp.zeros((chunk, steps), jnp.float32)
                for r in range(records):
                    cols = pl.ds(r * steps, steps)
                    mixed = coef_ref[s, 0] * q_scr[0, pl.ds(g0, chunk), cols]
                    for cc in range(1, q_scr.shape[0]):
                        mixed = mixed + coef_ref[s, cc] * q_scr[cc, pl.ds(g0, chunk), cols]
                    pick = pick_ref[pl.ds(g0, chunk), pl.ds(s * records + r, 1)]
                    acc = acc + pick * mixed
                out_ref[pl.ds(g0 * cases + s, chunk, stride=cases), :] = acc
            return carry

        lax.fori_loop(0, groups // chunk, mix, 0)


def group_shares(case_coef, shape_groups, modal_resp, record_pick):
    comps, groups, modes = shape_groups.shape
    width = modal_resp.shape[1]
    cases = case_coef.shape[0]
    records = record_pick.shape[1] // cases
    steps = width // records
    return pl.pallas_call(
        functools.partial(mix_kernel, records=records),
        grid=(comps,),
        in_specs=[
            pl.BlockSpec(memory_space=pltpu.SMEM),
            pl.BlockSpec((1, groups, modes), lambda c: (c, 0, 0)),
            pl.BlockSpec((modes, width), lambda c: (0, 0)),
            pl.BlockSpec((groups, cases * records), lambda c: (0, 0)),
        ],
        out_specs=pl.BlockSpec((groups * cases, steps), lambda c: (0, 0)),
        out_shape=jax.ShapeDtypeStruct((groups * cases, steps), jnp.float32),
        scratch_shapes=[pltpu.VMEM((comps, groups, width), jnp.float32)],
        compiler_params=pltpu.CompilerParams(vmem_limit_bytes=48 * 1024 * 1024),
    )(case_coef, shape_groups, modal_resp, record_pick)


def local(
    ground_accel,
    modal_kernel,
    mode_shapes,
    member_owner,
    member_group,
    record_table,
    case_coef,
    gravity,
):
    tap_count = modal_kernel.shape[1]
    record_count = ground_accel.shape[0]
    comp_count = case_coef.shape[1]
    n_mode = lax.axis_size("mode")
    n_member = lax.axis_size("member")
    groups_here, case_count = gravity.shape
    owner_total = n_mode * n_member
    group_total = groups_here * owner_total
    group_index = member_owner[:, 0] * groups_here + member_group[:, 0]
    shape_groups = shape_sums(mode_shapes, group_index.reshape(1, -1), group_total, comp_count)
    lagged = lagged_table(ground_accel, tap_count)
    local_resp = lax.dot_general(
        modal_kernel[:, ::-1], lagged, (((1,), (1,)), ((), ())), preferred_element_type=jnp.float32
    ).astype(jnp.bfloat16)
    resp_rows, width = local_resp.shape
    rec_col = lax.all_to_all(
        jnp.broadcast_to(record_table[None], (n_mode,) + record_table.shape), "mode", 0, 0
    ).reshape(-1)
    rec_rows = -(-rec_col.shape[0] // width)
    rec_rows = -(-rec_rows // 8) * 8
    rec_block = jnp.zeros((rec_rows * width,), jnp.bfloat16).at[: rec_col.shape[0]].set(
        rec_col.astype(jnp.bfloat16)
    )
    payload = jnp.concatenate([local_resp, rec_block.reshape(rec_rows, width)], axis=0)
    gathered = lax.all_to_all(
        jnp.broadcast_to(payload[None], (n_member,) + payload.shape), "member", 0, 0
    )
    modal_resp = gathered[:, :resp_rows].reshape(n_member * resp_rows, width)
    rec_all = gathered[:, resp_rows:].reshape(n_member, -1)[:, : rec_col.shape[0]]
    rec_all = rec_all.astype(jnp.int32).reshape(n_member, n_mode, groups_here, case_count)
    rec_all = jnp.transpose(rec_all, (1, 0, 2, 3)).reshape(group_total, case_count)

    record_pick = (rec_all[:, :, None] == jnp.arange(record_count)[None, None, :]).astype(
        jnp.float32
    )
    share = group_shares(case_coef, shape_groups, modal_resp, record_pick.reshape(group_total, -1))
    share = share.reshape(owner_total, groups_here, case_count, share.shape[-1])
    received = lax.all_to_all(
        share.astype(jnp.bfloat16), ("mode", "member"), split_axis=0, concat_axis=0, tiled=True
    )
    selected = jnp.sum(received.astype(jnp.float32), axis=0)
    combined = gravity[:, :, None] + selected
    return jnp.max(jnp.abs(combined), axis=2)


def solution(mesh):
    placed = (
        P(),
        P(("mode", "member"), None),
        P("member", "mode"),
        P("member", None),
        P("member", None),
        P(("mode", "member"), None),
        P(),
        P(("mode", "member"), None),
    )
    return jax.shard_map(
        local, mesh=mesh, in_specs=placed, out_specs=P(("mode", "member"), None), check_vma=False
    )
```

time: 79.9 us -> 71 us (0.89)
  waiting for transfers between devices: 13.2 us -> 5.66 us
  other arithmetic: 4.65 us -> 1.09 us
  local copies, waits for them, and re-layouts: 7.48 us -> 10.3 us
  Pallas kernels: 16.9 us -> 16.1 us
    all_to_all x1, waiting for transfers between devices: 11.5 us -> 3.95 us  [local(): lax.all_to_all(jnp.broadcast_to(payload[None], (n_member,) + payload.shap...]
    slice x3, local copies, waits for them, and re-layouts: 0.5 us -> 3.11 us  [local(): gathered[:, resp_rows:].reshape(n_member, -1)[:, :rec_col.shape[0]]]
    convert_element_type x1, other arithmetic: 1.69 us -> 0.1 us  [local(): share.astype(jnp.bfloat16)]
    convert_element_type x1 -> x0, other arithmetic: 1.28 us -> none  [local(): (jnp.arange(group_total)[:, None] == group_index[None, :]).astype(jnp.bfl...]
    pallas_call x1 -> x2, Pallas kernels: 16.9 us -> 16.1 us  [the longest x1 8.88 us: shape_sums(): pl.pallas_call(functools.partial(shape_sum_kernel, comps=comps, tile=tile...]
  transfers between devices with their start and end apart: 2 -> 2, of which waited for: 2 -> 2; matrix products, arithmetic and copies ran while one was open for 6% -> 5% of each run, Pallas kernels for 0% -> 13%
where the time goes in v8:
time: 71 us; the launch traced here: 70.2 us
  blocking collectives  24 us (34%)
  Pallas kernels  16.1 us (23%)
  starting transfers between devices  12.5 us (18%)
  local copies, waits for them, and re-layouts  10.3 us (15%)
  waiting for transfers between devices  5.66 us (8%)
  other arithmetic  1.09 us (2%)
    all_to_all x1, blocking collectives, local(): lax.all_to_all(share.astype(jnp.bfloat16), ('mode', 'member'), split_axis...  24 us
    pallas_call x1, Pallas kernels, shape_sums(): pl.pallas_call(functools.partial(shape_sum_kernel, comps=comps, tile=tile...  8.88 us
    all_to_all x1, starting transfers between devices, local(): lax.all_to_all(jnp.broadcast_to(payload[None], (n_member,) + payload.shap...  8.09 us
    pallas_call x1, Pallas kernels, group_shares(): pl.pallas_call(functools.partial(mix_kernel, records=records), grid=(comp...  7.26 us
    all_to_all x1, starting transfers between devices, local(): lax.all_to_all(jnp.broadcast_to(record_table[None], (n_mode,) + record_ta...  4.38 us
    all_to_all x1, waiting for transfers between devices, local(): lax.all_to_all(jnp.broadcast_to(payload[None], (n_member,) + payload.shap...  3.95 us
    slice x3, local copies, waits for them, and re-layouts, local(): gathered[:, resp_rows:].reshape(n_member, -1)[:, :rec_col.shape[0]]  3.11 us
    all_to_all x1, waiting for transfers between devices, local(): lax.all_to_all(jnp.broadcast_to(record_table[None], (n_mode,) + record_ta...  1.71 us
  transfers between devices with their start and end apart: 2, of which 2 were waited for; matrix products, arithmetic and copies ran while one was open for 5% of the time, Pallas kernels for 13%

profile of v8, /device:TPU:0, one launch (start us, length us, event | category | flops | bytes accessed | tf_op | source)
XLA Modules:
  0.0 70.2 jit_solution(5262098849328491394)
XLA Ops:
  0.0 1.3 %broadcast_in_dim.4 = s32[8,4,8]{2,1,0:T(4,128)} broadcast(s32[4,8]{1,0:T(4,128)} %param.15), dimensions={1,2} | broadcast | bytes 1152 | tf_op jit(solution)/shard_map/broadcast_in_dim | solution.py:137
  1.3 4.4 %all-to-all-start = ((s32[8,4,8]{2,1,0:T(4,128)}), s32[8,4,8]{2,1,0:T(4,128)S(1)}, u32[]{:S(2)}, u32[]{:S(2)}) async-start(s32[8,4,8]{2,1,0:T(4,128)} %broadcast_in_dim.4), calls=%async_computation | async-start | bytes 32768 | tf_op jit(solution)/shard_map/all_to_all | solution.py:136
  5.7 1.6 %rev.3 = bf16[32,512]{1,0:T(8,128)(2,1)S(1)} reverse(bf16[32,512]{1,0:T(8,128)(2,1)} %param.11), dimensions={1} | reverse | bytes 65536 | tf_op jit(solution)/shard_map/rev | solution.py:133
  7.3 0.7 %tile.4 = bf16[4,129,639]{2,1,0:T(8,128)(2,1)S(1)} broadcast(bf16[4,639]{1,0:T(4,128)(2,1)} %param.10), dimensions={0,2} | broadcast | bytes 664560 | tf_op jit(solution)/shard_map/tile | solution.py:14
  8.1 0.6 tile.10
  8.7 0.0 copy-start.1
  8.7 0.0 copy-start.2
  8.7 0.2 slice.31
  8.9 0.1 copy.27
  9.1 0.2 convolution_convert_fusion
  9.3 1.7 %all-to-all-done = s32[8,4,8]{2,1,0:T(4,128)S(1)} async-done(((s32[8,4,8]{2,1,0:T(4,128)}), s32[8,4,8]{2,1,0:T(4,128)S(1)}, u32[]{:S(2)}, u32[]{:S(2)}) %all-to-all-start) | async-done | bytes 1056 | tf_op jit(solution)/shard_map/all_to_all | solution.py:136
  11.0 0.1 convert_element_type.25
  11.2 0.9 %broadcast_in_dim.5 = bf16[16,40,512]{2,1,0:T(8,128)(2,1)} broadcast(bf16[40,512]{1,0:T(8,128)(2,1)S(1)} %pad_maximum_fusion), dimensions={1,2} | broadcast | bytes 696320 | tf_op jit(solution)/shard_map/broadcast_in_dim | solution.py:146
  12.1 8.1 %all-to-all-start.1 = ((bf16[16,40,512]{2,1,0:T(8,128)(2,1)}), bf16[16,40,512]{2,1,0:T(8,128)(2,1)}, u32[]{:S(2)}, u32[]{:S(2)}) async-start(bf16[16,40,512]{2,1,0:T(8,128)(2,1)} %broadcast_in_dim.5), calls=%async_computation.1 | async-start | bytes 1310720 | tf_op jit(solution)/shard_map/all_to_all | solution.py:145
  20.2 0.1 eq.30
  20.3 0.0 copy-done.1
  20.3 0.0 copy-done.2
  20.3 8.9 %shard_map.82.gs_ref = bf16[6,512,512]{2,1,0:T(8,128)(2,1)S(1)} custom-call(bf16[6144,512]{1,0:T(8,128)(2,1)} %ms_ref.1, s32[1,1024]{1,0:T(1,128)S(1)} %add_bitcast_fusion.gi_ref), custom_call_target="tpu_custom_call" | custom-call | tf_op jit(solution)/shard_map/pallas_call | solution.py:46
  29.2 0.0 copy-start
  29.2 4.0 %all-to-all-done.1 = bf16[16,40,512]{2,1,0:T(8,128)(2,1)} async-done(((bf16[16,40,512]{2,1,0:T(8,128)(2,1)}), bf16[16,40,512]{2,1,0:T(8,128)(2,1)}, u32[]{:S(2)}, u32[]{:S(2)}) %all-to-all-start.1) | async-done | bytes 655392 | tf_op jit(solution)/shard_map/all_to_all | solution.py:145
  33.1 0.9 %slice.34 = bf16[16,8,512]{2,1,0:T(8,128)(2,1)S(1)} slice(bf16[16,40,512]{2,1,0:T(8,128)(2,1)} %all-to-all-done.1), slice={[0:16], [32:40], [0:512]} | slice | bytes 262144 | tf_op jit(solution)/shard_map/slice | solution.py:149
  34.0 1.4 %copy.20 = bf16[16,8,512]{0,2,1:T(8,128)(2,1)} copy(bf16[16,8,512]{2,1,0:T(8,128)(2,1)S(1)} %slice.34) | data formatting | bytes 262144 | tf_op jit(solution)/shard_map/slice | solution.py:149
  35.4 0.8 %slice.35 = bf16[16,256]{0,1:T(8,128)(2,1)S(1)} slice(bf16[16,4096]{0,1:T(8,128)(2,1)} %bitcast.24), slice={[0:16], [0:256]} | slice | bytes 16384 | tf_op jit(solution)/shard_map/slice | solution.py:149
  36.3 0.1 copy.21
  36.4 0.1 copy.22
  36.6 0.1 copy.23
  36.7 1.1 %slice.33 = bf16[16,32,512]{2,1,0:T(8,128)(2,1)S(1)} slice(bf16[16,40,512]{2,1,0:T(8,128)(2,1)} %all-to-all-done.1), slice={[0:16], [0:32], [0:512]} | slice | bytes 1048576 | tf_op jit(solution)/shard_map/slice | solution.py:148
  37.8 0.0 copy-done
  37.8 7.3 %shard_map.83 = f32[4096,128]{1,0:T(8,128)S(1)} custom-call(f32[8,6]{1,0:T(8,128)S(1)} %copy-done, bf16[6,512,512]{2,1,0:T(8,128)(2,1)S(1)} %shard_map.82.gs_ref, bf16[512,512]{1,0:T(8,128)(2,1)S(1)} %bitcast.19, f32[512,32]{1,0:T(8,128)S(1)} %compare_convert_fusion.pick_ref), custom_call_target="tpu_custom_call" | custom-call | tf_op jit(solution)/shard_map/pallas_call | solution.py:95
  45.1 0.0 copy-start.3
  45.1 0.1 convert_element_type.27
  45.2 24.0 %all_to_all.15 = bf16[128,4,8,128]{3,2,1,0:T(8,128)(2,1)S(1)} all-to-all(bf16[128,4,8,128]{3,2,1,0:T(8,128)(2,1)S(1)} %bitcast.20), channel_id=1, replica_groups=mesh['mode'=8,'member'=16] {'mode','member'}, dimensions={0} | all-to-all | bytes 2097152 | tf_op jit(solution)/shard_map/all_to_all | solution.py:158
  69.3 0.2 convert_reduce_fusion
  69.5 0.0 copy-done.3
  69.5 0.7 %abs_reduce_fusion = f32[4,8]{1,0:T(4,128)} fusion(f32[4,8,128]{2,1,0:T(8,128)S(1)} %convert_reduce_fusion, f32[4,8]{1,0:T(4,128)S(1)} %copy-done.3), kind=kLoop, calls=%fused_computation.6 | loop fusion | flops 12256 | bytes 16640 | tf_op jit(solution)/shard_map/reduce_max | solution.py:163
  (11 shorter events, 0.2 us)
Async XLA Ops:
  1.3 9.7 %all-to-all-start = ((s32[8,4,8]{2,1,0:T(4,128)}), s32[8,4,8]{2,1,0:T(4,128)S(1)}, u32[]{:S(2)}, u32[]{:S(2)}) async-start(s32[8,4,8]{2,1,0:T(4,128)} %broadcast_in_dim.4), calls=%async_computation | async-start | bytes 32768 | tf_op jit(solution)/shard_map/all_to_all | solution.py:136
  8.7 11.6 %copy-start.1 = (s32[1024,1]{0,1:T(1,128)S(1)}, s32[1024,1]{0,1:T(1,128)}, u32[]{:S(2)}) copy-start(s32[1024,1]{0,1:T(1,128)} %param.14) | copy-start | bytes 12292
  8.7 11.6 %copy-start.2 = (s32[1024,1]{0,1:T(1,128)S(1)}, s32[1024,1]{0,1:T(1,128)}, u32[]{:S(2)}) copy-start(s32[1024,1]{0,1:T(1,128)} %param.13) | copy-start | bytes 12292
  12.1 21.1 %all-to-all-start.1 = ((bf16[16,40,512]{2,1,0:T(8,128)(2,1)}), bf16[16,40,512]{2,1,0:T(8,128)(2,1)}, u32[]{:S(2)}, u32[]{:S(2)}) async-start(bf16[16,40,512]{2,1,0:T(8,128)(2,1)} %broadcast_in_dim.5), calls=%async_computation.1 | async-start | bytes 1310720 | tf_op jit(solution)/shard_map/all_to_all | solution.py:145
  29.2 8.7 %copy-start = (f32[8,6]{1,0:T(8,128)S(1)}, f32[8,6]{1,0:T(8,128)}, u32[]{:S(2)}) copy-start(f32[8,6]{1,0:T(8,128)} %coef_ref.1) | copy-start | bytes 580
  45.1 24.4 %copy-start.3 = (f32[4,8]{1,0:T(4,128)S(1)}, f32[4,8]{1,0:T(4,128)}, u32[]{:S(2)}) copy-start(f32[4,8]{1,0:T(4,128)} %param.17) | copy-start | bytes 388

commit v9 on v8

v9 whole, which is shorter than its diff:
```python
import functools

import jax
import jax.numpy as jnp
from jax import lax
from jax.experimental import pallas as pl
from jax.experimental.pallas import tpu as pltpu
from jax.sharding import PartitionSpec as P


def lagged_table(ground_accel, tap_count):
    record_count, span_len = ground_accel.shape
    step_count = span_len - tap_count + 1
    tiled = jnp.tile(ground_accel, (1, step_count + 1))[:, : step_count * (span_len + 1)]
    windows = tiled.reshape(record_count, step_count, span_len + 1)[:, :, :tap_count]
    return windows.reshape(record_count * step_count, tap_count)


def shape_sum_kernel(coef_ref, ms_ref, gi_ref, gs_ref, m_scr, g_scr, *, comps, tile):
    k = pl.program_id(0)
    rows = tile * comps
    slabs, _, lanes = m_scr.shape
    block = ms_ref[...].astype(jnp.float32)
    for l in range(slabs):
        m_scr[l, pl.ds(pl.multiple_of(k * rows, 8), rows), :] = block[:, l * lanes : (l + 1) * lanes]

    @pl.when(k == pl.num_programs(0) - 1)
    def _():
        groups = gs_ref.shape[1]
        members = gi_ref.shape[1]
        sel = (lax.broadcasted_iota(jnp.int32, (groups, members), 0) == gi_ref[...]).astype(
            jnp.bfloat16
        )
        for c in range(comps):
            comp_rows = jnp.concatenate(
                [m_scr[l, pl.ds(c, members, stride=comps), :] for l in range(slabs)], axis=1
            ).astype(jnp.bfloat16)
            g_scr[c] = jnp.dot(sel, comp_rows, preferred_element_type=jnp.float32)
        chunk = 64
        cases = gs_ref.shape[0]

        def mix(i, carry):
            g0 = pl.multiple_of(i * chunk, chunk)
            rows = pl.ds(g0, chunk)
            for s in range(cases):
                mixed = coef_ref[s, 0] * g_scr[0, rows, :]
                for c in range(1, comps):
                    mixed = mixed + coef_ref[s, c] * g_scr[c, rows, :]
                gs_ref[s, rows, :] = mixed.astype(jnp.bfloat16)
            return carry

        lax.fori_loop(0, groups // chunk, mix, 0)


def shape_sums(case_coef, mode_shapes, group_index, groups, tile=128):
    rows, modes = mode_shapes.shape
    cases, comps = case_coef.shape
    members = group_index.shape[1]
    return pl.pallas_call(
        functools.partial(shape_sum_kernel, comps=comps, tile=tile),
        grid=(members // tile,),
        in_specs=[
            pl.BlockSpec(memory_space=pltpu.SMEM),
            pl.BlockSpec((tile * comps, modes), lambda k: (k, 0)),
            pl.BlockSpec((1, members), lambda k: (0, 0)),
        ],
        out_specs=pl.BlockSpec((cases, groups, modes), lambda k: (0, 0, 0)),
        out_shape=jax.ShapeDtypeStruct((cases, groups, modes), jnp.bfloat16),
        scratch_shapes=[
            pltpu.VMEM((modes // 128, rows, 128), jnp.float32),
            pltpu.VMEM((comps, groups, modes), jnp.float32),
        ],
        compiler_params=pltpu.CompilerParams(vmem_limit_bytes=48 * 1024 * 1024),
    )(case_coef, mode_shapes, group_index)


def mix_kernel(gs_ref, resp_ref, pick_ref, out_ref, *, records):
    s = pl.program_id(0)
    cases = pl.num_programs(0)
    mixed = jnp.dot(gs_ref[0], resp_ref[...], preferred_element_type=jnp.float32)
    groups = mixed.shape[0]
    steps = mixed.shape[1] // records
    acc = None
    for r in range(records):
        pick = pick_ref[0, :, r : r + 1]
        term = pick * mixed[:, r * steps : (r + 1) * steps]
        acc = term if acc is None else acc + term
    out_ref[0] = acc


def group_shares(shape_groups, modal_resp, record_pick):
    cases, groups, modes = shape_groups.shape
    width = modal_resp.shape[1]
    records = record_pick.shape[2]
    steps = width // records
    return pl.pallas_call(
        functools.partial(mix_kernel, records=records),
        grid=(cases,),
        in_specs=[
            pl.BlockSpec((1, groups, modes), lambda s: (s, 0, 0)),
            pl.BlockSpec((modes, width), lambda s: (0, 0)),
            pl.BlockSpec((1, groups, records), lambda s: (s, 0, 0)),
        ],
        out_specs=pl.BlockSpec((1, groups, steps), lambda s: (s, 0, 0)),
        out_shape=jax.ShapeDtypeStruct((cases, groups, steps), jnp.float32),
        compiler_params=pltpu.CompilerParams(vmem_limit_bytes=48 * 1024 * 1024),
    )(shape_groups, modal_resp, record_pick)


def local(
    ground_accel,
    modal_kernel,
    mode_shapes,
    member_owner,
    member_group,
    record_table,
    case_coef,
    gravity,
):
    tap_count = modal_kernel.shape[1]
    record_count = ground_accel.shape[0]
    comp_count = case_coef.shape[1]
    n_mode = lax.axis_size("mode")
    n_member = lax.axis_size("member")
    groups_here, case_count = gravity.shape
    owner_total = n_mode * n_member
    group_total = groups_here * owner_total
    group_index = member_owner[:, 0] * groups_here + member_group[:, 0]
    shape_groups = shape_sums(case_coef, mode_shapes, group_index.reshape(1, -1), group_total)
    lagged = lagged_table(ground_accel, tap_count)
    local_resp = lax.dot_general(
        modal_kernel[:, ::-1], lagged, (((1,), (1,)), ((), ())), preferred_element_type=jnp.float32
    ).astype(jnp.bfloat16)
    resp_rows, width = local_resp.shape
    rec_col = lax.all_to_all(
        jnp.broadcast_to(record_table[None], (n_mode,) + record_table.shape), "mode", 0, 0
    ).reshape(-1)
    rec_rows = -(-rec_col.shape[0] // width)
    rec_rows = -(-rec_rows // 8) * 8
    rec_block = jnp.zeros((rec_rows * width,), jnp.bfloat16).at[: rec_col.shape[0]].set(
        rec_col.astype(jnp.bfloat16)
    )
    payload = jnp.concatenate([local_resp, rec_block.reshape(rec_rows, width)], axis=0)
    gathered = lax.all_to_all(
        jnp.broadcast_to(payload[None], (n_member,) + payload.shape), "member", 0, 0
    )
    modal_resp = gathered[:, :resp_rows].reshape(n_member * resp_rows, width)
    rec_all = gathered[:, resp_rows:].reshape(n_member, -1)[:, : rec_col.shape[0]]
    rec_all = rec_all.astype(jnp.int32).reshape(n_member, n_mode, groups_here, case_count)
    rec_all = jnp.transpose(rec_all, (1, 0, 2, 3)).reshape(group_total, case_count)

    record_pick = (rec_all.T[:, :, None] == jnp.arange(record_count)[None, None, :]).astype(
        jnp.float32
    )
    share = group_shares(shape_groups, modal_resp, record_pick)
    share = share.reshape(case_count, owner_total, groups_here, share.shape[-1])
    share = jnp.transpose(share.astype(jnp.bfloat16), (1, 2, 0, 3))
    received = lax.all_to_all(
        share, ("mode", "member"), split_axis=0, concat_axis=0, tiled=True
    )
    selected = jnp.sum(received.astype(jnp.float32), axis=0)
    combined = gravity[:, :, None] + selected
    return jnp.max(jnp.abs(combined), axis=2)


def solution(mesh):
    placed = (
        P(),
        P(("mode", "member"), None),
        P("member", "mode"),
        P("member", None),
        P("member", None),
        P(("mode", "member"), None),
        P(),
        P(("mode", "member"), None),
    )
    return jax.shard_map(
        local, mesh=mesh, in_specs=placed, out_specs=P(("mode", "member"), None), check_vma=False
    )
```

time: 71 us -> 73.1 us (1.030)
  blocking collectives: 24 us -> 0 us
  waiting for transfers between devices: 5.66 us -> 21.6 us
  starting transfers between devices: 12.5 us -> 20.8 us
  Pallas kernels: 16.1 us -> 18.8 us
    all_to_all x1 -> x0, blocking collectives: 24 us -> none  [local(): lax.all_to_all(share.astype(jnp.bfloat16), ('mode', 'member'), split_axis...]
    all_to_all x0 -> x1, waiting for transfers between devices: none -> 19 us  [local(): lax.all_to_all(share, ('mode', 'member'), split_axis=0, concat_axis=0, ti...]
    all_to_all x0 -> x1, starting transfers between devices: none -> 8.36 us  [local(): lax.all_to_all(share, ('mode', 'member'), split_axis=0, concat_axis=0, ti...]
    all_to_all x1, waiting for transfers between devices: 3.95 us -> 0.01 us  [local(): lax.all_to_all(jnp.broadcast_to(payload[None], (n_member,) + payload.shap...]
    pallas_call x1, Pallas kernels: 8.88 us -> 12.1 us  [shape_sums(): pl.pallas_call(functools.partial(shape_sum_kernel, comps=comps, tile=tile...]
    slice x3, local copies, waits for them, and re-layouts: 3.11 us -> 0.57 us  [local(): gathered[:, resp_rows:].reshape(n_member, -1)[:, :rec_col.shape[0]]]
    unnamed x9 -> x14, local copies, waits for them, and re-layouts: 0.1 us -> 2.47 us
    convert_element_type x0 -> x1, local copies, waits for them, and re-layouts: none -> 1.33 us  [local(): share = jnp.transpose(share.astype(jnp.bfloat16), (1, 2, 0, 3))]
  transfers between devices with their start and end apart: 2 -> 3, of which waited for: 2 -> 2; matrix products, arithmetic and copies ran while one was open for 5% -> 3% of each run, Pallas kernels for 13% -> 17%
where the time goes in v9:
time: 73.1 us; the launch traced here: 72.3 us
  waiting for transfers between devices  21.6 us (30%)
  starting transfers between devices  20.8 us (28%)
  Pallas kernels  18.8 us (26%)
  local copies, waits for them, and re-layouts  9.57 us (13%)
  other arithmetic  1.11 us (2%)
    all_to_all x1, waiting for transfers between devices, local(): lax.all_to_all(share, ('mode', 'member'), split_axis=0, concat_axis=0, ti...  19 us
    pallas_call x1, Pallas kernels, shape_sums(): pl.pallas_call(functools.partial(shape_sum_kernel, comps=comps, tile=tile...  12.1 us
    all_to_all x1, starting transfers between devices, local(): lax.all_to_all(share, ('mode', 'member'), split_axis=0, concat_axis=0, ti...  8.36 us
    all_to_all x1, starting transfers between devices, local(): lax.all_to_all(jnp.broadcast_to(payload[None], (n_member,) + payload.shap...  8.05 us
    pallas_call x1, Pallas kernels, group_shares(): pl.pallas_call(functools.partial(mix_kernel, records=records), grid=(case...  6.62 us
    all_to_all x1, starting transfers between devices, local(): lax.all_to_all(jnp.broadcast_to(record_table[None], (n_mode,) + record_ta...  4.38 us
    all_to_all x1, waiting for transfers between devices, local(): lax.all_to_all(jnp.broadcast_to(record_table[None], (n_mode,) + record_ta...  2.64 us
    unnamed x14, local copies, waits for them, and re-layouts  2.47 us
  transfers between devices with their start and end apart: 3, of which 2 were waited for; matrix products, arithmetic and copies ran while one was open for 3% of the time, Pallas kernels for 17%

profile of v9, /device:TPU:0, one launch (start us, length us, event | category | flops | bytes accessed | tf_op | source)
XLA Modules:
  0.0 72.3 jit_solution(13206816127767856195)
XLA Ops:
  0.0 1.3 %broadcast_in_dim.4 = s32[8,4,8]{2,1,0:T(4,128)} broadcast(s32[4,8]{1,0:T(4,128)} %param.15), dimensions={1,2} | broadcast | bytes 1152 | tf_op jit(solution)/shard_map/broadcast_in_dim | solution.py:136
  1.3 4.4 %all-to-all-start = ((s32[8,4,8]{2,1,0:T(4,128)}), s32[8,4,8]{2,1,0:T(4,128)S(1)}, u32[]{:S(2)}, u32[]{:S(2)}) async-start(s32[8,4,8]{2,1,0:T(4,128)} %broadcast_in_dim.4), calls=%async_computation | async-start | bytes 32768 | tf_op jit(solution)/shard_map/all_to_all | solution.py:135
  5.7 0.7 %tile.4 = bf16[4,129,639]{2,1,0:T(8,128)(2,1)S(1)} broadcast(bf16[4,639]{1,0:T(4,128)(2,1)} %param.10), dimensions={0,2} | broadcast | bytes 664560 | tf_op jit(solution)/shard_map/tile | solution.py:14
  6.4 0.6 tile.10
  7.0 0.0 copy-start.2
  7.1 0.2 slice.31
  7.3 0.1 copy.44
  7.4 0.0 copy-start.3
  7.4 0.0 copy-start.4
  7.4 0.0 copy-start.1
  7.5 0.3 copy-done.2
  7.8 0.3 rev.3
  8.1 0.2 convolution_convert_fusion
  8.4 2.6 %all-to-all-done = s32[8,4,8]{2,1,0:T(4,128)S(1)} async-done(((s32[8,4,8]{2,1,0:T(4,128)}), s32[8,4,8]{2,1,0:T(4,128)S(1)}, u32[]{:S(2)}, u32[]{:S(2)}) %all-to-all-start) | async-done | bytes 1056 | tf_op jit(solution)/shard_map/all_to_all | solution.py:135
  11.0 0.1 convert_element_type.24
  11.2 0.9 %broadcast_in_dim.5 = bf16[16,40,512]{2,1,0:T(8,128)(2,1)} broadcast(bf16[40,512]{1,0:T(8,128)(2,1)S(1)} %pad_maximum_fusion), dimensions={1,2} | broadcast | bytes 696320 | tf_op jit(solution)/shard_map/broadcast_in_dim | solution.py:145
  12.1 8.0 %all-to-all-start.1 = ((bf16[16,40,512]{2,1,0:T(8,128)(2,1)}), bf16[16,40,512]{2,1,0:T(8,128)(2,1)S(1)}, u32[]{:S(2)}, u32[]{:S(2)}) async-start(bf16[16,40,512]{2,1,0:T(8,128)(2,1)} %broadcast_in_dim.5), calls=%async_computation.1 | async-start | bytes 1310720 | tf_op jit(solution)/shard_map/all_to_all | solution.py:144
  20.1 0.0 copy-done.3
  20.1 0.0 copy-done.4
  20.2 0.0 copy-done.1
  20.2 12.1 %shard_map.82.gs_ref = bf16[8,512,512]{2,1,0:T(8,128)(2,1)S(1)} custom-call(f32[8,6]{1,0:T(8,128)S(1)} %copy-done.1, bf16[6144,512]{1,0:T(8,128)(2,1)} %ms_ref.1, s32[1,1024]{1,0:T(1,128)S(1)} %add_bitcast_fusion.gi_ref), custom_call_target="tpu_custom_call" | custom-call | tf_op jit(solution)/shard_map/pallas_call | solution.py:59
  32.3 0.0 copy-start
  32.3 1.9 %copy-done = bf16[8,512,512]{2,1,0:T(8,128)(2,1)} copy-done((bf16[8,512,512]{2,1,0:T(8,128)(2,1)}, bf16[8,512,512]{2,1,0:T(8,128)(2,1)S(1)}, u32[]{:S(2)}) %copy-start) | copy-done | bytes 4194328
  34.3 0.0 all-to-all-done.1
  34.3 0.6 copy.26
  34.9 0.1 copy.27
  35.0 0.1 copy.28
  35.1 0.6 fusion.pick_ref
  35.8 6.6 %shard_map.83 = f32[8,512,128]{2,1,0:T(8,128)S(1)} custom-call(bf16[8,512,512]{2,1,0:T(8,128)(2,1)} %copy-done, bf16[512,512]{1,0:T(8,128)(2,1)S(1)} %bitcast.22, f32[8,512,4]{2,1,0:T(8,128)S(1)} %fusion.pick_ref), custom_call_target="tpu_custom_call" | custom-call | tf_op jit(solution)/shard_map/pallas_call | solution.py:96
  42.4 0.2 convert_element_type.26
  42.6 0.0 copy-start.5
  42.6 1.3 %copy.43 = bf16[8,128,4,128]{3,2,0,1:T(4,128)(2,1)} copy(bf16[8,128,4,128]{3,2,1,0:T(4,128)(2,1)S(1)} %bitcast.23) | data formatting | bytes 2097152 | tf_op jit(solution)/shard_map/convert_element_type | solution.py:157
  43.9 8.4 %all-to-all-start.2 = ((bf16[128,4,8,128]{3,1,2,0:T(4,128)(2,1)}), bf16[128,4,8,128]{3,1,2,0:T(4,128)(2,1)S(1)}, u32[]{:S(2)}, u32[]{:S(2)}) async-start(bf16[128,4,8,128]{3,1,2,0:T(4,128)(2,1)} %bitcast.20), calls=%async_computation.2 | async-start | bytes 2097152 | tf_op jit(solution)/shard_map/all_to_all | solution.py:158
  52.3 0.0 copy-done.5
  52.3 0.1 copy.25
  52.4 19.0 %all-to-all-done.2 = bf16[128,4,8,128]{3,1,2,0:T(4,128)(2,1)S(1)} async-done(((bf16[128,4,8,128]{3,1,2,0:T(4,128)(2,1)}), bf16[128,4,8,128]{3,1,2,0:T(4,128)(2,1)S(1)}, u32[]{:S(2)}, u32[]{:S(2)}) %all-to-all-start.2) | async-done | bytes 1048608 | tf_op jit(solution)/shard_map/all_to_all | solution.py:158
  71.4 0.1 convert_reduce_fusion
  71.5 0.2 fusion.2
  71.7 0.7 copy.32
  (10 shorter events, 0.2 us)
Async XLA Ops:
  1.3 9.7 %all-to-all-start = ((s32[8,4,8]{2,1,0:T(4,128)}), s32[8,4,8]{2,1,0:T(4,128)S(1)}, u32[]{:S(2)}, u32[]{:S(2)}) async-start(s32[8,4,8]{2,1,0:T(4,128)} %broadcast_in_dim.4), calls=%async_computation | async-start | bytes 32768 | tf_op jit(solution)/shard_map/all_to_all | solution.py:135
  7.0 0.8 %copy-start.2 = (bf16[32,512]{1,0:T(8,128)(2,1)S(1)}, bf16[32,512]{1,0:T(8,128)(2,1)}, u32[]{:S(2)}) copy-start(bf16[32,512]{1,0:T(8,128)(2,1)} %param.11) | copy-start | bytes 98308
  7.4 12.8 %copy-start.3 = (s32[1024,1]{0,1:T(1,128)S(1)}, s32[1024,1]{0,1:T(1,128)}, u32[]{:S(2)}) copy-start(s32[1024,1]{0,1:T(1,128)} %param.14) | copy-start | bytes 12292
  7.4 12.8 %copy-start.4 = (s32[1024,1]{0,1:T(1,128)S(1)}, s32[1024,1]{0,1:T(1,128)}, u32[]{:S(2)}) copy-start(s32[1024,1]{0,1:T(1,128)} %param.13) | copy-start | bytes 12292
  7.4 12.8 %copy-start.1 = (f32[8,6]{1,0:T(8,128)S(1)}, f32[8,6]{1,0:T(8,128)}, u32[]{:S(2)}) copy-start(f32[8,6]{1,0:T(8,128)} %coef_ref.1) | copy-start | bytes 580
  12.1 22.2 %all-to-all-start.1 = ((bf16[16,40,512]{2,1,0:T(8,128)(2,1)}), bf16[16,40,512]{2,1,0:T(8,128)(2,1)S(1)}, u32[]{:S(2)}, u32[]{:S(2)}) async-start(bf16[16,40,512]{2,1,0:T(8,128)(2,1)} %broadcast_in_dim.5), calls=%async_computation.1 | async-start | bytes 1310720 | tf_op jit(solution)/shard_map/all_to_all | solution.py:144
  32.3 1.9 %copy-start = (bf16[8,512,512]{2,1,0:T(8,128)(2,1)}, bf16[8,512,512]{2,1,0:T(8,128)(2,1)S(1)}, u32[]{:S(2)}) copy-start(bf16[8,512,512]{2,1,0:T(8,128)(2,1)S(1)} %shard_map.82.gs_ref) | copy-start | bytes 12582916
  42.6 9.7 %copy-start.5 = (f32[4,8]{1,0:T(4,128)S(1)}, f32[4,8]{1,0:T(4,128)}, u32[]{:S(2)}) copy-start(f32[4,8]{1,0:T(4,128)} %param.17) | copy-start | bytes 388
  43.9 27.4 %all-to-all-start.2 = ((bf16[128,4,8,128]{3,1,2,0:T(4,128)(2,1)}), bf16[128,4,8,128]{3,1,2,0:T(4,128)(2,1)S(1)}, u32[]{:S(2)}, u32[]{:S(2)}) async-start(bf16[128,4,8,128]{3,1,2,0:T(4,128)(2,1)} %bitcast.20), calls=%async_computation.2 | async-start | bytes 2097152 | tf_op jit(solution)/shard_map/all_to_all | solution.py:158

commit v10 on v8

--- a/solution.py
+++ b/solution.py
@@ -57,38 +57,48 @@
     )(mode_shapes, group_index)
 
 
-def mix_kernel(coef_ref, gs_ref, resp_ref, pick_ref, out_ref, q_scr, *, records):
+def mix_kernel(coef_ref, gs_ref, g_ref, pick_ref, out_ref, q_scr, r_scr, *, records):
     c = pl.program_id(0)
     comps = pl.num_programs(0)
-    q_scr[c] = jnp.dot(gs_ref[0], resp_ref[...], preferred_element_type=jnp.float32)
+    senders, _, width = g_ref.shape
+    resp_rows = r_scr.shape[0] // senders
+
+    @pl.when(c == 0)
+    def _():
+        for j in range(senders):
+            r_scr[pl.ds(j * resp_rows, resp_rows), :] = g_ref[j, pl.ds(0, resp_rows), :]
+
+    q_scr[c] = jnp.dot(gs_ref[0], r_scr[...], preferred_element_type=jnp.float32)
 
     @pl.when(c == comps - 1)
     def _():
         groups = q_scr.shape[1]
         cases = coef_ref.shape[0]
         steps = q_scr.shape[2] // records
-        chunk = 64
+        chunk = 32
 
         def mix(i, carry):
             g0 = pl.multiple_of(i * chunk, chunk)
+            rows = pl.ds(g0, chunk)
+            accs = [jnp.zeros((chunk, steps), jnp.float32) for _ in range(cases)]
+            for r in range(records):
+                cols = pl.ds(r * steps, steps)
+                slabs = [q_scr[cc, rows, cols] for cc in range(q_scr.shape[0])]
+                for s in range(cases):
+                    mixed = coef_ref[s, 0] * slabs[0]
+                    for cc in range(1, len(slabs)):
+                        mixed = mixed + coef_ref[s, cc] * slabs[cc]
+                    accs[s] = accs[s] + pick_ref[rows, pl.ds(s * records + r, 1)] * mixed
             for s in range(cases):
-                acc = jnp.zeros((chunk, steps), jnp.float32)
-                for r in range(records):
-                    cols = pl.ds(r * steps, steps)
-                    mixed = coef_ref[s, 0] * q_scr[0, pl.ds(g0, chunk), cols]
-                    for cc in range(1, q_scr.shape[0]):
-                        mixed = mixed + coef_ref[s, cc] * q_scr[cc, pl.ds(g0, chunk), cols]
-                    pick = pick_ref[pl.ds(g0, chunk), pl.ds(s * records + r, 1)]
-                    acc = acc + pick * mixed
-                out_ref[pl.ds(g0 * cases + s, chunk, stride=cases), :] = acc
+                out_ref[pl.ds(g0 * cases + s, chunk, stride=cases), :] = accs[s]
             return carry
 
         lax.fori_loop(0, groups // chunk, mix, 0)
 
 
-def group_shares(case_coef, shape_groups, modal_resp, record_pick):
+def group_shares(case_coef, shape_groups, gathered, resp_rows, record_pick):
     comps, groups, modes = shape_groups.shape
-    width = modal_resp.shape[1]
+    width = gathered.shape[2]
     cases = case_coef.shape[0]
     records = record_pick.shape[1] // cases
     steps = width // records
@@ -98,14 +108,17 @@
         in_specs=[
             pl.BlockSpec(memory_space=pltpu.SMEM),
             pl.BlockSpec((1, groups, modes), lambda c: (c, 0, 0)),
-            pl.BlockSpec((modes, width), lambda c: (0, 0)),
+            pl.BlockSpec(gathered.shape, lambda c: (0, 0, 0)),
             pl.BlockSpec((groups, cases * records), lambda c: (0, 0)),
         ],
         out_specs=pl.BlockSpec((groups * cases, steps), lambda c: (0, 0)),
         out_shape=jax.ShapeDtypeStruct((groups * cases, steps), jnp.float32),
-        scratch_shapes=[pltpu.VMEM((comps, groups, width), jnp.float32)],
+        scratch_shapes=[
+            pltpu.VMEM((comps, groups, width), jnp.float32),
+            pltpu.VMEM((modes, width), gathered.dtype),
+        ],
         compiler_params=pltpu.CompilerParams(vmem_limit_bytes=48 * 1024 * 1024),
-    )(case_coef, shape_groups, modal_resp, record_pick)
+    )(case_coef, shape_groups, gathered, record_pick)
 
 
 def local(
@@ -145,7 +158,6 @@
     gathered = lax.all_to_all(
         jnp.broadcast_to(payload[None], (n_member,) + payload.shape), "member", 0, 0
     )
-    modal_resp = gathered[:, :resp_rows].reshape(n_member * resp_rows, width)
     rec_all = gathered[:, resp_rows:].reshape(n_member, -1)[:, : rec_col.shape[0]]
     rec_all = rec_all.astype(jnp.int32).reshape(n_member, n_mode, groups_here, case_count)
     rec_all = jnp.transpose(rec_all, (1, 0, 2, 3)).reshape(group_total, case_count)
@@ -153,7 +165,9 @@
     record_pick = (rec_all[:, :, None] == jnp.arange(record_count)[None, None, :]).astype(
         jnp.float32
     )
-    share = group_shares(case_coef, shape_groups, modal_resp, record_pick.reshape(group_total, -1))
+    share = group_shares(
+        case_coef, shape_groups, gathered, resp_rows, record_pick.reshape(group_total, -1)
+    )
     share = share.reshape(owner_total, groups_here, case_count, share.shape[-1])
     received = lax.all_to_all(
         share.astype(jnp.bfloat16), ("mode", "member"), split_axis=0, concat_axis=0, tiled=True

time: 71 us -> 70.8 us (level)
  local copies, waits for them, and re-layouts: 10.3 us -> 9.25 us
  Pallas kernels: 16.1 us -> 17 us
    slice x3 -> x2, local copies, waits for them, and re-layouts: 3.11 us -> 1.76 us  [local(): gathered[:, resp_rows:].reshape(n_member, -1)[:, :rec_col.shape[0]]]
    reshape x0 -> x1, local copies, waits for them, and re-layouts: none -> 1.35 us  [local(): gathered[:, resp_rows:].reshape(n_member, -1)[:, :rec_col.shape[0]]]
    slice x1 -> x0, local copies, waits for them, and re-layouts: 1.09 us -> none  [local(): modal_resp = gathered[:, :resp_rows].reshape(n_member * resp_rows, width)]
    pallas_call x1, Pallas kernels: 7.26 us -> 8.17 us  [group_shares(): pl.pallas_call(functools.partial(mix_kernel, records=records), grid=(comp...]
where the time goes in v10:
time: 70.8 us; the launch traced here: 70 us
  blocking collectives  24 us (34%)
  Pallas kernels  17 us (24%)
  starting transfers between devices  12.5 us (18%)
  local copies, waits for them, and re-layouts  9.25 us (13%)
  waiting for transfers between devices  5.66 us (8%)
  other arithmetic  1.09 us (2%)
    all_to_all x1, blocking collectives, local(): lax.all_to_all(share.astype(jnp.bfloat16), ('mode', 'member'), split_axis...  24 us
    pallas_call x1, Pallas kernels, shape_sums(): pl.pallas_call(functools.partial(shape_sum_kernel, comps=comps, tile=tile...  8.88 us
    pallas_call x1, Pallas kernels, group_shares(): pl.pallas_call(functools.partial(mix_kernel, records=records), grid=(comp...  8.17 us
    all_to_all x1, starting transfers between devices, local(): lax.all_to_all(jnp.broadcast_to(payload[None], (n_member,) + payload.shap...  8.09 us
    all_to_all x1, starting transfers between devices, local(): lax.all_to_all(jnp.broadcast_to(record_table[None], (n_mode,) + record_ta...  4.38 us
    all_to_all x1, waiting for transfers between devices, local(): lax.all_to_all(jnp.broadcast_to(payload[None], (n_member,) + payload.shap...  3.95 us
    slice x2, local copies, waits for them, and re-layouts, local(): gathered[:, resp_rows:].reshape(n_member, -1)[:, :rec_col.shape[0]]  1.76 us
    all_to_all x1, waiting for transfers between devices, local(): lax.all_to_all(jnp.broadcast_to(record_table[None], (n_mode,) + record_ta...  1.71 us
  transfers between devices with their start and end apart: 2, of which 2 were waited for; matrix products, arithmetic and copies ran while one was open for 5% of the time, Pallas kernels for 13%

profile of v10, /device:TPU:0, one launch (start us, length us, event | category | flops | bytes accessed | tf_op | source)
XLA Modules:
  0.0 70.0 jit_solution(16056128745221569559)
XLA Ops:
  0.0 1.3 %broadcast_in_dim.4 = s32[8,4,8]{2,1,0:T(4,128)} broadcast(s32[4,8]{1,0:T(4,128)} %param.15), dimensions={1,2} | broadcast | bytes 1152 | tf_op jit(solution)/shard_map/broadcast_in_dim | solution.py:150
  1.3 4.4 %all-to-all-start = ((s32[8,4,8]{2,1,0:T(4,128)}), s32[8,4,8]{2,1,0:T(4,128)S(1)}, u32[]{:S(2)}, u32[]{:S(2)}) async-start(s32[8,4,8]{2,1,0:T(4,128)} %broadcast_in_dim.4), calls=%async_computation | async-start | bytes 32768 | tf_op jit(solution)/shard_map/all_to_all | solution.py:149
  5.7 1.6 %rev.3 = bf16[32,512]{1,0:T(8,128)(2,1)S(1)} reverse(bf16[32,512]{1,0:T(8,128)(2,1)} %param.11), dimensions={1} | reverse | bytes 65536 | tf_op jit(solution)/shard_map/rev | solution.py:146
  7.3 0.7 %tile.4 = bf16[4,129,639]{2,1,0:T(8,128)(2,1)S(1)} broadcast(bf16[4,639]{1,0:T(4,128)(2,1)} %param.10), dimensions={0,2} | broadcast | bytes 664560 | tf_op jit(solution)/shard_map/tile | solution.py:14
  8.1 0.6 tile.10
  8.7 0.0 copy-start.1
  8.7 0.0 copy-start.2
  8.7 0.2 slice.27
  8.9 0.1 copy.28
  9.1 0.2 convolution_convert_fusion
  9.3 1.7 %all-to-all-done = s32[8,4,8]{2,1,0:T(4,128)S(1)} async-done(((s32[8,4,8]{2,1,0:T(4,128)}), s32[8,4,8]{2,1,0:T(4,128)S(1)}, u32[]{:S(2)}, u32[]{:S(2)}) %all-to-all-start) | async-done | bytes 1056 | tf_op jit(solution)/shard_map/all_to_all | solution.py:149
  11.0 0.1 convert_element_type.25
  11.2 0.9 %broadcast_in_dim.5 = bf16[16,40,512]{2,1,0:T(8,128)(2,1)} broadcast(bf16[40,512]{1,0:T(8,128)(2,1)S(1)} %pad_maximum_fusion), dimensions={1,2} | broadcast | bytes 696320 | tf_op jit(solution)/shard_map/broadcast_in_dim | solution.py:159
  12.1 8.1 %all-to-all-start.1 = ((bf16[16,40,512]{2,1,0:T(8,128)(2,1)}), bf16[16,40,512]{2,1,0:T(8,128)(2,1)}, u32[]{:S(2)}, u32[]{:S(2)}) async-start(bf16[16,40,512]{2,1,0:T(8,128)(2,1)} %broadcast_in_dim.5), calls=%async_computation.1 | async-start | bytes 1310720 | tf_op jit(solution)/shard_map/all_to_all | solution.py:158
  20.2 0.1 eq.30
  20.3 0.0 copy-done.1
  20.3 0.0 copy-done.2
  20.3 8.9 %shard_map.82.gs_ref = bf16[6,512,512]{2,1,0:T(8,128)(2,1)S(1)} custom-call(bf16[6144,512]{1,0:T(8,128)(2,1)} %ms_ref.1, s32[1,1024]{1,0:T(1,128)S(1)} %add_bitcast_fusion.gi_ref), custom_call_target="tpu_custom_call" | custom-call | tf_op jit(solution)/shard_map/pallas_call | solution.py:46
  29.2 0.0 copy-start
  29.2 4.0 %all-to-all-done.1.g_ref = bf16[16,40,512]{2,1,0:T(8,128)(2,1)} async-done(((bf16[16,40,512]{2,1,0:T(8,128)(2,1)}), bf16[16,40,512]{2,1,0:T(8,128)(2,1)}, u32[]{:S(2)}, u32[]{:S(2)}) %all-to-all-start.1) | async-done | bytes 655392 | tf_op jit(solution)/shard_map/all_to_all | solution.py:158
  33.1 0.9 %slice.29 = bf16[16,8,512]{2,1,0:T(8,128)(2,1)S(1)} slice(bf16[16,40,512]{2,1,0:T(8,128)(2,1)} %all-to-all-done.1.g_ref), slice={[0:16], [32:40], [0:512]} | slice | bytes 262144 | tf_op jit(solution)/shard_map/slice | solution.py:161
  34.0 1.4 %copy.25 = bf16[16,8,512]{0,2,1:T(8,128)(2,1)} copy(bf16[16,8,512]{2,1,0:T(8,128)(2,1)S(1)} %slice.29) | data formatting | bytes 262144 | tf_op jit(solution)/shard_map/reshape | solution.py:161
  35.4 0.8 %slice.30 = bf16[16,256]{0,1:T(8,128)(2,1)S(1)} slice(bf16[16,4096]{0,1:T(8,128)(2,1)} %bitcast.22), slice={[0:16], [0:256]} | slice | bytes 16384 | tf_op jit(solution)/shard_map/slice | solution.py:161
  36.3 0.1 copy.21
  36.4 0.1 copy.22
  36.6 0.1 copy.23
  36.7 0.0 copy-done
  36.7 8.2 %shard_map.83 = f32[4096,128]{1,0:T(8,128)S(1)} custom-call(f32[8,6]{1,0:T(8,128)S(1)} %copy-done, bf16[6,512,512]{2,1,0:T(8,128)(2,1)S(1)} %shard_map.82.gs_ref, bf16[16,40,512]{2,1,0:T(8,128)(2,1)} %all-to-all-done.1.g_ref, f32[512,32]{1,0:T(8,128)S(1)} %compare_convert_fusion.pick_ref), custom_call_target="tpu_custom_call" | custom-call | tf_op jit(solution)/shard_map/pallas_call | solution.py:105
  44.9 0.0 copy-start.3
  44.9 0.1 convert_element_type.27
  45.0 24.0 %all_to_all.15 = bf16[128,4,8,128]{3,2,1,0:T(8,128)(2,1)S(1)} all-to-all(bf16[128,4,8,128]{3,2,1,0:T(8,128)(2,1)S(1)} %bitcast.18), channel_id=1, replica_groups=mesh['mode'=8,'member'=16] {'mode','member'}, dimensions={0} | all-to-all | bytes 2097152 | tf_op jit(solution)/shard_map/all_to_all | solution.py:172
  69.1 0.2 convert_reduce_fusion
  69.3 0.0 copy-done.3
  69.3 0.7 %abs_reduce_fusion = f32[4,8]{1,0:T(4,128)} fusion(f32[4,8,128]{2,1,0:T(8,128)S(1)} %convert_reduce_fusion, f32[4,8]{1,0:T(4,128)S(1)} %copy-done.3), kind=kLoop, calls=%fused_computation.6 | loop fusion | flops 12256 | bytes 16640 | tf_op jit(solution)/shard_map/reduce_max | solution.py:177
  (11 shorter events, 0.2 us)
Async XLA Ops:
  1.3 9.7 %all-to-all-start = ((s32[8,4,8]{2,1,0:T(4,128)}), s32[8,4,8]{2,1,0:T(4,128)S(1)}, u32[]{:S(2)}, u32[]{:S(2)}) async-start(s32[8,4,8]{2,1,0:T(4,128)} %broadcast_in_dim.4), calls=%async_computation | async-start | bytes 32768 | tf_op jit(solution)/shard_map/all_to_all | solution.py:149
  8.7 11.6 %copy-start.1 = (s32[1024,1]{0,1:T(1,128)S(1)}, s32[1024,1]{0,1:T(1,128)}, u32[]{:S(2)}) copy-start(s32[1024,1]{0,1:T(1,128)} %param.14) | copy-start | bytes 12292
  8.7 11.6 %copy-start.2 = (s32[1024,1]{0,1:T(1,128)S(1)}, s32[1024,1]{0,1:T(1,128)}, u32[]{:S(2)}) copy-start(s32[1024,1]{0,1:T(1,128)} %param.13) | copy-start | bytes 12292
  12.1 21.1 %all-to-all-start.1 = ((bf16[16,40,512]{2,1,0:T(8,128)(2,1)}), bf16[16,40,512]{2,1,0:T(8,128)(2,1)}, u32[]{:S(2)}, u32[]{:S(2)}) async-start(bf16[16,40,512]{2,1,0:T(8,128)(2,1)} %broadcast_in_dim.5), calls=%async_computation.1 | async-start | bytes 1310720 | tf_op jit(solution)/shard_map/all_to_all | solution.py:158
  29.2 7.6 %copy-start = (f32[8,6]{1,0:T(8,128)S(1)}, f32[8,6]{1,0:T(8,128)}, u32[]{:S(2)}) copy-start(f32[8,6]{1,0:T(8,128)} %coef_ref.1) | copy-start | bytes 580
  44.9 24.3 %copy-start.3 = (f32[4,8]{1,0:T(4,128)S(1)}, f32[4,8]{1,0:T(4,128)}, u32[]{:S(2)}) copy-start(f32[4,8]{1,0:T(4,128)} %param.17) | copy-start | bytes 388

commit v11 on v10

--- a/solution.py
+++ b/solution.py
@@ -68,32 +68,34 @@
         for j in range(senders):
             r_scr[pl.ds(j * resp_rows, resp_rows), :] = g_ref[j, pl.ds(0, resp_rows), :]
 
-    q_scr[c] = jnp.dot(gs_ref[0], r_scr[...], preferred_element_type=jnp.float32)
+    q_scr[...] = jnp.dot(gs_ref[0], r_scr[...], preferred_element_type=jnp.float32)
+    groups = q_scr.shape[0]
+    cases = coef_ref.shape[0]
+    steps = q_scr.shape[1] // records
+    chunk = 32
 
-    @pl.when(c == comps - 1)
-    def _():
-        groups = q_scr.shape[1]
-        cases = coef_ref.shape[0]
-        steps = q_scr.shape[2] // records
-        chunk = 32
+    def mix(i, carry):
+        g0 = pl.multiple_of(i * chunk, chunk)
+        rows = pl.ds(g0, chunk)
+        for s in range(cases):
+            picked = None
+            for r in range(records):
+                term = pick_ref[rows, pl.ds(s * records + r, 1)] * q_scr[rows, pl.ds(r * steps, steps)]
+                picked = term if picked is None else picked + term
+            dst = pl.ds(g0 * cases + s, chunk, stride=cases)
+            term = coef_ref[s, c] * picked
 
-        def mix(i, carry):
-            g0 = pl.multiple_of(i * chunk, chunk)
-            rows = pl.ds(g0, chunk)
-            accs = [jnp.zeros((chunk, steps), jnp.float32) for _ in range(cases)]
-            for r in range(records):
-                cols = pl.ds(r * steps, steps)
-                slabs = [q_scr[cc, rows, cols] for cc in range(q_scr.shape[0])]
-                for s in range(cases):
-                    mixed = coef_ref[s, 0] * slabs[0]
-                    for cc in range(1, len(slabs)):
-                        mixed = mixed + coef_ref[s, cc] * slabs[cc]
-                    accs[s] = accs[s] + pick_ref[rows, pl.ds(s * records + r, 1)] * mixed
-            for s in range(cases):
-                out_ref[pl.ds(g0 * cases + s, chunk, stride=cases), :] = accs[s]
-            return carry
+            @pl.when(c == 0)
+            def _():
+                out_ref[dst, :] = term
 
-        lax.fori_loop(0, groups // chunk, mix, 0)
+            @pl.when(c > 0)
+            def _():
+                out_ref[dst, :] = out_ref[dst, :] + term
+
+        return carry
+
+    lax.fori_loop(0, groups // chunk, mix, 0)
 
 
 def group_shares(case_coef, shape_groups, gathered, resp_rows, record_pick):
@@ -114,7 +116,7 @@
         out_specs=pl.BlockSpec((groups * cases, steps), lambda c: (0, 0)),
         out_shape=jax.ShapeDtypeStruct((groups * cases, steps), jnp.float32),
         scratch_shapes=[
-            pltpu.VMEM((comps, groups, width), jnp.float32),
+            pltpu.VMEM((groups, width), jnp.float32),
             pltpu.VMEM((modes, width), gathered.dtype),
         ],
         compiler_params=pltpu.CompilerParams(vmem_limit_bytes=48 * 1024 * 1024),

time: 70.8 us -> 140 us (1.98)
  Pallas kernels: 17 us -> 86.3 us
    pallas_call x1, Pallas kernels: 8.17 us -> 77.4 us  [group_shares(): pl.pallas_call(functools.partial(mix_kernel, records=records), grid=(comp...]
  transfers between devices with their start and end apart: 2 -> 2, of which waited for: 2 -> 2; matrix products, arithmetic and copies ran while one was open for 5% -> 3% of each run, Pallas kernels for 13% -> 6%
where the time goes in v11:
time: 140 us; the launch traced here: 139 us
  Pallas kernels  86.3 us (62%)
  blocking collectives  24 us (17%)
  starting transfers between devices  12.5 us (9%)
  local copies, waits for them, and re-layouts  9.25 us (7%)
  waiting for transfers between devices  5.66 us (4%)
    pallas_call x1, Pallas kernels, group_shares(): pl.pallas_call(functools.partial(mix_kernel, records=records), grid=(comp...  77.4 us
    all_to_all x1, blocking collectives, local(): lax.all_to_all(share.astype(jnp.bfloat16), ('mode', 'member'), split_axis...  24 us
    pallas_call x1, Pallas kernels, shape_sums(): pl.pallas_call(functools.partial(shape_sum_kernel, comps=comps, tile=tile...  8.88 us
    all_to_all x1, starting transfers between devices, local(): lax.all_to_all(jnp.broadcast_to(payload[None], (n_member,) + payload.shap...  8.09 us
    all_to_all x1, starting transfers between devices, local(): lax.all_to_all(jnp.broadcast_to(record_table[None], (n_mode,) + record_ta...  4.38 us
    all_to_all x1, waiting for transfers between devices, local(): lax.all_to_all(jnp.broadcast_to(payload[None], (n_member,) + payload.shap...  3.95 us
  transfers between devices with their start and end apart: 2, of which 2 were waited for; matrix products, arithmetic and copies ran while one was open for 3% of the time, Pallas kernels for 6%

profile of v11, /device:TPU:0, one launch (start us, length us, event | category | flops | bytes accessed | tf_op | source)
XLA Modules:
  0.0 139.2 jit_solution(1085322628457521391)
XLA Ops:
  0.0 1.3 broadcast_in_dim.4
  1.3 4.4 %all-to-all-start = ((s32[8,4,8]{2,1,0:T(4,128)}), s32[8,4,8]{2,1,0:T(4,128)S(1)}, u32[]{:S(2)}, u32[]{:S(2)}) async-start(s32[8,4,8]{2,1,0:T(4,128)} %broadcast_in_dim.4), calls=%async_computation | async-start | bytes 32768 | tf_op jit(solution)/shard_map/all_to_all | solution.py:151
  5.7 1.6 %rev.3 = bf16[32,512]{1,0:T(8,128)(2,1)S(1)} reverse(bf16[32,512]{1,0:T(8,128)(2,1)} %param.11), dimensions={1} | reverse | bytes 65536 | tf_op jit(solution)/shard_map/rev | solution.py:148
  7.3 0.7 tile.4
  8.1 0.6 tile.10
  8.7 0.0 copy-start.1
  8.7 0.0 copy-start.2
  8.7 0.2 slice.27
  8.9 0.1 copy.28
  9.1 0.2 convolution_convert_fusion
  9.3 1.7 %all-to-all-done = s32[8,4,8]{2,1,0:T(4,128)S(1)} async-done(((s32[8,4,8]{2,1,0:T(4,128)}), s32[8,4,8]{2,1,0:T(4,128)S(1)}, u32[]{:S(2)}, u32[]{:S(2)}) %all-to-all-start) | async-done | bytes 1056 | tf_op jit(solution)/shard_map/all_to_all | solution.py:151
  11.0 0.1 convert_element_type.25
  11.2 0.9 broadcast_in_dim.5
  12.1 8.1 %all-to-all-start.1 = ((bf16[16,40,512]{2,1,0:T(8,128)(2,1)}), bf16[16,40,512]{2,1,0:T(8,128)(2,1)}, u32[]{:S(2)}, u32[]{:S(2)}) async-start(bf16[16,40,512]{2,1,0:T(8,128)(2,1)} %broadcast_in_dim.5), calls=%async_computation.1 | async-start | bytes 1310720 | tf_op jit(solution)/shard_map/all_to_all | solution.py:160
  20.2 0.1 eq.30
  20.3 0.0 copy-done.1
  20.3 0.0 copy-done.2
  20.3 8.9 %shard_map.82.gs_ref = bf16[6,512,512]{2,1,0:T(8,128)(2,1)S(1)} custom-call(bf16[6144,512]{1,0:T(8,128)(2,1)} %ms_ref.1, s32[1,1024]{1,0:T(1,128)S(1)} %add_bitcast_fusion.gi_ref), custom_call_target="tpu_custom_call" | custom-call | tf_op jit(solution)/shard_map/pallas_call | solution.py:46
  29.2 0.0 copy-start
  29.2 4.0 %all-to-all-done.1.g_ref = bf16[16,40,512]{2,1,0:T(8,128)(2,1)} async-done(((bf16[16,40,512]{2,1,0:T(8,128)(2,1)}), bf16[16,40,512]{2,1,0:T(8,128)(2,1)}, u32[]{:S(2)}, u32[]{:S(2)}) %all-to-all-start.1) | async-done | bytes 655392 | tf_op jit(solution)/shard_map/all_to_all | solution.py:160
  33.1 0.9 slice.29
  34.0 1.4 copy.25
  35.4 0.8 slice.30
  36.3 0.1 copy.21
  36.4 0.1 copy.22
  36.6 0.1 copy.23
  36.7 0.0 copy-done
  36.7 77.4 %shard_map.83 = f32[4096,128]{1,0:T(8,128)S(1)} custom-call(f32[8,6]{1,0:T(8,128)S(1)} %copy-done, bf16[6,512,512]{2,1,0:T(8,128)(2,1)S(1)} %shard_map.82.gs_ref, bf16[16,40,512]{2,1,0:T(8,128)(2,1)} %all-to-all-done.1.g_ref, f32[512,32]{1,0:T(8,128)S(1)} %compare_convert_fusion.pick_ref), custom_call_target="tpu_custom_call" | custom-call | tf_op jit(solution)/shard_map/pallas_call | solution.py:107
  114.1 0.0 copy-start.3
  114.1 0.1 convert_element_type.27
  114.3 24.0 %all_to_all.15 = bf16[128,4,8,128]{3,2,1,0:T(8,128)(2,1)S(1)} all-to-all(bf16[128,4,8,128]{3,2,1,0:T(8,128)(2,1)S(1)} %bitcast.18), channel_id=1, replica_groups=mesh['mode'=8,'member'=16] {'mode','member'}, dimensions={0} | all-to-all | bytes 2097152 | tf_op jit(solution)/shard_map/all_to_all | solution.py:174
  138.3 0.2 convert_reduce_fusion
  138.5 0.0 copy-done.3
  138.5 0.7 abs_reduce_fusion
  (11 shorter events, 0.2 us)
Async XLA Ops:
  1.3 9.7 %all-to-all-start = ((s32[8,4,8]{2,1,0:T(4,128)}), s32[8,4,8]{2,1,0:T(4,128)S(1)}, u32[]{:S(2)}, u32[]{:S(2)}) async-start(s32[8,4,8]{2,1,0:T(4,128)} %broadcast_in_dim.4), calls=%async_computation | async-start | bytes 32768 | tf_op jit(solution)/shard_map/all_to_all | solution.py:151
  8.7 11.6 %copy-start.1 = (s32[1024,1]{0,1:T(1,128)S(1)}, s32[1024,1]{0,1:T(1,128)}, u32[]{:S(2)}) copy-start(s32[1024,1]{0,1:T(1,128)} %param.14) | copy-start | bytes 12292
  8.7 11.6 %copy-start.2 = (s32[1024,1]{0,1:T(1,128)S(1)}, s32[1024,1]{0,1:T(1,128)}, u32[]{:S(2)}) copy-start(s32[1024,1]{0,1:T(1,128)} %param.13) | copy-start | bytes 12292
  12.1 21.1 %all-to-all-start.1 = ((bf16[16,40,512]{2,1,0:T(8,128)(2,1)}), bf16[16,40,512]{2,1,0:T(8,128)(2,1)}, u32[]{:S(2)}, u32[]{:S(2)}) async-start(bf16[16,40,512]{2,1,0:T(8,128)(2,1)} %broadcast_in_dim.5), calls=%async_computation.1 | async-start | bytes 1310720 | tf_op jit(solution)/shard_map/all_to_all | solution.py:160
  29.2 7.6 %copy-start = (f32[8,6]{1,0:T(8,128)S(1)}, f32[8,6]{1,0:T(8,128)}, u32[]{:S(2)}) copy-start(f32[8,6]{1,0:T(8,128)} %coef_ref.1) | copy-start | bytes 580
  114.1 24.4 %copy-start.3 = (f32[4,8]{1,0:T(4,128)S(1)}, f32[4,8]{1,0:T(4,128)}, u32[]{:S(2)}) copy-start(f32[4,8]{1,0:T(4,128)} %param.17) | copy-start | bytes 388

commit v12 on v10

--- a/solution.py
+++ b/solution.py
@@ -75,22 +75,20 @@
         groups = q_scr.shape[1]
         cases = coef_ref.shape[0]
         steps = q_scr.shape[2] // records
-        chunk = 32
+        chunk = 64
 
         def mix(i, carry):
             g0 = pl.multiple_of(i * chunk, chunk)
-            rows = pl.ds(g0, chunk)
-            accs = [jnp.zeros((chunk, steps), jnp.float32) for _ in range(cases)]
-            for r in range(records):
-                cols = pl.ds(r * steps, steps)
-                slabs = [q_scr[cc, rows, cols] for cc in range(q_scr.shape[0])]
-                for s in range(cases):
-                    mixed = coef_ref[s, 0] * slabs[0]
-                    for cc in range(1, len(slabs)):
-                        mixed = mixed + coef_ref[s, cc] * slabs[cc]
-                    accs[s] = accs[s] + pick_ref[rows, pl.ds(s * records + r, 1)] * mixed
             for s in range(cases):
-                out_ref[pl.ds(g0 * cases + s, chunk, stride=cases), :] = accs[s]
+                acc = jnp.zeros((chunk, steps), jnp.float32)
+                for r in range(records):
+                    cols = pl.ds(r * steps, steps)
+                    mixed = coef_ref[s, 0] * q_scr[0, pl.ds(g0, chunk), cols]
+                    for cc in range(1, q_scr.shape[0]):
+                        mixed = mixed + coef_ref[s, cc] * q_scr[cc, pl.ds(g0, chunk), cols]
+                    pick = pick_ref[pl.ds(g0, chunk), pl.ds(s * records + r, 1)]
+                    acc = acc + pick * mixed
+                out_ref[pl.ds(g0 * cases + s, chunk, stride=cases), :] = acc
             return carry
 
         lax.fori_loop(0, groups // chunk, mix, 0)

time: 70.8 us -> 70.4 us (level)
  no operation moved by 1% of the time
where the time goes in v12:
time: 70.4 us; the launch traced here: 69.7 us
  blocking collectives  24 us (34%)
  Pallas kernels  16.7 us (24%)
  starting transfers between devices  12.5 us (18%)
  local copies, waits for them, and re-layouts  9.25 us (13%)
  waiting for transfers between devices  5.66 us (8%)
  other arithmetic  1.09 us (2%)
    all_to_all x1, blocking collectives, local(): lax.all_to_all(share.astype(jnp.bfloat16), ('mode', 'member'), split_axis...  24 us
    pallas_call x1, Pallas kernels, shape_sums(): pl.pallas_call(functools.partial(shape_sum_kernel, comps=comps, tile=tile...  8.88 us
    all_to_all x1, starting transfers between devices, local(): lax.all_to_all(jnp.broadcast_to(payload[None], (n_member,) + payload.shap...  8.09 us
    pallas_call x1, Pallas kernels, group_shares(): pl.pallas_call(functools.partial(mix_kernel, records=records), grid=(comp...  7.83 us
    all_to_all x1, starting transfers between devices, local(): lax.all_to_all(jnp.broadcast_to(record_table[None], (n_mode,) + record_ta...  4.38 us
    all_to_all x1, waiting for transfers between devices, local(): lax.all_to_all(jnp.broadcast_to(payload[None], (n_member,) + payload.shap...  3.95 us
    slice x2, local copies, waits for them, and re-layouts, local(): gathered[:, resp_rows:].reshape(n_member, -1)[:, :rec_col.shape[0]]  1.76 us
    all_to_all x1, waiting for transfers between devices, local(): lax.all_to_all(jnp.broadcast_to(record_table[None], (n_mode,) + record_ta...  1.71 us
  transfers between devices with their start and end apart: 2, of which 2 were waited for; matrix products, arithmetic and copies ran while one was open for 5% of the time, Pallas kernels for 13%

profile of v12, /device:TPU:0, one launch (start us, length us, event | category | flops | bytes accessed | tf_op | source)
XLA Modules:
  0.0 69.7 jit_solution(3595533933421853042)
XLA Ops:
  0.0 1.3 %broadcast_in_dim.4 = s32[8,4,8]{2,1,0:T(4,128)} broadcast(s32[4,8]{1,0:T(4,128)} %param.15), dimensions={1,2} | broadcast | bytes 1152 | tf_op jit(solution)/shard_map/broadcast_in_dim | solution.py:148
  1.3 4.4 %all-to-all-start = ((s32[8,4,8]{2,1,0:T(4,128)}), s32[8,4,8]{2,1,0:T(4,128)S(1)}, u32[]{:S(2)}, u32[]{:S(2)}) async-start(s32[8,4,8]{2,1,0:T(4,128)} %broadcast_in_dim.4), calls=%async_computation | async-start | bytes 32768 | tf_op jit(solution)/shard_map/all_to_all | solution.py:147
  5.7 1.6 %rev.3 = bf16[32,512]{1,0:T(8,128)(2,1)S(1)} reverse(bf16[32,512]{1,0:T(8,128)(2,1)} %param.11), dimensions={1} | reverse | bytes 65536 | tf_op jit(solution)/shard_map/rev | solution.py:144
  7.3 0.7 %tile.4 = bf16[4,129,639]{2,1,0:T(8,128)(2,1)S(1)} broadcast(bf16[4,639]{1,0:T(4,128)(2,1)} %param.10), dimensions={0,2} | broadcast | bytes 664560 | tf_op jit(solution)/shard_map/tile | solution.py:14
  8.1 0.6 tile.10
  8.7 0.0 copy-start.1
  8.7 0.0 copy-start.2
  8.7 0.2 slice.27
  8.9 0.1 copy.28
  9.1 0.2 convolution_convert_fusion
  9.3 1.7 %all-to-all-done = s32[8,4,8]{2,1,0:T(4,128)S(1)} async-done(((s32[8,4,8]{2,1,0:T(4,128)}), s32[8,4,8]{2,1,0:T(4,128)S(1)}, u32[]{:S(2)}, u32[]{:S(2)}) %all-to-all-start) | async-done | bytes 1056 | tf_op jit(solution)/shard_map/all_to_all | solution.py:147
  11.0 0.1 convert_element_type.25
  11.2 0.9 %broadcast_in_dim.5 = bf16[16,40,512]{2,1,0:T(8,128)(2,1)} broadcast(bf16[40,512]{1,0:T(8,128)(2,1)S(1)} %pad_maximum_fusion), dimensions={1,2} | broadcast | bytes 696320 | tf_op jit(solution)/shard_map/broadcast_in_dim | solution.py:157
  12.1 8.1 %all-to-all-start.1 = ((bf16[16,40,512]{2,1,0:T(8,128)(2,1)}), bf16[16,40,512]{2,1,0:T(8,128)(2,1)}, u32[]{:S(2)}, u32[]{:S(2)}) async-start(bf16[16,40,512]{2,1,0:T(8,128)(2,1)} %broadcast_in_dim.5), calls=%async_computation.1 | async-start | bytes 1310720 | tf_op jit(solution)/shard_map/all_to_all | solution.py:156
  20.2 0.1 eq.30
  20.3 0.0 copy-done.1
  20.3 0.0 copy-done.2
  20.3 8.9 %shard_map.82.gs_ref = bf16[6,512,512]{2,1,0:T(8,128)(2,1)S(1)} custom-call(bf16[6144,512]{1,0:T(8,128)(2,1)} %ms_ref.1, s32[1,1024]{1,0:T(1,128)S(1)} %add_bitcast_fusion.gi_ref), custom_call_target="tpu_custom_call" | custom-call | tf_op jit(solution)/shard_map/pallas_call | solution.py:46
  29.2 0.0 copy-start
  29.2 4.0 %all-to-all-done.1.g_ref = bf16[16,40,512]{2,1,0:T(8,128)(2,1)} async-done(((bf16[16,40,512]{2,1,0:T(8,128)(2,1)}), bf16[16,40,512]{2,1,0:T(8,128)(2,1)}, u32[]{:S(2)}, u32[]{:S(2)}) %all-to-all-start.1) | async-done | bytes 655392 | tf_op jit(solution)/shard_map/all_to_all | solution.py:156
  33.1 0.9 %slice.29 = bf16[16,8,512]{2,1,0:T(8,128)(2,1)S(1)} slice(bf16[16,40,512]{2,1,0:T(8,128)(2,1)} %all-to-all-done.1.g_ref), slice={[0:16], [32:40], [0:512]} | slice | bytes 262144 | tf_op jit(solution)/shard_map/slice | solution.py:159
  34.0 1.4 %copy.25 = bf16[16,8,512]{0,2,1:T(8,128)(2,1)} copy(bf16[16,8,512]{2,1,0:T(8,128)(2,1)S(1)} %slice.29) | data formatting | bytes 262144 | tf_op jit(solution)/shard_map/reshape | solution.py:159
  35.4 0.8 %slice.30 = bf16[16,256]{0,1:T(8,128)(2,1)S(1)} slice(bf16[16,4096]{0,1:T(8,128)(2,1)} %bitcast.22), slice={[0:16], [0:256]} | slice | bytes 16384 | tf_op jit(solution)/shard_map/slice | solution.py:159
  36.3 0.1 copy.21
  36.4 0.1 copy.22
  36.6 0.1 copy.23
  36.7 0.0 copy-done
  36.7 7.8 %shard_map.83 = f32[4096,128]{1,0:T(8,128)S(1)} custom-call(f32[8,6]{1,0:T(8,128)S(1)} %copy-done, bf16[6,512,512]{2,1,0:T(8,128)(2,1)S(1)} %shard_map.82.gs_ref, bf16[16,40,512]{2,1,0:T(8,128)(2,1)} %all-to-all-done.1.g_ref, f32[512,32]{1,0:T(8,128)S(1)} %compare_convert_fusion.pick_ref), custom_call_target="tpu_custom_call" | custom-call | tf_op jit(solution)/shard_map/pallas_call | solution.py:103
  44.6 0.0 copy-start.3
  44.6 0.1 convert_element_type.27
  44.7 24.0 %all_to_all.15 = bf16[128,4,8,128]{3,2,1,0:T(8,128)(2,1)S(1)} all-to-all(bf16[128,4,8,128]{3,2,1,0:T(8,128)(2,1)S(1)} %bitcast.18), channel_id=1, replica_groups=mesh['mode'=8,'member'=16] {'mode','member'}, dimensions={0} | all-to-all | bytes 2097152 | tf_op jit(solution)/shard_map/all_to_all | solution.py:170
  68.7 0.2 convert_reduce_fusion
  68.9 0.0 copy-done.3
  68.9 0.7 %abs_reduce_fusion = f32[4,8]{1,0:T(4,128)} fusion(f32[4,8,128]{2,1,0:T(8,128)S(1)} %convert_reduce_fusion, f32[4,8]{1,0:T(4,128)S(1)} %copy-done.3), kind=kLoop, calls=%fused_computation.6 | loop fusion | flops 12256 | bytes 16640 | tf_op jit(solution)/shard_map/reduce_max | solution.py:175
  (11 shorter events, 0.2 us)
Async XLA Ops:
  1.3 9.7 %all-to-all-start = ((s32[8,4,8]{2,1,0:T(4,128)}), s32[8,4,8]{2,1,0:T(4,128)S(1)}, u32[]{:S(2)}, u32[]{:S(2)}) async-start(s32[8,4,8]{2,1,0:T(4,128)} %broadcast_in_dim.4), calls=%async_computation | async-start | bytes 32768 | tf_op jit(solution)/shard_map/all_to_all | solution.py:147
  8.7 11.6 %copy-start.1 = (s32[1024,1]{0,1:T(1,128)S(1)}, s32[1024,1]{0,1:T(1,128)}, u32[]{:S(2)}) copy-start(s32[1024,1]{0,1:T(1,128)} %param.14) | copy-start | bytes 12292
  8.7 11.6 %copy-start.2 = (s32[1024,1]{0,1:T(1,128)S(1)}, s32[1024,1]{0,1:T(1,128)}, u32[]{:S(2)}) copy-start(s32[1024,1]{0,1:T(1,128)} %param.13) | copy-start | bytes 12292
  12.1 21.1 %all-to-all-start.1 = ((bf16[16,40,512]{2,1,0:T(8,128)(2,1)}), bf16[16,40,512]{2,1,0:T(8,128)(2,1)}, u32[]{:S(2)}, u32[]{:S(2)}) async-start(bf16[16,40,512]{2,1,0:T(8,128)(2,1)} %broadcast_in_dim.5), calls=%async_computation.1 | async-start | bytes 1310720 | tf_op jit(solution)/shard_map/all_to_all | solution.py:156
  29.2 7.6 %copy-start = (f32[8,6]{1,0:T(8,128)S(1)}, f32[8,6]{1,0:T(8,128)}, u32[]{:S(2)}) copy-start(f32[8,6]{1,0:T(8,128)} %coef_ref.1) | copy-start | bytes 580
  44.6 24.3 %copy-start.3 = (f32[4,8]{1,0:T(4,128)S(1)}, f32[4,8]{1,0:T(4,128)}, u32[]{:S(2)}) copy-start(f32[4,8]{1,0:T(4,128)} %param.17) | copy-start | bytes 388

commit v13 on v12

--- a/solution.py
+++ b/solution.py
@@ -57,7 +57,7 @@
     )(mode_shapes, group_index)
 
 
-def mix_kernel(coef_ref, gs_ref, g_ref, pick_ref, out_ref, q_scr, r_scr, *, records):
+def mix_kernel(coef_ref, gs_ref, g_ref, rec_ref, out_ref, q_scr, r_scr, *, records, per_owner):
     c = pl.program_id(0)
     comps = pl.num_programs(0)
     senders, _, width = g_ref.shape
@@ -75,10 +75,19 @@
         groups = q_scr.shape[1]
         cases = coef_ref.shape[0]
         steps = q_scr.shape[2] // records
-        chunk = 64
-
-        def mix(i, carry):
-            g0 = pl.multiple_of(i * chunk, chunk)
+        slots = width // 128
+        chunk = senders * per_owner
+        for i in range(groups // chunk):
+            g0 = i * chunk
+            pick = jnp.concatenate(
+                [
+                    rec_ref[j, pl.ds(q * (rec_ref.shape[1] // per_owner) + i // slots, 1),
+                            pl.ds((i % slots) * 128, 128)]
+                    for j in range(senders)
+                    for q in range(per_owner)
+                ],
+                axis=0,
+            )
             for s in range(cases):
                 acc = jnp.zeros((chunk, steps), jnp.float32)
                 for r in range(records):
@@ -86,28 +95,23 @@
                     mixed = coef_ref[s, 0] * q_scr[0, pl.ds(g0, chunk), cols]
                     for cc in range(1, q_scr.shape[0]):
                         mixed = mixed + coef_ref[s, cc] * q_scr[cc, pl.ds(g0, chunk), cols]
-                    pick = pick_ref[pl.ds(g0, chunk), pl.ds(s * records + r, 1)]
-                    acc = acc + pick * mixed
+                    acc = acc + pick[:, s * records + r : s * records + r + 1] * mixed
                 out_ref[pl.ds(g0 * cases + s, chunk, stride=cases), :] = acc
-            return carry
-
-        lax.fori_loop(0, groups // chunk, mix, 0)
 
 
-def group_shares(case_coef, shape_groups, gathered, resp_rows, record_pick):
+def group_shares(case_coef, shape_groups, gathered, rec_rows, records, per_owner):
     comps, groups, modes = shape_groups.shape
-    width = gathered.shape[2]
+    senders, _, width = gathered.shape
     cases = case_coef.shape[0]
-    records = record_pick.shape[1] // cases
     steps = width // records
     return pl.pallas_call(
-        functools.partial(mix_kernel, records=records),
+        functools.partial(mix_kernel, records=records, per_owner=per_owner),
         grid=(comps,),
         in_specs=[
             pl.BlockSpec(memory_space=pltpu.SMEM),
             pl.BlockSpec((1, groups, modes), lambda c: (c, 0, 0)),
             pl.BlockSpec(gathered.shape, lambda c: (0, 0, 0)),
-            pl.BlockSpec((groups, cases * records), lambda c: (0, 0)),
+            pl.BlockSpec(rec_rows.shape, lambda c: (0, 0, 0)),
         ],
         out_specs=pl.BlockSpec((groups * cases, steps), lambda c: (0, 0)),
         out_shape=jax.ShapeDtypeStruct((groups * cases, steps), jnp.float32),
@@ -116,7 +120,7 @@
             pltpu.VMEM((modes, width), gathered.dtype),
         ],
         compiler_params=pltpu.CompilerParams(vmem_limit_bytes=48 * 1024 * 1024),
-    )(case_coef, shape_groups, gathered, record_pick)
+    )(case_coef, shape_groups, gathered, rec_rows)
 
 
 def local(
@@ -147,24 +151,18 @@
     rec_col = lax.all_to_all(
         jnp.broadcast_to(record_table[None], (n_mode,) + record_table.shape), "mode", 0, 0
     ).reshape(-1)
-    rec_rows = -(-rec_col.shape[0] // width)
-    rec_rows = -(-rec_rows // 8) * 8
-    rec_block = jnp.zeros((rec_rows * width,), jnp.bfloat16).at[: rec_col.shape[0]].set(
-        rec_col.astype(jnp.bfloat16)
-    )
-    payload = jnp.concatenate([local_resp, rec_block.reshape(rec_rows, width)], axis=0)
+    onehot = (rec_col.reshape(n_mode, groups_here, case_count)[..., None] == jnp.arange(record_count))
+    onehot = onehot.reshape(n_mode, groups_here, case_count * record_count)
+    onehot = jnp.pad(onehot, ((0, 0), (0, 0), (0, 128 - case_count * record_count)))
+    rec_rows = groups_here * (n_mode * 128 // width)
+    rec_block = jnp.transpose(onehot, (1, 0, 2)).reshape(rec_rows, width).astype(jnp.bfloat16)
+    payload = jnp.concatenate([local_resp, rec_block], axis=0)
     gathered = lax.all_to_all(
         jnp.broadcast_to(payload[None], (n_member,) + payload.shape), "member", 0, 0
     )
-    rec_all = gathered[:, resp_rows:].reshape(n_member, -1)[:, : rec_col.shape[0]]
-    rec_all = rec_all.astype(jnp.int32).reshape(n_member, n_mode, groups_here, case_count)
-    rec_all = jnp.transpose(rec_all, (1, 0, 2, 3)).reshape(group_total, case_count)
-
-    record_pick = (rec_all[:, :, None] == jnp.arange(record_count)[None, None, :]).astype(
-        jnp.float32
-    )
+    rec_rows_in = gathered[:, resp_rows:].astype(jnp.float32)
     share = group_shares(
-        case_coef, shape_groups, gathered, resp_rows, record_pick.reshape(group_total, -1)
+        case_coef, shape_groups, gathered, rec_rows_in, record_count, groups_here
     )
     share = share.reshape(owner_total, groups_here, case_count, share.shape[-1])
     received = lax.all_to_all(

time: 70.4 us -> 68.7 us (0.976)
  local copies, waits for them, and re-layouts: 9.25 us -> 5.85 us
  other arithmetic: 1.09 us -> 2.06 us
    slice x2 -> x0, local copies, waits for them, and re-layouts: 1.76 us -> none  [local(): gathered[:, resp_rows:].reshape(n_member, -1)[:, :rec_col.shape[0]]]
    reshape x2 -> x0, local copies, waits for them, and re-layouts: 1.37 us -> none  [the longest x1 1.35 us: local(): gathered[:, resp_rows:].reshape(n_member, -1)[:, :rec_col.shape[0]]]
    convert_element_type x2, other arithmetic: 0.03 us -> 0.94 us  [the longest x1 0.92 us: local(): rec_rows_in = gathered[:, resp_rows:].astype(jnp.float32)]
where the time goes in v13:
time: 68.7 us; the launch traced here: 67.9 us
  blocking collectives  24.1 us (35%)
  Pallas kernels  17.4 us (25%)
  starting transfers between devices  12.5 us (18%)
  local copies, waits for them, and re-layouts  5.85 us (9%)
  waiting for transfers between devices  5.63 us (8%)
  other arithmetic  2.06 us (3%)
    all_to_all x1, blocking collectives, local(): lax.all_to_all(share.astype(jnp.bfloat16), ('mode', 'member'), split_axis...  24.1 us
    pallas_call x1, Pallas kernels, shape_sums(): pl.pallas_call(functools.partial(shape_sum_kernel, comps=comps, tile=tile...  8.88 us
    pallas_call x1, Pallas kernels, group_shares(): pl.pallas_call(functools.partial(mix_kernel, records=records, per_owner=p...  8.5 us
    all_to_all x1, starting transfers between devices, local(): lax.all_to_all(jnp.broadcast_to(payload[None], (n_member,) + payload.shap...  8.09 us
    all_to_all x1, starting transfers between devices, local(): lax.all_to_all(jnp.broadcast_to(record_table[None], (n_mode,) + record_ta...  4.38 us
    all_to_all x1, waiting for transfers between devices, local(): lax.all_to_all(jnp.broadcast_to(payload[None], (n_member,) + payload.shap...  4.03 us
    rev x1, local copies, waits for them, and re-layouts, local(): modal_kernel[:, ::-1]  1.64 us
    all_to_all x1, waiting for transfers between devices, local(): lax.all_to_all(jnp.broadcast_to(record_table[None], (n_mode,) + record_ta...  1.6 us
  transfers between devices with their start and end apart: 2, of which 2 were waited for; matrix products, arithmetic and copies ran while one was open for 5% of the time, Pallas kernels for 13%

profile of v13, /device:TPU:0, one launch (start us, length us, event | category | flops | bytes accessed | tf_op | source)
XLA Modules:
  0.0 67.9 jit_solution(10955292717584949685)
XLA Ops:
  0.0 1.3 %broadcast_in_dim.4 = s32[8,4,8]{2,1,0:T(4,128)} broadcast(s32[4,8]{1,0:T(4,128)} %param.13), dimensions={1,2} | broadcast | bytes 1152 | tf_op jit(solution)/shard_map/broadcast_in_dim | solution.py:152
  1.3 4.4 %all-to-all-start = ((s32[8,4,8]{2,1,0:T(4,128)}), s32[8,4,8]{2,1,0:T(4,128)S(1)}, u32[]{:S(2)}, u32[]{:S(2)}) async-start(s32[8,4,8]{2,1,0:T(4,128)} %broadcast_in_dim.4), calls=%async_computation | async-start | bytes 32768 | tf_op jit(solution)/shard_map/all_to_all | solution.py:151
  5.7 1.6 %rev.3 = bf16[32,512]{1,0:T(8,128)(2,1)S(1)} reverse(bf16[32,512]{1,0:T(8,128)(2,1)} %param.9), dimensions={1} | reverse | bytes 65536 | tf_op jit(solution)/shard_map/rev | solution.py:148
  7.3 0.7 %tile.4 = bf16[4,129,639]{2,1,0:T(8,128)(2,1)S(1)} broadcast(bf16[4,639]{1,0:T(4,128)(2,1)} %param.8), dimensions={0,2} | broadcast | bytes 664560 | tf_op jit(solution)/shard_map/tile | solution.py:14
  8.1 0.6 tile.10
  8.7 0.0 copy-start.1
  8.7 0.0 copy-start.2
  8.7 0.2 slice.12
  8.9 0.1 copy.16
  9.1 0.2 convolution_convert_fusion
  9.3 0.1 eq.23
  9.4 1.6 %all-to-all-done = s32[8,4,8]{2,1,0:T(4,128)S(1)} async-done(((s32[8,4,8]{2,1,0:T(4,128)}), s32[8,4,8]{2,1,0:T(4,128)S(1)}, u32[]{:S(2)}, u32[]{:S(2)}) %all-to-all-start) | async-done | bytes 1056 | tf_op jit(solution)/shard_map/all_to_all | solution.py:151
  11.0 0.1 copy.12
  11.1 0.1 broadcast_compare_fusion
  11.2 0.1 copy.13
  11.4 0.9 %broadcast_in_dim.5 = bf16[16,40,512]{2,1,0:T(8,128)(2,1)} broadcast(bf16[40,512]{1,0:T(8,128)(2,1)S(1)} %pad_maximum_fusion), dimensions={1,2} | broadcast | bytes 696320 | tf_op jit(solution)/shard_map/broadcast_in_dim | solution.py:161
  12.3 8.1 %all-to-all-start.1 = ((bf16[16,40,512]{2,1,0:T(8,128)(2,1)}), bf16[16,40,512]{2,1,0:T(8,128)(2,1)}, u32[]{:S(2)}, u32[]{:S(2)}) async-start(bf16[16,40,512]{2,1,0:T(8,128)(2,1)} %broadcast_in_dim.5), calls=%async_computation.1 | async-start | bytes 1310720 | tf_op jit(solution)/shard_map/all_to_all | solution.py:160
  20.4 0.0 copy-done.1
  20.4 0.0 copy-done.2
  20.4 0.0 copy-start
  20.4 8.9 %shard_map.82.gs_ref = bf16[6,512,512]{2,1,0:T(8,128)(2,1)S(1)} custom-call(bf16[6144,512]{1,0:T(8,128)(2,1)} %ms_ref.1, s32[1,1024]{1,0:T(1,128)S(1)} %add_bitcast_fusion.gi_ref), custom_call_target="tpu_custom_call" | custom-call | tf_op jit(solution)/shard_map/pallas_call | solution.py:46
  29.3 4.0 %all-to-all-done.1.g_ref = bf16[16,40,512]{2,1,0:T(8,128)(2,1)} async-done(((bf16[16,40,512]{2,1,0:T(8,128)(2,1)}), bf16[16,40,512]{2,1,0:T(8,128)(2,1)}, u32[]{:S(2)}, u32[]{:S(2)}) %all-to-all-start.1) | async-done | bytes 655392 | tf_op jit(solution)/shard_map/all_to_all | solution.py:160
  33.3 0.9 %slice_convert_fusion.rec_ref = f32[16,8,512]{2,1,0:T(8,128)S(1)} fusion(bf16[16,40,512]{2,1,0:T(8,128)(2,1)} %all-to-all-done.1.g_ref), kind=kLoop, calls=%fused_computation.5 | loop fusion | flops 65536 | bytes 393216 | tf_op jit(solution)/shard_map/convert_element_type | solution.py:163
  34.2 0.0 copy-done
  34.3 8.5 %shard_map.83 = f32[4096,128]{1,0:T(8,128)S(1)} custom-call(f32[8,6]{1,0:T(8,128)S(1)} %copy-done, bf16[6,512,512]{2,1,0:T(8,128)(2,1)S(1)} %shard_map.82.gs_ref, bf16[16,40,512]{2,1,0:T(8,128)(2,1)} %all-to-all-done.1.g_ref, f32[16,8,512]{2,1,0:T(8,128)S(1)} %slice_convert_fusion.rec_ref), custom_call_target="tpu_custom_call" | custom-call | tf_op jit(solution)/shard_map/pallas_call | solution.py:107
  42.8 0.0 copy-start.3
  42.8 0.1 convert_element_type.31
  42.9 24.1 %all_to_all.15 = bf16[128,4,8,128]{3,2,1,0:T(8,128)(2,1)S(1)} all-to-all(bf16[128,4,8,128]{3,2,1,0:T(8,128)(2,1)S(1)} %bitcast.13), channel_id=1, replica_groups=mesh['mode'=8,'member'=16] {'mode','member'}, dimensions={0} | all-to-all | bytes 2097152 | tf_op jit(solution)/shard_map/all_to_all | solution.py:168
  67.0 0.2 convert_reduce_fusion
  67.2 0.0 copy-done.3
  67.2 0.7 %abs_reduce_fusion = f32[4,8]{1,0:T(4,128)} fusion(f32[4,8,128]{2,1,0:T(8,128)S(1)} %convert_reduce_fusion, f32[4,8]{1,0:T(4,128)S(1)} %copy-done.3), kind=kLoop, calls=%fused_computation.8 | loop fusion | flops 12256 | bytes 16640 | tf_op jit(solution)/shard_map/reduce_max | solution.py:173
  (7 shorter events, 0.1 us)
Async XLA Ops:
  1.3 9.7 %all-to-all-start = ((s32[8,4,8]{2,1,0:T(4,128)}), s32[8,4,8]{2,1,0:T(4,128)S(1)}, u32[]{:S(2)}, u32[]{:S(2)}) async-start(s32[8,4,8]{2,1,0:T(4,128)} %broadcast_in_dim.4), calls=%async_computation | async-start | bytes 32768 | tf_op jit(solution)/shard_map/all_to_all | solution.py:151
  8.7 11.7 %copy-start.1 = (s32[1024,1]{0,1:T(1,128)S(1)}, s32[1024,1]{0,1:T(1,128)}, u32[]{:S(2)}) copy-start(s32[1024,1]{0,1:T(1,128)} %param.12) | copy-start | bytes 12292
  8.7 11.7 %copy-start.2 = (s32[1024,1]{0,1:T(1,128)S(1)}, s32[1024,1]{0,1:T(1,128)}, u32[]{:S(2)}) copy-start(s32[1024,1]{0,1:T(1,128)} %param.11) | copy-start | bytes 12292
  12.3 21.1 %all-to-all-start.1 = ((bf16[16,40,512]{2,1,0:T(8,128)(2,1)}), bf16[16,40,512]{2,1,0:T(8,128)(2,1)}, u32[]{:S(2)}, u32[]{:S(2)}) async-start(bf16[16,40,512]{2,1,0:T(8,128)(2,1)} %broadcast_in_dim.5), calls=%async_computation.1 | async-start | bytes 1310720 | tf_op jit(solution)/shard_map/all_to_all | solution.py:160
  20.4 13.9 %copy-start = (f32[8,6]{1,0:T(8,128)S(1)}, f32[8,6]{1,0:T(8,128)}, u32[]{:S(2)}) copy-start(f32[8,6]{1,0:T(8,128)} %coef_ref.1) | copy-start | bytes 580
  42.8 24.4 %copy-start.3 = (f32[4,8]{1,0:T(4,128)S(1)}, f32[4,8]{1,0:T(4,128)}, u32[]{:S(2)}) copy-start(f32[4,8]{1,0:T(4,128)} %param.15) | copy-start | bytes 388

commit v14 on v13

--- a/solution.py
+++ b/solution.py
@@ -57,11 +57,12 @@
     )(mode_shapes, group_index)
 
 
-def mix_kernel(coef_ref, gs_ref, g_ref, rec_ref, out_ref, q_scr, r_scr, *, records, per_owner):
+def mix_kernel(
+    coef_ref, gs_ref, g_ref, out_ref, q_scr, r_scr, *, records, per_owner, resp_rows, rec_rows
+):
     c = pl.program_id(0)
     comps = pl.num_programs(0)
     senders, _, width = g_ref.shape
-    resp_rows = r_scr.shape[0] // senders
 
     @pl.when(c == 0)
     def _():
@@ -81,8 +82,8 @@
             g0 = i * chunk
             pick = jnp.concatenate(
                 [
-                    rec_ref[j, pl.ds(q * (rec_ref.shape[1] // per_owner) + i // slots, 1),
-                            pl.ds((i % slots) * 128, 128)]
+                    g_ref[j, pl.ds(resp_rows + q * (rec_rows // per_owner) + i // slots, 1),
+                          pl.ds((i % slots) * 128, 128)].astype(jnp.float32)
                     for j in range(senders)
                     for q in range(per_owner)
                 ],
@@ -99,19 +100,24 @@
                 out_ref[pl.ds(g0 * cases + s, chunk, stride=cases), :] = acc
 
 
-def group_shares(case_coef, shape_groups, gathered, rec_rows, records, per_owner):
+def group_shares(case_coef, shape_groups, gathered, resp_rows, records, per_owner):
     comps, groups, modes = shape_groups.shape
     senders, _, width = gathered.shape
     cases = case_coef.shape[0]
     steps = width // records
     return pl.pallas_call(
-        functools.partial(mix_kernel, records=records, per_owner=per_owner),
+        functools.partial(
+            mix_kernel,
+            records=records,
+            per_owner=per_owner,
+            resp_rows=resp_rows,
+            rec_rows=gathered.shape[1] - resp_rows,
+        ),
         grid=(comps,),
         in_specs=[
             pl.BlockSpec(memory_space=pltpu.SMEM),
             pl.BlockSpec((1, groups, modes), lambda c: (c, 0, 0)),
             pl.BlockSpec(gathered.shape, lambda c: (0, 0, 0)),
-            pl.BlockSpec(rec_rows.shape, lambda c: (0, 0, 0)),
         ],
         out_specs=pl.BlockSpec((groups * cases, steps), lambda c: (0, 0)),
         out_shape=jax.ShapeDtypeStruct((groups * cases, steps), jnp.float32),
@@ -120,7 +126,7 @@
             pltpu.VMEM((modes, width), gathered.dtype),
         ],
         compiler_params=pltpu.CompilerParams(vmem_limit_bytes=48 * 1024 * 1024),
-    )(case_coef, shape_groups, gathered, rec_rows)
+    )(case_coef, shape_groups, gathered)
 
 
 def local(
@@ -160,9 +166,8 @@
     gathered = lax.all_to_all(
         jnp.broadcast_to(payload[None], (n_member,) + payload.shape), "member", 0, 0
     )
-    rec_rows_in = gathered[:, resp_rows:].astype(jnp.float32)
     share = group_shares(
-        case_coef, shape_groups, gathered, rec_rows_in, record_count, groups_here
+        case_coef, shape_groups, gathered, resp_rows, record_count, groups_here
     )
     share = share.reshape(owner_total, groups_here, case_count, share.shape[-1])
     received = lax.all_to_all(

time: 68.7 us -> 67.7 us (0.985)
  other arithmetic: 2.06 us -> 1.14 us
    convert_element_type x1 -> x0, other arithmetic: 0.92 us -> none  [local(): rec_rows_in = gathered[:, resp_rows:].astype(jnp.float32)]
  transfers between devices with their start and end apart: 2 -> 2, of which waited for: 2 -> 2; matrix products, arithmetic and copies ran while one was open for 5% -> 6% of each run, Pallas kernels for 13% -> 13%
where the time goes in v14:
time: 67.7 us; the launch traced here: 67 us
  blocking collectives  24.1 us (36%)
  Pallas kernels  17.4 us (26%)
  starting transfers between devices  12.5 us (18%)
  local copies, waits for them, and re-layouts  5.85 us (9%)
  waiting for transfers between devices  5.63 us (8%)
  other arithmetic  1.14 us (2%)
    all_to_all x1, blocking collectives, local(): lax.all_to_all(share.astype(jnp.bfloat16), ('mode', 'member'), split_axis...  24.1 us
    pallas_call x1, Pallas kernels, shape_sums(): pl.pallas_call(functools.partial(shape_sum_kernel, comps=comps, tile=tile...  8.88 us
    pallas_call x1, Pallas kernels, group_shares(): pl.pallas_call(functools.partial(mix_kernel, records=records, per_owner=p...  8.47 us
    all_to_all x1, starting transfers between devices, local(): lax.all_to_all(jnp.broadcast_to(payload[None], (n_member,) + payload.shap...  8.09 us
    all_to_all x1, starting transfers between devices, local(): lax.all_to_all(jnp.broadcast_to(record_table[None], (n_mode,) + record_ta...  4.38 us
    all_to_all x1, waiting for transfers between devices, local(): lax.all_to_all(jnp.broadcast_to(payload[None], (n_member,) + payload.shap...  4.03 us
    rev x1, local copies, waits for them, and re-layouts, local(): modal_kernel[:, ::-1]  1.64 us
    all_to_all x1, waiting for transfers between devices, local(): lax.all_to_all(jnp.broadcast_to(record_table[None], (n_mode,) + record_ta...  1.6 us
  transfers between devices with their start and end apart: 2, of which 2 were waited for; matrix products, arithmetic and copies ran while one was open for 6% of the time, Pallas kernels for 13%

profile of v14, /device:TPU:0, one launch (start us, length us, event | category | flops | bytes accessed | tf_op | source)
XLA Modules:
  0.0 67.0 jit_solution(17145126734223961122)
XLA Ops:
  0.0 1.3 %broadcast_in_dim.4 = s32[8,4,8]{2,1,0:T(4,128)} broadcast(s32[4,8]{1,0:T(4,128)} %param.13), dimensions={1,2} | broadcast | bytes 1152 | tf_op jit(solution)/shard_map/broadcast_in_dim | solution.py:158
  1.3 4.4 %all-to-all-start = ((s32[8,4,8]{2,1,0:T(4,128)}), s32[8,4,8]{2,1,0:T(4,128)S(1)}, u32[]{:S(2)}, u32[]{:S(2)}) async-start(s32[8,4,8]{2,1,0:T(4,128)} %broadcast_in_dim.4), calls=%async_computation | async-start | bytes 32768 | tf_op jit(solution)/shard_map/all_to_all | solution.py:157
  5.7 1.6 %rev.3 = bf16[32,512]{1,0:T(8,128)(2,1)S(1)} reverse(bf16[32,512]{1,0:T(8,128)(2,1)} %param.9), dimensions={1} | reverse | bytes 65536 | tf_op jit(solution)/shard_map/rev | solution.py:154
  7.3 0.7 %tile.4 = bf16[4,129,639]{2,1,0:T(8,128)(2,1)S(1)} broadcast(bf16[4,639]{1,0:T(4,128)(2,1)} %param.8), dimensions={0,2} | broadcast | bytes 664560 | tf_op jit(solution)/shard_map/tile | solution.py:14
  8.1 0.6 tile.10
  8.7 0.0 copy-start.1
  8.7 0.0 copy-start.2
  8.7 0.2 slice.8
  8.9 0.1 copy.16
  9.1 0.2 convolution_convert_fusion
  9.3 0.1 eq.23
  9.4 1.6 %all-to-all-done = s32[8,4,8]{2,1,0:T(4,128)S(1)} async-done(((s32[8,4,8]{2,1,0:T(4,128)}), s32[8,4,8]{2,1,0:T(4,128)S(1)}, u32[]{:S(2)}, u32[]{:S(2)}) %all-to-all-start) | async-done | bytes 1056 | tf_op jit(solution)/shard_map/all_to_all | solution.py:157
  11.0 0.1 copy.12
  11.1 0.1 broadcast_compare_fusion
  11.2 0.1 copy.13
  11.4 0.9 %broadcast_in_dim.5 = bf16[16,40,512]{2,1,0:T(8,128)(2,1)} broadcast(bf16[40,512]{1,0:T(8,128)(2,1)S(1)} %pad_maximum_fusion), dimensions={1,2} | broadcast | bytes 696320 | tf_op jit(solution)/shard_map/broadcast_in_dim | solution.py:167
  12.3 8.1 %all-to-all-start.1 = ((bf16[16,40,512]{2,1,0:T(8,128)(2,1)}), bf16[16,40,512]{2,1,0:T(8,128)(2,1)}, u32[]{:S(2)}, u32[]{:S(2)}) async-start(bf16[16,40,512]{2,1,0:T(8,128)(2,1)} %broadcast_in_dim.5), calls=%async_computation.1 | async-start | bytes 1310720 | tf_op jit(solution)/shard_map/all_to_all | solution.py:166
  20.4 0.0 copy-done.1
  20.4 0.0 copy-done.2
  20.4 0.0 copy-start
  20.4 8.9 %shard_map.82.gs_ref = bf16[6,512,512]{2,1,0:T(8,128)(2,1)S(1)} custom-call(bf16[6144,512]{1,0:T(8,128)(2,1)} %ms_ref.1, s32[1,1024]{1,0:T(1,128)S(1)} %add_bitcast_fusion.gi_ref), custom_call_target="tpu_custom_call" | custom-call | tf_op jit(solution)/shard_map/pallas_call | solution.py:46
  29.3 4.0 %all-to-all-done.1.g_ref = bf16[16,40,512]{2,1,0:T(8,128)(2,1)} async-done(((bf16[16,40,512]{2,1,0:T(8,128)(2,1)}), bf16[16,40,512]{2,1,0:T(8,128)(2,1)}, u32[]{:S(2)}, u32[]{:S(2)}) %all-to-all-start.1) | async-done | bytes 655392 | tf_op jit(solution)/shard_map/all_to_all | solution.py:166
  33.3 0.0 copy-done
  33.3 8.5 %shard_map.83 = f32[4096,128]{1,0:T(8,128)S(1)} custom-call(f32[8,6]{1,0:T(8,128)S(1)} %copy-done, bf16[6,512,512]{2,1,0:T(8,128)(2,1)S(1)} %shard_map.82.gs_ref, bf16[16,40,512]{2,1,0:T(8,128)(2,1)} %all-to-all-done.1.g_ref), custom_call_target="tpu_custom_call" | custom-call | tf_op jit(solution)/shard_map/pallas_call | solution.py:108
  41.8 0.0 copy-start.3
  41.8 0.1 convert_element_type.27
  41.9 24.1 %all_to_all.15 = bf16[128,4,8,128]{3,2,1,0:T(8,128)(2,1)S(1)} all-to-all(bf16[128,4,8,128]{3,2,1,0:T(8,128)(2,1)S(1)} %bitcast.13), channel_id=1, replica_groups=mesh['mode'=8,'member'=16] {'mode','member'}, dimensions={0} | all-to-all | bytes 2097152 | tf_op jit(solution)/shard_map/all_to_all | solution.py:173
  66.0 0.2 convert_reduce_fusion
  66.2 0.0 copy-done.3
  66.2 0.7 %abs_reduce_fusion = f32[4,8]{1,0:T(4,128)} fusion(f32[4,8,128]{2,1,0:T(8,128)S(1)} %convert_reduce_fusion, f32[4,8]{1,0:T(4,128)S(1)} %copy-done.3), kind=kLoop, calls=%fused_computation.7 | loop fusion | flops 12256 | bytes 16640 | tf_op jit(solution)/shard_map/reduce_max | solution.py:178
  (7 shorter events, 0.1 us)
Async XLA Ops:
  1.3 9.7 %all-to-all-start = ((s32[8,4,8]{2,1,0:T(4,128)}), s32[8,4,8]{2,1,0:T(4,128)S(1)}, u32[]{:S(2)}, u32[]{:S(2)}) async-start(s32[8,4,8]{2,1,0:T(4,128)} %broadcast_in_dim.4), calls=%async_computation | async-start | bytes 32768 | tf_op jit(solution)/shard_map/all_to_all | solution.py:157
  8.7 11.7 %copy-start.1 = (s32[1024,1]{0,1:T(1,128)S(1)}, s32[1024,1]{0,1:T(1,128)}, u32[]{:S(2)}) copy-start(s32[1024,1]{0,1:T(1,128)} %param.12) | copy-start | bytes 12292
  8.7 11.7 %copy-start.2 = (s32[1024,1]{0,1:T(1,128)S(1)}, s32[1024,1]{0,1:T(1,128)}, u32[]{:S(2)}) copy-start(s32[1024,1]{0,1:T(1,128)} %param.11) | copy-start | bytes 12292
  12.3 21.1 %all-to-all-start.1 = ((bf16[16,40,512]{2,1,0:T(8,128)(2,1)}), bf16[16,40,512]{2,1,0:T(8,128)(2,1)}, u32[]{:S(2)}, u32[]{:S(2)}) async-start(bf16[16,40,512]{2,1,0:T(8,128)(2,1)} %broadcast_in_dim.5), calls=%async_computation.1 | async-start | bytes 1310720 | tf_op jit(solution)/shard_map/all_to_all | solution.py:166
  20.4 12.9 %copy-start = (f32[8,6]{1,0:T(8,128)S(1)}, f32[8,6]{1,0:T(8,128)}, u32[]{:S(2)}) copy-start(f32[8,6]{1,0:T(8,128)} %coef_ref.1) | copy-start | bytes 580
  41.8 24.4 %copy-start.3 = (f32[4,8]{1,0:T(4,128)S(1)}, f32[4,8]{1,0:T(4,128)}, u32[]{:S(2)}) copy-start(f32[4,8]{1,0:T(4,128)} %param.15) | copy-start | bytes 388

commit v15 on v9

--- a/solution.py
+++ b/solution.py
@@ -74,37 +74,68 @@
     )(case_coef, mode_shapes, group_index)
 
 
-def mix_kernel(gs_ref, resp_ref, pick_ref, out_ref, *, records):
+def mix_kernel(gs_ref, g_ref, out_ref, r_scr, p_scr, *, records, per_owner, resp_rows, rec_rows):
     s = pl.program_id(0)
     cases = pl.num_programs(0)
-    mixed = jnp.dot(gs_ref[0], resp_ref[...], preferred_element_type=jnp.float32)
-    groups = mixed.shape[0]
+    senders, _, width = g_ref.shape
+    groups = p_scr.shape[0]
+    slots = width // 128
+    chunk = senders * per_owner
+
+    @pl.when(s == 0)
+    def _():
+        for j in range(senders):
+            r_scr[pl.ds(j * resp_rows, resp_rows), :] = g_ref[j, pl.ds(0, resp_rows), :]
+        for i in range(groups // chunk):
+            for j in range(senders):
+                for q in range(per_owner):
+                    row = resp_rows + q * (rec_rows // per_owner) + i // slots
+                    p_scr[pl.ds(i * chunk + j * per_owner + q, 1), :] = g_ref[
+                        j, pl.ds(row, 1), pl.ds((i % slots) * 128, 128)
+                    ].astype(jnp.float32)
+
+    mixed = jnp.dot(gs_ref[0], r_scr[...], preferred_element_type=jnp.float32)
     steps = mixed.shape[1] // records
-    acc = None
+    picked = None
     for r in range(records):
-        pick = pick_ref[0, :, r : r + 1]
+        col = p_scr[:, pl.ds(0, 128)]
+        pick = jnp.sum(
+            jnp.where(
+                lax.broadcasted_iota(jnp.int32, col.shape, 1) == s * records + r, col, 0.0
+            ),
+            axis=1,
+            keepdims=True,
+        )
         term = pick * mixed[:, r * steps : (r + 1) * steps]
-        acc = term if acc is None else acc + term
-    out_ref[0] = acc
-
-
-def group_shares(shape_groups, modal_resp, record_pick):
+        picked = term if picked is None else picked + term
+    out_ref[pl.ds(s, groups, stride=cases), :] = picked
+
+
+def group_shares(shape_groups, gathered, resp_rows, records, per_owner):
     cases, groups, modes = shape_groups.shape
-    width = modal_resp.shape[1]
-    records = record_pick.shape[2]
+    senders, _, width = gathered.shape
     steps = width // records
     return pl.pallas_call(
-        functools.partial(mix_kernel, records=records),
+        functools.partial(
+            mix_kernel,
+            records=records,
+            per_owner=per_owner,
+            resp_rows=resp_rows,
+            rec_rows=gathered.shape[1] - resp_rows,
+        ),
         grid=(cases,),
         in_specs=[
             pl.BlockSpec((1, groups, modes), lambda s: (s, 0, 0)),
-            pl.BlockSpec((modes, width), lambda s: (0, 0)),
-            pl.BlockSpec((1, groups, records), lambda s: (s, 0, 0)),
-        ],
-        out_specs=pl.BlockSpec((1, groups, steps), lambda s: (s, 0, 0)),
-        out_shape=jax.ShapeDtypeStruct((cases, groups, steps), jnp.float32),
+            pl.BlockSpec(gathered.shape, lambda s: (0, 0, 0)),
+        ],
+        out_specs=pl.BlockSpec((groups * cases, steps), lambda s: (0, 0)),
+        out_shape=jax.ShapeDtypeStruct((groups * cases, steps), jnp.float32),
+        scratch_shapes=[
+            pltpu.VMEM((modes, width), gathered.dtype),
+            pltpu.VMEM((groups, 128), jnp.float32),
+        ],
         compiler_params=pltpu.CompilerParams(vmem_limit_bytes=48 * 1024 * 1024),
-    )(shape_groups, modal_resp, record_pick)
+    )(shape_groups, gathered)
 
 
 def local(
@@ -135,28 +166,19 @@
     rec_col = lax.all_to_all(
         jnp.broadcast_to(record_table[None], (n_mode,) + record_table.shape), "mode", 0, 0
     ).reshape(-1)
-    rec_rows = -(-rec_col.shape[0] // width)
-    rec_rows = -(-rec_rows // 8) * 8
-    rec_block = jnp.zeros((rec_rows * width,), jnp.bfloat16).at[: rec_col.shape[0]].set(
-        rec_col.astype(jnp.bfloat16)
-    )
-    payload = jnp.concatenate([local_resp, rec_block.reshape(rec_rows, width)], axis=0)
+    onehot = (rec_col.reshape(n_mode, groups_here, case_count)[..., None] == jnp.arange(record_count))
+    onehot = onehot.reshape(n_mode, groups_here, case_count * record_count)
+    onehot = jnp.pad(onehot, ((0, 0), (0, 0), (0, 128 - case_count * record_count)))
+    rec_rows = groups_here * (n_mode * 128 // width)
+    rec_block = jnp.transpose(onehot, (1, 0, 2)).reshape(rec_rows, width).astype(jnp.bfloat16)
+    payload = jnp.concatenate([local_resp, rec_block], axis=0)
     gathered = lax.all_to_all(
         jnp.broadcast_to(payload[None], (n_member,) + payload.shape), "member", 0, 0
     )
-    modal_resp = gathered[:, :resp_rows].reshape(n_member * resp_rows, width)
-    rec_all = gathered[:, resp_rows:].reshape(n_member, -1)[:, : rec_col.shape[0]]
-    rec_all = rec_all.astype(jnp.int32).reshape(n_member, n_mode, groups_here, case_count)
-    rec_all = jnp.transpose(rec_all, (1, 0, 2, 3)).reshape(group_total, case_count)
-
-    record_pick = (rec_all.T[:, :, None] == jnp.arange(record_count)[None, None, :]).astype(
-        jnp.float32
-    )
-    share = group_shares(shape_groups, modal_resp, record_pick)
-    share = share.reshape(case_count, owner_total, groups_here, share.shape[-1])
-    share = jnp.transpose(share.astype(jnp.bfloat16), (1, 2, 0, 3))
+    share = group_shares(shape_groups, gathered, resp_rows, record_count, groups_here)
+    share = share.reshape(owner_total, groups_here, case_count, share.shape[-1])
     received = lax.all_to_all(
-        share, ("mode", "member"), split_axis=0, concat_axis=0, tiled=True
+        share.astype(jnp.bfloat16), ("mode", "member"), split_axis=0, concat_axis=0, tiled=True
     )
     selected = jnp.sum(received.astype(jnp.float32), axis=0)
     combined = gravity[:, :, None] + selected

time: 73.1 us -> 71.1 us (0.973)
  blocking collectives: 0 us -> 28 us
  waiting for transfers between devices: 21.6 us -> 1.58 us
  starting transfers between devices: 20.8 us -> 12.4 us
  local copies, waits for them, and re-layouts: 9.57 us -> 7.79 us
    all_to_all x0 -> x1, blocking collectives: none -> 28 us  [local(): lax.all_to_all(share.astype(jnp.bfloat16), ('mode', 'member'), split_axis...]
    all_to_all x1 -> x0, waiting for transfers between devices: 19 us -> none  [local(): lax.all_to_all(share, ('mode', 'member'), split_axis=0, concat_axis=0, ti...]
    all_to_all x1 -> x0, starting transfers between devices: 8.36 us -> none  [local(): lax.all_to_all(share, ('mode', 'member'), split_axis=0, concat_axis=0, ti...]
    convert_element_type x2, local copies, waits for them, and re-layouts: 1.43 us -> 0.11 us  [local(): jnp.transpose(onehot, (1, 0, 2)).reshape(rec_rows, width)]
    rev x1, local copies, waits for them, and re-layouts: 0.33 us -> 1.64 us  [local(): modal_kernel[:, ::-1]]
    all_to_all x1, waiting for transfers between devices: 2.64 us -> 1.57 us  [local(): lax.all_to_all(jnp.broadcast_to(record_table[None], (n_mode,) + record_ta...]
    unnamed x14 -> x11, local copies, waits for them, and re-layouts: 2.47 us -> 2.03 us
  transfers between devices with their start and end apart: 3 -> 2, of which waited for: 2 -> 1; matrix products, arithmetic and copies ran while one was open for 3% -> 5% of each run, Pallas kernels for 17% -> 17%
where the time goes in v15:
time: 71.1 us; the launch traced here: 70.3 us
  blocking collectives  28 us (39%)
  Pallas kernels  19 us (27%)
  starting transfers between devices  12.4 us (17%)
  local copies, waits for them, and re-layouts  7.79 us (11%)
  waiting for transfers between devices  1.58 us (2%)
  other arithmetic  1.14 us (2%)
    all_to_all x1, blocking collectives, local(): lax.all_to_all(share.astype(jnp.bfloat16), ('mode', 'member'), split_axis...  28 us
    pallas_call x1, Pallas kernels, shape_sums(): pl.pallas_call(functools.partial(shape_sum_kernel, comps=comps, tile=tile...  12.1 us
    all_to_all x1, starting transfers between devices, local(): lax.all_to_all(jnp.broadcast_to(payload[None], (n_member,) + payload.shap...  8.05 us
    pallas_call x1, Pallas kernels, group_shares(): pl.pallas_call(functools.partial(mix_kernel, records=records, per_owner=p...  6.82 us
    all_to_all x1, starting transfers between devices, local(): lax.all_to_all(jnp.broadcast_to(record_table[None], (n_mode,) + record_ta...  4.38 us
    unnamed x11, local copies, waits for them, and re-layouts  2.03 us
    rev x1, local copies, waits for them, and re-layouts, local(): modal_kernel[:, ::-1]  1.64 us
    all_to_all x1, waiting for transfers between devices, local(): lax.all_to_all(jnp.broadcast_to(record_table[None], (n_mode,) + record_ta...  1.57 us
  transfers between devices with their start and end apart: 2, of which 1 were waited for; matrix products, arithmetic and copies ran while one was open for 5% of the time, Pallas kernels for 17%

profile of v15, /device:TPU:0, one launch (start us, length us, event | category | flops | bytes accessed | tf_op | source)
XLA Modules:
  0.0 70.3 jit_solution(1449151514713857205)
XLA Ops:
  0.0 1.3 %broadcast_in_dim.4 = s32[8,4,8]{2,1,0:T(4,128)} broadcast(s32[4,8]{1,0:T(4,128)} %param.13), dimensions={1,2} | broadcast | bytes 1152 | tf_op jit(solution)/shard_map/broadcast_in_dim | solution.py:167
  1.3 4.4 %all-to-all-start = ((s32[8,4,8]{2,1,0:T(4,128)}), s32[8,4,8]{2,1,0:T(4,128)S(1)}, u32[]{:S(2)}, u32[]{:S(2)}) async-start(s32[8,4,8]{2,1,0:T(4,128)} %broadcast_in_dim.4), calls=%async_computation | async-start | bytes 32768 | tf_op jit(solution)/shard_map/all_to_all | solution.py:166
  5.7 1.6 %rev.3 = bf16[32,512]{1,0:T(8,128)(2,1)S(1)} reverse(bf16[32,512]{1,0:T(8,128)(2,1)} %param.9), dimensions={1} | reverse | bytes 65536 | tf_op jit(solution)/shard_map/rev | solution.py:163
  7.3 0.7 %tile.4 = bf16[4,129,639]{2,1,0:T(8,128)(2,1)S(1)} broadcast(bf16[4,639]{1,0:T(4,128)(2,1)} %param.8), dimensions={0,2} | broadcast | bytes 664560 | tf_op jit(solution)/shard_map/tile | solution.py:14
  8.1 0.0 copy-start.2
  8.1 0.0 copy-start.3
  8.1 0.0 copy-start.1
  8.1 0.6 tile.10
  8.7 0.2 slice.8
  9.0 0.1 copy.16
  9.1 0.2 convolution_convert_fusion
  9.4 0.1 eq.23
  9.5 1.6 %all-to-all-done = s32[8,4,8]{2,1,0:T(4,128)S(1)} async-done(((s32[8,4,8]{2,1,0:T(4,128)}), s32[8,4,8]{2,1,0:T(4,128)S(1)}, u32[]{:S(2)}, u32[]{:S(2)}) %all-to-all-start) | async-done | bytes 1056 | tf_op jit(solution)/shard_map/all_to_all | solution.py:166
  11.0 0.1 copy.12
  11.1 0.1 broadcast_compare_fusion
  11.2 0.1 copy.13
  11.4 0.9 %broadcast_in_dim.5 = bf16[16,40,512]{2,1,0:T(8,128)(2,1)} broadcast(bf16[40,512]{1,0:T(8,128)(2,1)S(1)} %pad_maximum_fusion), dimensions={1,2} | broadcast | bytes 696320 | tf_op jit(solution)/shard_map/broadcast_in_dim | solution.py:176
  12.2 8.0 %all-to-all-start.1 = ((bf16[16,40,512]{2,1,0:T(8,128)(2,1)}), bf16[16,40,512]{2,1,0:T(8,128)(2,1)S(1)}, u32[]{:S(2)}, u32[]{:S(2)}) async-start(bf16[16,40,512]{2,1,0:T(8,128)(2,1)} %broadcast_in_dim.5), calls=%async_computation.1 | async-start | bytes 1310720 | tf_op jit(solution)/shard_map/all_to_all | solution.py:175
  20.3 0.0 copy-done.2
  20.3 0.0 copy-done.3
  20.3 0.0 copy-done.1
  20.3 12.1 %shard_map.82.gs_ref = bf16[8,512,512]{2,1,0:T(8,128)(2,1)S(1)} custom-call(f32[8,6]{1,0:T(8,128)S(1)} %copy-done.1, bf16[6144,512]{1,0:T(8,128)(2,1)} %ms_ref.1, s32[1,1024]{1,0:T(1,128)S(1)} %add_bitcast_fusion.gi_ref), custom_call_target="tpu_custom_call" | custom-call | tf_op jit(solution)/shard_map/pallas_call | solution.py:59
  32.5 0.0 copy-start
  32.5 1.9 %copy-done = bf16[8,512,512]{2,1,0:T(8,128)(2,1)} copy-done((bf16[8,512,512]{2,1,0:T(8,128)(2,1)}, bf16[8,512,512]{2,1,0:T(8,128)(2,1)S(1)}, u32[]{:S(2)}) %copy-start) | copy-done | bytes 4194328
  34.4 0.0 all-to-all-done.1.g_ref
  34.4 6.8 %shard_map.83 = f32[4096,128]{1,0:T(8,128)S(1)} custom-call(bf16[8,512,512]{2,1,0:T(8,128)(2,1)} %copy-done, bf16[16,40,512]{2,1,0:T(8,128)(2,1)S(1)} %all-to-all-done.1.g_ref), custom_call_target="tpu_custom_call" | custom-call | tf_op jit(solution)/shard_map/pallas_call | solution.py:118
  41.3 0.0 copy-start.4
  41.3 0.1 convert_element_type.27
  41.4 28.0 %all_to_all.15 = bf16[128,4,8,128]{3,2,1,0:T(8,128)(2,1)S(1)} all-to-all(bf16[128,4,8,128]{3,2,1,0:T(8,128)(2,1)S(1)} %bitcast.13), channel_id=1, replica_groups=mesh['mode'=8,'member'=16] {'mode','member'}, dimensions={0} | all-to-all | bytes 2097152 | tf_op jit(solution)/shard_map/all_to_all | solution.py:180
  69.4 0.2 convert_reduce_fusion
  69.6 0.0 copy-done.4
  69.6 0.7 %abs_reduce_fusion = f32[4,8]{1,0:T(4,128)} fusion(f32[4,8,128]{2,1,0:T(8,128)S(1)} %convert_reduce_fusion, f32[4,8]{1,0:T(4,128)S(1)} %copy-done.4), kind=kLoop, calls=%fused_computation.7 | loop fusion | flops 12256 | bytes 16640 | tf_op jit(solution)/shard_map/reduce_max | solution.py:185
  (7 shorter events, 0.1 us)
Async XLA Ops:
  1.3 9.7 %all-to-all-start = ((s32[8,4,8]{2,1,0:T(4,128)}), s32[8,4,8]{2,1,0:T(4,128)S(1)}, u32[]{:S(2)}, u32[]{:S(2)}) async-start(s32[8,4,8]{2,1,0:T(4,128)} %broadcast_in_dim.4), calls=%async_computation | async-start | bytes 32768 | tf_op jit(solution)/shard_map/all_to_all | solution.py:166
  8.1 12.2 %copy-start.2 = (s32[1024,1]{0,1:T(1,128)S(1)}, s32[1024,1]{0,1:T(1,128)}, u32[]{:S(2)}) copy-start(s32[1024,1]{0,1:T(1,128)} %param.12) | copy-start | bytes 12292
  8.1 12.2 %copy-start.3 = (s32[1024,1]{0,1:T(1,128)S(1)}, s32[1024,1]{0,1:T(1,128)}, u32[]{:S(2)}) copy-start(s32[1024,1]{0,1:T(1,128)} %param.11) | copy-start | bytes 12292
  8.1 12.3 %copy-start.1 = (f32[8,6]{1,0:T(8,128)S(1)}, f32[8,6]{1,0:T(8,128)}, u32[]{:S(2)}) copy-start(f32[8,6]{1,0:T(8,128)} %coef_ref.1) | copy-start | bytes 580
  12.2 22.2 %all-to-all-start.1 = ((bf16[16,40,512]{2,1,0:T(8,128)(2,1)}), bf16[16,40,512]{2,1,0:T(8,128)(2,1)S(1)}, u32[]{:S(2)}, u32[]{:S(2)}) async-start(bf16[16,40,512]{2,1,0:T(8,128)(2,1)} %broadcast_in_dim.5), calls=%async_computation.1 | async-start | bytes 1310720 | tf_op jit(solution)/shard_map/all_to_all | solution.py:175
  32.5 1.9 %copy-start = (bf16[8,512,512]{2,1,0:T(8,128)(2,1)}, bf16[8,512,512]{2,1,0:T(8,128)(2,1)S(1)}, u32[]{:S(2)}) copy-start(bf16[8,512,512]{2,1,0:T(8,128)(2,1)S(1)} %shard_map.82.gs_ref) | copy-start | bytes 12582916
  41.3 28.3 %copy-start.4 = (f32[4,8]{1,0:T(4,128)S(1)}, f32[4,8]{1,0:T(4,128)}, u32[]{:S(2)}) copy-start(f32[4,8]{1,0:T(4,128)} %param.15) | copy-start | bytes 388

commit v16 on v14

--- a/solution.py
+++ b/solution.py
@@ -5,7 +5,7 @@
 from jax import lax
 from jax.experimental import pallas as pl
 from jax.experimental.pallas import tpu as pltpu
-from jax.sharding import PartitionSpec as P
+from jax.sharding import Mesh, PartitionSpec as P
 
 
 def lagged_table(ground_accel, tap_count):
@@ -142,8 +142,8 @@
     tap_count = modal_kernel.shape[1]
     record_count = ground_accel.shape[0]
     comp_count = case_coef.shape[1]
-    n_mode = lax.axis_size("mode")
-    n_member = lax.axis_size("member")
+    n_mode = lax.axis_size(MODE)
+    n_member = lax.axis_size(MEMBER)
     groups_here, case_count = gravity.shape
     owner_total = n_mode * n_member
     group_total = groups_here * owner_total
@@ -155,7 +155,7 @@
     ).astype(jnp.bfloat16)
     resp_rows, width = local_resp.shape
     rec_col = lax.all_to_all(
-        jnp.broadcast_to(record_table[None], (n_mode,) + record_table.shape), "mode", 0, 0
+        jnp.broadcast_to(record_table[None], (n_mode,) + record_table.shape), MODE, 0, 0
     ).reshape(-1)
     onehot = (rec_col.reshape(n_mode, groups_here, case_count)[..., None] == jnp.arange(record_count))
     onehot = onehot.reshape(n_mode, groups_here, case_count * record_count)
@@ -163,32 +163,45 @@
     rec_rows = groups_here * (n_mode * 128 // width)
     rec_block = jnp.transpose(onehot, (1, 0, 2)).reshape(rec_rows, width).astype(jnp.bfloat16)
     payload = jnp.concatenate([local_resp, rec_block], axis=0)
+    inner = lax.axis_size(MEMBER[1])
     gathered = lax.all_to_all(
-        jnp.broadcast_to(payload[None], (n_member,) + payload.shape), "member", 0, 0
-    )
+        jnp.broadcast_to(payload[None], (inner,) + payload.shape), MEMBER[1], 0, 0
+    )
+    gathered = lax.all_to_all(
+        jnp.broadcast_to(gathered[None], (n_member // inner,) + gathered.shape), MEMBER[0], 0, 0
+    ).reshape((n_member,) + payload.shape)
     share = group_shares(
         case_coef, shape_groups, gathered, resp_rows, record_count, groups_here
     )
     share = share.reshape(owner_total, groups_here, case_count, share.shape[-1])
     received = lax.all_to_all(
-        share.astype(jnp.bfloat16), ("mode", "member"), split_axis=0, concat_axis=0, tiled=True
+        share.astype(jnp.bfloat16), MODE + MEMBER, split_axis=0, concat_axis=0, tiled=True
     )
     selected = jnp.sum(received.astype(jnp.float32), axis=0)
     combined = gravity[:, :, None] + selected
     return jnp.max(jnp.abs(combined), axis=2)
 
 
+MODE = ("x", "core")
+MEMBER = ("z", "y")
+
+
 def solution(mesh):
+    n_mode, n_member = mesh.devices.shape
+    outer = 2
+    inner = 4
+    fine = Mesh(
+        mesh.devices.reshape(n_mode // outer, outer, n_member // inner, inner), MODE + MEMBER
+    )
+    every = MODE + MEMBER
     placed = (
         P(),
-        P(("mode", "member"), None),
-        P("member", "mode"),
-        P("member", None),
-        P("member", None),
-        P(("mode", "member"), None),
+        P(every, None),
+        P(MEMBER, MODE),
+        P(MEMBER, None),
+        P(MEMBER, None),
+        P(every, None),
         P(),
-        P(("mode", "member"), None),
-    )
-    return jax.shard_map(
-        local, mesh=mesh, in_specs=placed, out_specs=P(("mode", "member"), None), check_vma=False
-    )
+        P(every, None),
+    )
+    return jax.shard_map(local, mesh=fine, in_specs=placed, out_specs=P(every, None), check_vma=False)

time: 67.7 us -> 73.5 us (1.086)
  blocking collectives: 24.1 us -> 36.1 us
  waiting for transfers between devices: 5.63 us -> 2.21 us
  starting transfers between devices: 12.5 us -> 9.69 us
    all_to_all x1 -> x2, blocking collectives: 24.1 us -> 36.1 us  [the longest x1 25.7 us: local(): lax.all_to_all(share.astype(jnp.bfloat16), MODE + MEMBER, split_axis=0, c...]
    all_to_all x1, waiting for transfers between devices: 4.03 us -> 0.61 us  [local(): lax.all_to_all(jnp.broadcast_to(gathered[None], (n_member // inner,) + ga...]
    all_to_all x1, starting transfers between devices: 8.09 us -> 5.31 us  [local(): lax.all_to_all(jnp.broadcast_to(gathered[None], (n_member // inner,) + ga...]
  transfers between devices with their start and end apart: 2 -> 2, of which waited for: 2 -> 2; matrix products, arithmetic and copies ran while one was open for 6% -> 5% of each run, Pallas kernels for 13% -> 12%
where the time goes in v16:
time: 73.5 us; the launch traced here: 72.8 us
  blocking collectives  36.1 us (49%)
  Pallas kernels  17.4 us (24%)
  starting transfers between devices  9.69 us (13%)
  local copies, waits for them, and re-layouts  5.88 us (8%)
  waiting for transfers between devices  2.21 us (3%)
  other arithmetic  1.14 us (2%)
    all_to_all x1, blocking collectives, local(): lax.all_to_all(share.astype(jnp.bfloat16), MODE + MEMBER, split_axis=0, c...  25.7 us
    all_to_all x1, blocking collectives, local(): lax.all_to_all(jnp.broadcast_to(payload[None], (inner,) + payload.shape),...  10.4 us
    pallas_call x1, Pallas kernels, shape_sums(): pl.pallas_call(functools.partial(shape_sum_kernel, comps=comps, tile=tile...  8.88 us
    pallas_call x1, Pallas kernels, group_shares(): pl.pallas_call(functools.partial(mix_kernel, records=records, per_owner=p...  8.48 us
    all_to_all x1, starting transfers between devices, local(): lax.all_to_all(jnp.broadcast_to(gathered[None], (n_member // inner,) + ga...  5.31 us
    all_to_all x1, starting transfers between devices, local(): lax.all_to_all(jnp.broadcast_to(record_table[None], (n_mode,) + record_ta...  4.38 us
    rev x1, local copies, waits for them, and re-layouts, local(): modal_kernel[:, ::-1]  1.64 us
    all_to_all x1, waiting for transfers between devices, local(): lax.all_to_all(jnp.broadcast_to(record_table[None], (n_mode,) + record_ta...  1.6 us
  transfers between devices with their start and end apart: 2, of which 2 were waited for; matrix products, arithmetic and copies ran while one was open for 5% of the time, Pallas kernels for 12%

profile of v16, /device:TPU:0, one launch (start us, length us, event | category | flops | bytes accessed | tf_op | source)
XLA Modules:
  0.0 72.8 jit_solution(1435836320701404562)
XLA Ops:
  0.0 1.3 %broadcast_in_dim.6 = s32[8,4,8]{2,1,0:T(4,128)} broadcast(s32[4,8]{1,0:T(4,128)} %param.13), dimensions={1,2} | broadcast | bytes 1152 | tf_op jit(solution)/shard_map/broadcast_in_dim | solution.py:158
  1.3 4.4 %all-to-all-start = ((s32[8,4,8]{2,1,0:T(4,128)}), s32[8,4,8]{2,1,0:T(4,128)S(1)}, u32[]{:S(2)}, u32[]{:S(2)}) async-start(s32[8,4,8]{2,1,0:T(4,128)} %broadcast_in_dim.6), calls=%async_computation | async-start | bytes 32768 | tf_op jit(solution)/shard_map/all_to_all | solution.py:157
  5.7 1.6 %rev.3 = bf16[32,512]{1,0:T(8,128)(2,1)S(1)} reverse(bf16[32,512]{1,0:T(8,128)(2,1)} %param.9), dimensions={1} | reverse | bytes 65536 | tf_op jit(solution)/shard_map/rev | solution.py:154
  7.3 0.7 %tile.4 = bf16[4,129,639]{2,1,0:T(8,128)(2,1)S(1)} broadcast(bf16[4,639]{1,0:T(4,128)(2,1)} %param.8), dimensions={0,2} | broadcast | bytes 664560 | tf_op jit(solution)/shard_map/tile | solution.py:14
  8.1 0.6 tile.10
  8.7 0.2 slice.8
  8.9 0.0 copy-start.1
  8.9 0.0 copy-start.2
  8.9 0.1 copy.16
  9.1 0.2 convolution_convert_fusion
  9.3 0.1 eq.23
  9.4 1.6 %all-to-all-done = s32[8,4,8]{2,1,0:T(4,128)S(1)} async-done(((s32[8,4,8]{2,1,0:T(4,128)}), s32[8,4,8]{2,1,0:T(4,128)S(1)}, u32[]{:S(2)}, u32[]{:S(2)}) %all-to-all-start) | async-done | bytes 1056 | tf_op jit(solution)/shard_map/all_to_all | solution.py:157
  11.0 0.1 copy.12
  11.1 0.1 broadcast_compare_fusion
  11.2 0.1 copy.13
  11.4 10.4 %all_to_all.20 = bf16[4,40,512]{2,1,0:T(8,128)(2,1)S(1)} all-to-all(bf16[4,40,512]{2,1,0:T(8,128)(2,1)S(1)} %broadcast_in_dim.7), channel_id=1, replica_groups=mesh['x'=4,'core'=2,'z'=4,'y'=4] {'y'}, dimensions={0} | all-to-all | bytes 327680 | tf_op jit(solution)/shard_map/all_to_all | solution.py:167
  21.8 0.9 %broadcast_in_dim.8 = bf16[4,4,40,512]{3,2,1,0:T(8,128)(2,1)} broadcast(bf16[4,40,512]{2,1,0:T(8,128)(2,1)S(1)} %all_to_all.20), dimensions={1,2,3} | broadcast | bytes 819200 | tf_op jit(solution)/shard_map/broadcast_in_dim | solution.py:171
  22.7 5.3 %all-to-all-start.2 = ((bf16[4,4,40,512]{3,2,1,0:T(8,128)(2,1)}), bf16[4,4,40,512]{3,2,1,0:T(8,128)(2,1)}, u32[]{:S(2)}, u32[]{:S(2)}) async-start(bf16[4,4,40,512]{3,2,1,0:T(8,128)(2,1)} %broadcast_in_dim.8), calls=%async_computation.2 | async-start | bytes 1310720 | tf_op jit(solution)/shard_map/all_to_all | solution.py:170
  28.0 0.0 copy-done.1
  28.0 0.0 copy-done.2
  28.0 0.0 copy-start
  28.0 8.9 %shard_map.82.gs_ref = bf16[6,512,512]{2,1,0:T(8,128)(2,1)S(1)} custom-call(bf16[6144,512]{1,0:T(8,128)(2,1)} %ms_ref.1, s32[1,1024]{1,0:T(1,128)S(1)} %add_bitcast_fusion.gi_ref), custom_call_target="tpu_custom_call" | custom-call | tf_op jit(solution)/shard_map/pallas_call | solution.py:46
  36.9 0.6 all-to-all-done.2
  37.5 0.0 copy-done
  37.5 8.5 %shard_map.83 = f32[4096,128]{1,0:T(8,128)S(1)} custom-call(f32[8,6]{1,0:T(8,128)S(1)} %copy-done, bf16[6,512,512]{2,1,0:T(8,128)(2,1)S(1)} %shard_map.82.gs_ref, bf16[16,40,512]{2,1,0:T(8,128)(2,1)} %bitcast.4.g_ref), custom_call_target="tpu_custom_call" | custom-call | tf_op jit(solution)/shard_map/pallas_call | solution.py:108
  46.0 0.0 copy-start.3
  46.0 0.1 convert_element_type.27
  46.1 25.7 %all_to_all.21 = bf16[128,4,8,128]{3,2,1,0:T(8,128)(2,1)S(1)} all-to-all(bf16[128,4,8,128]{3,2,1,0:T(8,128)(2,1)S(1)} %bitcast.14), channel_id=1, replica_groups=mesh['x'=4,'core'=2,'z'=4,'y'=4] {'x','core','z','y'}, dimensions={0} | all-to-all | bytes 2097152 | tf_op jit(solution)/shard_map/all_to_all | solution.py:177
  71.9 0.2 convert_reduce_fusion
  72.1 0.0 copy-done.3
  72.1 0.7 %abs_reduce_fusion = f32[4,8]{1,0:T(4,128)} fusion(f32[4,8,128]{2,1,0:T(8,128)S(1)} %convert_reduce_fusion, f32[4,8]{1,0:T(4,128)S(1)} %copy-done.3), kind=kLoop, calls=%fused_computation.7 | loop fusion | flops 12256 | bytes 16640 | tf_op jit(solution)/shard_map/reduce_max | solution.py:182
  (8 shorter events, 0.1 us)
Async XLA Ops:
  1.3 9.7 %all-to-all-start = ((s32[8,4,8]{2,1,0:T(4,128)}), s32[8,4,8]{2,1,0:T(4,128)S(1)}, u32[]{:S(2)}, u32[]{:S(2)}) async-start(s32[8,4,8]{2,1,0:T(4,128)} %broadcast_in_dim.6), calls=%async_computation | async-start | bytes 32768 | tf_op jit(solution)/shard_map/all_to_all | solution.py:157
  8.9 19.1 %copy-start.1 = (s32[1024,1]{0,1:T(1,128)S(1)}, s32[1024,1]{0,1:T(1,128)}, u32[]{:S(2)}) copy-start(s32[1024,1]{0,1:T(1,128)} %param.12) | copy-start | bytes 12292
  8.9 19.1 %copy-start.2 = (s32[1024,1]{0,1:T(1,128)S(1)}, s32[1024,1]{0,1:T(1,128)}, u32[]{:S(2)}) copy-start(s32[1024,1]{0,1:T(1,128)} %param.11) | copy-start | bytes 12292
  22.7 14.8 %all-to-all-start.2 = ((bf16[4,4,40,512]{3,2,1,0:T(8,128)(2,1)}), bf16[4,4,40,512]{3,2,1,0:T(8,128)(2,1)}, u32[]{:S(2)}, u32[]{:S(2)}) async-start(bf16[4,4,40,512]{3,2,1,0:T(8,128)(2,1)} %broadcast_in_dim.8), calls=%async_computation.2 | async-start | bytes 1310720 | tf_op jit(solution)/shard_map/all_to_all | solution.py:170
  28.0 9.5 %copy-start = (f32[8,6]{1,0:T(8,128)S(1)}, f32[8,6]{1,0:T(8,128)}, u32[]{:S(2)}) copy-start(f32[8,6]{1,0:T(8,128)} %coef_ref.1) | copy-start | bytes 580
  46.0 26.0 %copy-start.3 = (f32[4,8]{1,0:T(4,128)S(1)}, f32[4,8]{1,0:T(4,128)}, u32[]{:S(2)}) copy-start(f32[4,8]{1,0:T(4,128)} %param.15) | copy-start | bytes 388

commit v17 on v14

--- a/solution.py
+++ b/solution.py
@@ -69,7 +69,10 @@
         for j in range(senders):
             r_scr[pl.ds(j * resp_rows, resp_rows), :] = g_ref[j, pl.ds(0, resp_rows), :]
 
-    q_scr[c] = jnp.dot(gs_ref[0], r_scr[...], preferred_element_type=jnp.float32)
+    for e in range(gs_ref.shape[0]):
+        q_scr[c * gs_ref.shape[0] + e] = jnp.dot(
+            gs_ref[e], r_scr[...], preferred_element_type=jnp.float32
+        )
 
     @pl.when(c == comps - 1)
     def _():
@@ -113,10 +116,10 @@
             resp_rows=resp_rows,
             rec_rows=gathered.shape[1] - resp_rows,
         ),
-        grid=(comps,),
+        grid=(comps // 2,),
         in_specs=[
             pl.BlockSpec(memory_space=pltpu.SMEM),
-            pl.BlockSpec((1, groups, modes), lambda c: (c, 0, 0)),
+            pl.BlockSpec((2, groups, modes), lambda c: (c, 0, 0)),
             pl.BlockSpec(gathered.shape, lambda c: (0, 0, 0)),
         ],
         out_specs=pl.BlockSpec((groups * cases, steps), lambda c: (0, 0)),

time: 67.7 us -> 67.1 us (level)
  no operation moved by 1% of the time
where the time goes in v17:
time: 67.1 us; the launch traced here: 66.4 us
  blocking collectives  24.1 us (36%)
  Pallas kernels  16.8 us (25%)
  starting transfers between devices  12.5 us (19%)
  local copies, waits for them, and re-layouts  5.85 us (9%)
  waiting for transfers between devices  5.63 us (8%)
  other arithmetic  1.14 us (2%)
    all_to_all x1, blocking collectives, local(): lax.all_to_all(share.astype(jnp.bfloat16), ('mode', 'member'), split_axis...  24.1 us
    pallas_call x1, Pallas kernels, shape_sums(): pl.pallas_call(functools.partial(shape_sum_kernel, comps=comps, tile=tile...  8.88 us
    all_to_all x1, starting transfers between devices, local(): lax.all_to_all(jnp.broadcast_to(payload[None], (n_member,) + payload.shap...  8.09 us
    pallas_call x1, Pallas kernels, group_shares(): pl.pallas_call(functools.partial(mix_kernel, records=records, per_owner=p...  7.93 us
    all_to_all x1, starting transfers between devices, local(): lax.all_to_all(jnp.broadcast_to(record_table[None], (n_mode,) + record_ta...  4.38 us
    all_to_all x1, waiting for transfers between devices, local(): lax.all_to_all(jnp.broadcast_to(payload[None], (n_member,) + payload.shap...  4.03 us
    rev x1, local copies, waits for them, and re-layouts, local(): modal_kernel[:, ::-1]  1.64 us
    all_to_all x1, waiting for transfers between devices, local(): lax.all_to_all(jnp.broadcast_to(record_table[None], (n_mode,) + record_ta...  1.6 us
  transfers between devices with their start and end apart: 2, of which 2 were waited for; matrix products, arithmetic and copies ran while one was open for 6% of the time, Pallas kernels for 13%

profile of v17, /device:TPU:0, one launch (start us, length us, event | category | flops | bytes accessed | tf_op | source)
XLA Modules:
  0.0 66.4 jit_solution(8437102021603957674)
XLA Ops:
  0.0 1.3 %broadcast_in_dim.4 = s32[8,4,8]{2,1,0:T(4,128)} broadcast(s32[4,8]{1,0:T(4,128)} %param.13), dimensions={1,2} | broadcast | bytes 1152 | tf_op jit(solution)/shard_map/broadcast_in_dim | solution.py:161
  1.3 4.4 %all-to-all-start = ((s32[8,4,8]{2,1,0:T(4,128)}), s32[8,4,8]{2,1,0:T(4,128)S(1)}, u32[]{:S(2)}, u32[]{:S(2)}) async-start(s32[8,4,8]{2,1,0:T(4,128)} %broadcast_in_dim.4), calls=%async_computation | async-start | bytes 32768 | tf_op jit(solution)/shard_map/all_to_all | solution.py:160
  5.7 1.6 %rev.3 = bf16[32,512]{1,0:T(8,128)(2,1)S(1)} reverse(bf16[32,512]{1,0:T(8,128)(2,1)} %param.9), dimensions={1} | reverse | bytes 65536 | tf_op jit(solution)/shard_map/rev | solution.py:157
  7.3 0.7 %tile.4 = bf16[4,129,639]{2,1,0:T(8,128)(2,1)S(1)} broadcast(bf16[4,639]{1,0:T(4,128)(2,1)} %param.8), dimensions={0,2} | broadcast | bytes 664560 | tf_op jit(solution)/shard_map/tile | solution.py:14
  8.1 0.6 tile.10
  8.7 0.0 copy-start.1
  8.7 0.0 copy-start.2
  8.7 0.2 slice.8
  8.9 0.1 copy.16
  9.1 0.2 convolution_convert_fusion
  9.3 0.1 eq.23
  9.4 1.6 %all-to-all-done = s32[8,4,8]{2,1,0:T(4,128)S(1)} async-done(((s32[8,4,8]{2,1,0:T(4,128)}), s32[8,4,8]{2,1,0:T(4,128)S(1)}, u32[]{:S(2)}, u32[]{:S(2)}) %all-to-all-start) | async-done | bytes 1056 | tf_op jit(solution)/shard_map/all_to_all | solution.py:160
  11.0 0.1 copy.12
  11.1 0.1 broadcast_compare_fusion
  11.2 0.1 copy.13
  11.4 0.9 %broadcast_in_dim.5 = bf16[16,40,512]{2,1,0:T(8,128)(2,1)} broadcast(bf16[40,512]{1,0:T(8,128)(2,1)S(1)} %pad_maximum_fusion), dimensions={1,2} | broadcast | bytes 696320 | tf_op jit(solution)/shard_map/broadcast_in_dim | solution.py:170
  12.3 8.1 %all-to-all-start.1 = ((bf16[16,40,512]{2,1,0:T(8,128)(2,1)}), bf16[16,40,512]{2,1,0:T(8,128)(2,1)}, u32[]{:S(2)}, u32[]{:S(2)}) async-start(bf16[16,40,512]{2,1,0:T(8,128)(2,1)} %broadcast_in_dim.5), calls=%async_computation.1 | async-start | bytes 1310720 | tf_op jit(solution)/shard_map/all_to_all | solution.py:169
  20.4 0.0 copy-done.1
  20.4 0.0 copy-done.2
  20.4 0.0 copy-start
  20.4 8.9 %shard_map.82.gs_ref = bf16[6,512,512]{2,1,0:T(8,128)(2,1)S(1)} custom-call(bf16[6144,512]{1,0:T(8,128)(2,1)} %ms_ref.1, s32[1,1024]{1,0:T(1,128)S(1)} %add_bitcast_fusion.gi_ref), custom_call_target="tpu_custom_call" | custom-call | tf_op jit(solution)/shard_map/pallas_call | solution.py:46
  29.3 4.0 %all-to-all-done.1.g_ref = bf16[16,40,512]{2,1,0:T(8,128)(2,1)} async-done(((bf16[16,40,512]{2,1,0:T(8,128)(2,1)}), bf16[16,40,512]{2,1,0:T(8,128)(2,1)}, u32[]{:S(2)}, u32[]{:S(2)}) %all-to-all-start.1) | async-done | bytes 655392 | tf_op jit(solution)/shard_map/all_to_all | solution.py:169
  33.3 0.0 copy-done
  33.3 7.9 %shard_map.83 = f32[4096,128]{1,0:T(8,128)S(1)} custom-call(f32[8,6]{1,0:T(8,128)S(1)} %copy-done, bf16[6,512,512]{2,1,0:T(8,128)(2,1)S(1)} %shard_map.82.gs_ref, bf16[16,40,512]{2,1,0:T(8,128)(2,1)} %all-to-all-done.1.g_ref), custom_call_target="tpu_custom_call" | custom-call | tf_op jit(solution)/shard_map/pallas_call | solution.py:111
  41.3 0.0 copy-start.3
  41.3 0.1 convert_element_type.27
  41.4 24.1 %all_to_all.15 = bf16[128,4,8,128]{3,2,1,0:T(8,128)(2,1)S(1)} all-to-all(bf16[128,4,8,128]{3,2,1,0:T(8,128)(2,1)S(1)} %bitcast.13), channel_id=1, replica_groups=mesh['mode'=8,'member'=16] {'mode','member'}, dimensions={0} | all-to-all | bytes 2097152 | tf_op jit(solution)/shard_map/all_to_all | solution.py:176
  65.5 0.2 convert_reduce_fusion
  65.7 0.0 copy-done.3
  65.7 0.7 %abs_reduce_fusion = f32[4,8]{1,0:T(4,128)} fusion(f32[4,8,128]{2,1,0:T(8,128)S(1)} %convert_reduce_fusion, f32[4,8]{1,0:T(4,128)S(1)} %copy-done.3), kind=kLoop, calls=%fused_computation.7 | loop fusion | flops 12256 | bytes 16640 | tf_op jit(solution)/shard_map/reduce_max | solution.py:181
  (7 shorter events, 0.1 us)
Async XLA Ops:
  1.3 9.7 %all-to-all-start = ((s32[8,4,8]{2,1,0:T(4,128)}), s32[8,4,8]{2,1,0:T(4,128)S(1)}, u32[]{:S(2)}, u32[]{:S(2)}) async-start(s32[8,4,8]{2,1,0:T(4,128)} %broadcast_in_dim.4), calls=%async_computation | async-start | bytes 32768 | tf_op jit(solution)/shard_map/all_to_all | solution.py:160
  8.7 11.7 %copy-start.1 = (s32[1024,1]{0,1:T(1,128)S(1)}, s32[1024,1]{0,1:T(1,128)}, u32[]{:S(2)}) copy-start(s32[1024,1]{0,1:T(1,128)} %param.12) | copy-start | bytes 12292
  8.7 11.7 %copy-start.2 = (s32[1024,1]{0,1:T(1,128)S(1)}, s32[1024,1]{0,1:T(1,128)}, u32[]{:S(2)}) copy-start(s32[1024,1]{0,1:T(1,128)} %param.11) | copy-start | bytes 12292
  12.3 21.1 %all-to-all-start.1 = ((bf16[16,40,512]{2,1,0:T(8,128)(2,1)}), bf16[16,40,512]{2,1,0:T(8,128)(2,1)}, u32[]{:S(2)}, u32[]{:S(2)}) async-start(bf16[16,40,512]{2,1,0:T(8,128)(2,1)} %broadcast_in_dim.5), calls=%async_computation.1 | async-start | bytes 1310720 | tf_op jit(solution)/shard_map/all_to_all | solution.py:169
  20.4 12.9 %copy-start = (f32[8,6]{1,0:T(8,128)S(1)}, f32[8,6]{1,0:T(8,128)}, u32[]{:S(2)}) copy-start(f32[8,6]{1,0:T(8,128)} %coef_ref.1) | copy-start | bytes 580
  41.3 24.4 %copy-start.3 = (f32[4,8]{1,0:T(4,128)S(1)}, f32[4,8]{1,0:T(4,128)}, u32[]{:S(2)}) copy-start(f32[4,8]{1,0:T(4,128)} %param.15) | copy-start | bytes 388

commit v18 on v17

--- a/solution.py
+++ b/solution.py
@@ -116,10 +116,10 @@
             resp_rows=resp_rows,
             rec_rows=gathered.shape[1] - resp_rows,
         ),
-        grid=(comps // 2,),
+        grid=(comps // 3,),
         in_specs=[
             pl.BlockSpec(memory_space=pltpu.SMEM),
-            pl.BlockSpec((2, groups, modes), lambda c: (c, 0, 0)),
+            pl.BlockSpec((3, groups, modes), lambda c: (c, 0, 0)),
             pl.BlockSpec(gathered.shape, lambda c: (0, 0, 0)),
         ],
         out_specs=pl.BlockSpec((groups * cases, steps), lambda c: (0, 0)),

time: 67.1 us -> 67 us (level)
  no operation moved by 1% of the time
where the time goes in v18:
time: 67 us; the launch traced here: 66.2 us
  blocking collectives  24.1 us (36%)
  Pallas kernels  16.6 us (25%)
  starting transfers between devices  12.5 us (19%)
  local copies, waits for them, and re-layouts  5.85 us (9%)
  waiting for transfers between devices  5.63 us (8%)
  other arithmetic  1.14 us (2%)
    all_to_all x1, blocking collectives, local(): lax.all_to_all(share.astype(jnp.bfloat16), ('mode', 'member'), split_axis...  24.1 us
    pallas_call x1, Pallas kernels, shape_sums(): pl.pallas_call(functools.partial(shape_sum_kernel, comps=comps, tile=tile...  8.88 us
    all_to_all x1, starting transfers between devices, local(): lax.all_to_all(jnp.broadcast_to(payload[None], (n_member,) + payload.shap...  8.09 us
    pallas_call x1, Pallas kernels, group_shares(): pl.pallas_call(functools.partial(mix_kernel, records=records, per_owner=p...  7.75 us
    all_to_all x1, starting transfers between devices, local(): lax.all_to_all(jnp.broadcast_to(record_table[None], (n_mode,) + record_ta...  4.38 us
    all_to_all x1, waiting for transfers between devices, local(): lax.all_to_all(jnp.broadcast_to(payload[None], (n_member,) + payload.shap...  4.03 us
    rev x1, local copies, waits for them, and re-layouts, local(): modal_kernel[:, ::-1]  1.64 us
    all_to_all x1, waiting for transfers between devices, local(): lax.all_to_all(jnp.broadcast_to(record_table[None], (n_mode,) + record_ta...  1.6 us
  transfers between devices with their start and end apart: 2, of which 2 were waited for; matrix products, arithmetic and copies ran while one was open for 6% of the time, Pallas kernels for 13%

profile of v18, /device:TPU:0, one launch (start us, length us, event | category | flops | bytes accessed | tf_op | source)
XLA Modules:
  0.0 66.2 jit_solution(18316670780132459005)
XLA Ops:
  0.0 1.3 %broadcast_in_dim.4 = s32[8,4,8]{2,1,0:T(4,128)} broadcast(s32[4,8]{1,0:T(4,128)} %param.13), dimensions={1,2} | broadcast | bytes 1152 | tf_op jit(solution)/shard_map/broadcast_in_dim | solution.py:161
  1.3 4.4 %all-to-all-start = ((s32[8,4,8]{2,1,0:T(4,128)}), s32[8,4,8]{2,1,0:T(4,128)S(1)}, u32[]{:S(2)}, u32[]{:S(2)}) async-start(s32[8,4,8]{2,1,0:T(4,128)} %broadcast_in_dim.4), calls=%async_computation | async-start | bytes 32768 | tf_op jit(solution)/shard_map/all_to_all | solution.py:160
  5.7 1.6 %rev.3 = bf16[32,512]{1,0:T(8,128)(2,1)S(1)} reverse(bf16[32,512]{1,0:T(8,128)(2,1)} %param.9), dimensions={1} | reverse | bytes 65536 | tf_op jit(solution)/shard_map/rev | solution.py:157
  7.3 0.7 %tile.4 = bf16[4,129,639]{2,1,0:T(8,128)(2,1)S(1)} broadcast(bf16[4,639]{1,0:T(4,128)(2,1)} %param.8), dimensions={0,2} | broadcast | bytes 664560 | tf_op jit(solution)/shard_map/tile | solution.py:14
  8.1 0.6 tile.10
  8.7 0.0 copy-start.1
  8.7 0.0 copy-start.2
  8.7 0.2 slice.8
  8.9 0.1 copy.16
  9.1 0.2 convolution_convert_fusion
  9.3 0.1 eq.23
  9.4 1.6 %all-to-all-done = s32[8,4,8]{2,1,0:T(4,128)S(1)} async-done(((s32[8,4,8]{2,1,0:T(4,128)}), s32[8,4,8]{2,1,0:T(4,128)S(1)}, u32[]{:S(2)}, u32[]{:S(2)}) %all-to-all-start) | async-done | bytes 1056 | tf_op jit(solution)/shard_map/all_to_all | solution.py:160
  11.0 0.1 copy.12
  11.1 0.1 broadcast_compare_fusion
  11.2 0.1 copy.13
  11.4 0.9 %broadcast_in_dim.5 = bf16[16,40,512]{2,1,0:T(8,128)(2,1)} broadcast(bf16[40,512]{1,0:T(8,128)(2,1)S(1)} %pad_maximum_fusion), dimensions={1,2} | broadcast | bytes 696320 | tf_op jit(solution)/shard_map/broadcast_in_dim | solution.py:170
  12.3 8.1 %all-to-all-start.1 = ((bf16[16,40,512]{2,1,0:T(8,128)(2,1)}), bf16[16,40,512]{2,1,0:T(8,128)(2,1)}, u32[]{:S(2)}, u32[]{:S(2)}) async-start(bf16[16,40,512]{2,1,0:T(8,128)(2,1)} %broadcast_in_dim.5), calls=%async_computation.1 | async-start | bytes 1310720 | tf_op jit(solution)/shard_map/all_to_all | solution.py:169
  20.4 0.0 copy-done.1
  20.4 0.0 copy-done.2
  20.4 0.0 copy-start
  20.4 8.9 %shard_map.82.gs_ref = bf16[6,512,512]{2,1,0:T(8,128)(2,1)S(1)} custom-call(bf16[6144,512]{1,0:T(8,128)(2,1)} %ms_ref.1, s32[1,1024]{1,0:T(1,128)S(1)} %add_bitcast_fusion.gi_ref), custom_call_target="tpu_custom_call" | custom-call | tf_op jit(solution)/shard_map/pallas_call | solution.py:46
  29.3 4.0 %all-to-all-done.1.g_ref = bf16[16,40,512]{2,1,0:T(8,128)(2,1)} async-done(((bf16[16,40,512]{2,1,0:T(8,128)(2,1)}), bf16[16,40,512]{2,1,0:T(8,128)(2,1)}, u32[]{:S(2)}, u32[]{:S(2)}) %all-to-all-start.1) | async-done | bytes 655392 | tf_op jit(solution)/shard_map/all_to_all | solution.py:169
  33.3 0.0 copy-done
  33.3 7.8 %shard_map.83 = f32[4096,128]{1,0:T(8,128)S(1)} custom-call(f32[8,6]{1,0:T(8,128)S(1)} %copy-done, bf16[6,512,512]{2,1,0:T(8,128)(2,1)S(1)} %shard_map.82.gs_ref, bf16[16,40,512]{2,1,0:T(8,128)(2,1)} %all-to-all-done.1.g_ref), custom_call_target="tpu_custom_call" | custom-call | tf_op jit(solution)/shard_map/pallas_call | solution.py:111
  41.1 0.0 copy-start.3
  41.1 0.1 convert_element_type.27
  41.2 24.1 %all_to_all.15 = bf16[128,4,8,128]{3,2,1,0:T(8,128)(2,1)S(1)} all-to-all(bf16[128,4,8,128]{3,2,1,0:T(8,128)(2,1)S(1)} %bitcast.13), channel_id=1, replica_groups=mesh['mode'=8,'member'=16] {'mode','member'}, dimensions={0} | all-to-all | bytes 2097152 | tf_op jit(solution)/shard_map/all_to_all | solution.py:176
  65.3 0.2 convert_reduce_fusion
  65.5 0.0 copy-done.3
  65.5 0.7 %abs_reduce_fusion = f32[4,8]{1,0:T(4,128)} fusion(f32[4,8,128]{2,1,0:T(8,128)S(1)} %convert_reduce_fusion, f32[4,8]{1,0:T(4,128)S(1)} %copy-done.3), kind=kLoop, calls=%fused_computation.7 | loop fusion | flops 12256 | bytes 16640 | tf_op jit(solution)/shard_map/reduce_max | solution.py:181
  (7 shorter events, 0.1 us)
Async XLA Ops:
  1.3 9.7 %all-to-all-start = ((s32[8,4,8]{2,1,0:T(4,128)}), s32[8,4,8]{2,1,0:T(4,128)S(1)}, u32[]{:S(2)}, u32[]{:S(2)}) async-start(s32[8,4,8]{2,1,0:T(4,128)} %broadcast_in_dim.4), calls=%async_computation | async-start | bytes 32768 | tf_op jit(solution)/shard_map/all_to_all | solution.py:160
  8.7 11.7 %copy-start.1 = (s32[1024,1]{0,1:T(1,128)S(1)}, s32[1024,1]{0,1:T(1,128)}, u32[]{:S(2)}) copy-start(s32[1024,1]{0,1:T(1,128)} %param.12) | copy-start | bytes 12292
  8.7 11.7 %copy-start.2 = (s32[1024,1]{0,1:T(1,128)S(1)}, s32[1024,1]{0,1:T(1,128)}, u32[]{:S(2)}) copy-start(s32[1024,1]{0,1:T(1,128)} %param.11) | copy-start | bytes 12292
  12.3 21.1 %all-to-all-start.1 = ((bf16[16,40,512]{2,1,0:T(8,128)(2,1)}), bf16[16,40,512]{2,1,0:T(8,128)(2,1)}, u32[]{:S(2)}, u32[]{:S(2)}) async-start(bf16[16,40,512]{2,1,0:T(8,128)(2,1)} %broadcast_in_dim.5), calls=%async_computation.1 | async-start | bytes 1310720 | tf_op jit(solution)/shard_map/all_to_all | solution.py:169
  20.4 12.9 %copy-start = (f32[8,6]{1,0:T(8,128)S(1)}, f32[8,6]{1,0:T(8,128)}, u32[]{:S(2)}) copy-start(f32[8,6]{1,0:T(8,128)} %coef_ref.1) | copy-start | bytes 580
  41.1 24.4 %copy-start.3 = (f32[4,8]{1,0:T(4,128)S(1)}, f32[4,8]{1,0:T(4,128)}, u32[]{:S(2)}) copy-start(f32[4,8]{1,0:T(4,128)} %param.15) | copy-start | bytes 388
